TPU v7x, 32 devices: a whole 2x2x4 slice. The times are simulated.
32 devices in a mesh: groups: 2 (over y), sect: 4 (over z), band: 2 (over x), sub: 2 (over core).
Axes of the slice: x: 2, y: 2, z: 4, core: 2. Of those that a mesh axis runs over, the one named last changes fastest.
Arguments:
- images: bfloat16 [2, 256, 256, 256], P('band', ('groups', 'sect', 'sub')), parts along dimension 1, may hold values from -48 to 48
- offsets: float32 [2, 256, 2], P('band', ('groups', 'sect', 'sub')), parts along dimension 1, may hold values from -0.5 to 0.5
- widths: float32 [2, 256, 2], P('band', ('groups', 'sect', 'sub')), parts along dimension 1, may hold values from 0.1 to 1
- weights: bfloat16 [2, 256], P('band', ('groups', 'sect', 'sub')), parts along dimension 1, may hold values from 0.25 to 4
- dest: int32 [2, 256], P('band', ('groups', 'sect', 'sub')), parts along dimension 1, may hold values from 0 to 7, as said below
- cells: int32 [2, 256], P('band', ('groups', 'sect', 'sub')), parts along dimension 1, may hold values from 0 to 3, as said below
- band_gain: float32 [2], P('band'), may hold values from 2 to 8
Outputs:
- coadd: bfloat16 [2, 256, 16384], P('band', None, ('groups', 'sect', 'sub')), parts along dimension 2
- detection: float32 [256, 16384], P('band', ('groups', 'sect', 'sub')), parts along dimension 1
There are 2 independent parts, one for each index of `groups`. A program takes and returns all parts, laid end to end along the dimension named above; an argument that names none is the same for every part. Nothing has to cross between parts.
Inputs may be any that keep to these rules, and one draw needn't show every extreme that they name: `dest`: among the 16 blocks of one device in one band, no owner is named more than 4 times; in every band one owner is named exactly 4 times by every device's blocks. `cells`: in every band, at most one block of each owner falls in that owner's cell 4 - 1.
All inputs are finite; a program needn't handle non-finite values.
Results may differ from a plain program's by a relative error of at most 0.0012.
The roundings to bfloat16 on the way count: a program that leaves them out, or rounds other values in their place, can miss the bound.
Values may be sent and summed in bfloat16 or wider, within the bound.
No kernel may reach another device: no remote copies, remote signals or barrier semaphores. Data moves between devices by JAX's collectives and lax.ppermute only.
A program may use at most 64 MiB of HBM per device.

v0:
```python
import math

import jax
import jax.numpy as jnp
from jax import lax
from jax.sharding import PartitionSpec as P

CELL_DEV = 4
PSF_R = 8
DET_R = 4


det_sigma = 3.0


def extended(array, sides, width):
    for axis, dim in sides:
        size, length = (lax.axis_size(axis), array.shape[dim])
        up = [(i, (i + 1) % size) for i in range(size - 1)]
        down = [(j, i) for i, j in up]
        last = lax.slice_in_dim(array, length - width, length, axis=dim)
        initial = lax.slice_in_dim(array, 0, width, axis=dim)
        before = lax.ppermute(last, axis, up)
        after = lax.ppermute(initial, axis, down)
        array = jnp.concatenate([before, array, after], axis=dim)
    return array


def lanczos_tap(spacing):
    return jnp.where(jnp.abs(spacing) < 3.0, jnp.sinc(spacing) * jnp.sinc(spacing / 3.0), 0.0)


def block_kernels(shift, spread, side):
    position = jnp.arange(side, dtype=jnp.float32)
    spacing = position[:, None] - position[None, :]
    weight_total = jnp.zeros_like(spread)
    summed = jnp.zeros((shift.shape[0], side, side), jnp.float32)
    for tap_shift in range(-PSF_R, PSF_R + 1):
        tap_weight = jnp.exp(-spread * float(tap_shift * tap_shift))
        weight_total = weight_total + tap_weight
        summed = summed + tap_weight[:, None, None] * lanczos_tap(
            spacing[None] + (shift[:, None, None] + float(tap_shift))
        )
    return summed / weight_total[:, None, None]


def filter_taps():
    values = [
        math.exp(-float(tap * tap) / (2.0 * det_sigma * det_sigma))
        for tap in range(-DET_R, DET_R + 1)
    ]
    whole = sum(values)
    return [value / whole for value in values]


def smooth_columns(padded, width):
    taps = filter_taps()
    total = jnp.zeros((padded.shape[0], width), jnp.float32)
    for index, tap in enumerate(range(-DET_R, DET_R + 1)):
        total = total + taps[index] * padded[:, DET_R + tap : DET_R + tap + width]
    return total


def smooth_rows(image):
    taps = filter_taps()
    height = image.shape[0]
    padded = jnp.pad(image, ((DET_R, DET_R), (0, 0)))
    total = jnp.zeros_like(image)
    for index, tap in enumerate(range(-DET_R, DET_R + 1)):
        total = total + taps[index] * padded[DET_R + tap : DET_R + tap + height, :]
    return total


def local(images, offsets, widths, weights, dest, cells, band_gain):
    side = images.shape[-1]
    count = images.shape[1]
    sect_count = lax.axis_size("sect")
    sub_count = lax.axis_size("sub")
    owners = sect_count * sub_count
    capacity = max(2, -(-2 * count // owners))
    slot_count = owners * capacity
    row_kernel = block_kernels(offsets[0, :, 0], widths[0, :, 0], side).astype(jnp.bfloat16)
    col_kernel = block_kernels(offsets[0, :, 1], widths[0, :, 1], side).astype(jnp.bfloat16)
    section = jnp.einsum(
        "bij,bjk->bik", row_kernel, images[0], preferred_element_type=jnp.float32
    ).astype(jnp.bfloat16)
    warped = jnp.einsum(
        "bij,bkj->bik", section, col_kernel, preferred_element_type=jnp.float32
    ).astype(jnp.bfloat16)
    target = dest[0]
    same_owner = target[:, None] == target[None, :]
    block_order = jnp.arange(count, dtype=jnp.int32)
    earlier = block_order[None, :] < block_order[:, None]
    rank_within = jnp.sum(jnp.logical_and(same_owner, earlier), axis=1)
    slot_index = target * capacity + rank_within
    placing = (jnp.arange(slot_count, dtype=jnp.int32)[:, None] == slot_index[None, :]).astype(
        jnp.bfloat16
    )
    packed = jnp.dot(
        placing, warped.reshape(count, side * side), preferred_element_type=jnp.float32
    ).astype(jnp.bfloat16)
    cell_weight = jnp.where(
        cells[0][:, None] == jnp.arange(CELL_DEV, dtype=jnp.int32)[None, :],
        weights[0][:, None],
        jnp.zeros((), jnp.bfloat16),
    )
    packed_weight = jnp.dot(placing, cell_weight, preferred_element_type=jnp.float32).astype(
        jnp.bfloat16
    )
    received, received_weight = (
        lax.all_to_all(
            packed.reshape(owners, capacity, side * side),
            ("sect", "sub"),
            split_axis=0,
            concat_axis=0,
            tiled=True,
        ),
        lax.all_to_all(
            packed_weight.reshape(owners, capacity, CELL_DEV),
            ("sect", "sub"),
            split_axis=0,
            concat_axis=0,
            tiled=True,
        ),
    )
    received = received.reshape(slot_count, side * side)
    received_weight = received_weight.reshape(slot_count, CELL_DEV)
    numerator = jnp.einsum(
        "sc,sp->cp", received_weight, received, preferred_element_type=jnp.float32
    )
    denominator = jnp.sum(received_weight.astype(jnp.float32), axis=0)
    cell_mean = (numerator / jnp.maximum(denominator, 1.0)[:, None]).astype(jnp.bfloat16)
    coadd = (
        cell_mean.reshape(CELL_DEV, side, side).transpose(1, 0, 2).reshape(side, CELL_DEV * side)
    )
    padded = extended(coadd, ((("sect", "sub"), 1),), DET_R)
    smoothed = smooth_rows(smooth_columns(padded.astype(jnp.float32), CELL_DEV * side))
    band_term = band_gain[0] * smoothed
    detection = lax.psum_scatter(band_term, "band", scatter_dimension=0, tiled=True)
    return (coadd[None], detection)


def solution(mesh):
    return jax.shard_map(
        local,
        mesh=mesh,
        in_specs=(
            P("band", ("groups", "sect", "sub"), None, None),
            P("band", ("groups", "sect", "sub"), None),
            P("band", ("groups", "sect", "sub"), None),
            P("band", ("groups", "sect", "sub")),
            P("band", ("groups", "sect", "sub")),
            P("band", ("groups", "sect", "sub")),
            P("band"),
        ),
        out_specs=(
            P("band", None, ("groups", "sect", "sub")),
            P("band", ("groups", "sect", "sub")),
        ),
        check_vma=False,
    )
```

profile of v0, /device:TPU:1, one launch (start us, length us, event | category | flops | bytes accessed | tf_op | source)
XLA Modules:
  0.0 584.2 jit_solution(12201559465395783674)
XLA Ops:
  7.2 1.0 convert_reduce_fusion.1
  9.3 0.9 convolution_convert_fusion.1
  11.0 6.4 %all-to-all-start = ((bf16[8,4,4]{2,1,0:T(4,128)(2,1)}), bf16[8,4,4]{2,1,0:T(4,128)(2,1)}, u32[]{:S(2)}, u32[]{:S(2)}) async-start(bf16[8,4,4]{2,1,0:T(4,128)(2,1)} %bitcast.5), calls=%async_computation | async-start | bytes 16384 | tf_op jit(solution)/shard_map/all_to_all | solution.py:118
  17.3 1.4 broadcast_add_fusion.31
  18.7 1.4 exponential_bitcast_fusion.17
  20.1 1.3 add_add_fusion.1
  21.5 1.3 slice_bitcast_fusion.1
  23.0 226.8 %fusion.1704 = bf16[16,256,256]{2,1,0:T(8,128)(2,1)S(1)} fusion(bf16[1,16,256,256]{3,2,1,0:T(8,128)(2,1)S(1)} %copy-done, f32[16]{0:T(128)S(1)} %get-tuple-element.59, f32[16]{0:T(128)S(1)} %get-tuple-element.61, f32[16]{0:T(128)S(1)} %get-tuple-element.62, f32[16]{0:T(128)S(1)} %get-tuple-element.63, f32[16]{0:T(128)S(1)} %get-tuple-element.64, ...), kind=kOutput, calls=%fused_computation.2054.clone.clone.clone.2 | convolution fusion | flops 1840250880 | bytes 4458176 | tf_op jit(solution)/shard_map/bij,bjk->bik/dot_general | solution.py:84
  250.1 179.8 %fusion.1639 = bf16[16,256,256]{2,1,0:T(8,128)(2,1)S(1)} fusion(f32[16]{0:T(128)S(1)} %copy-done.12, f32[16]{0:T(128)S(1)} %copy-done.29, f32[16]{0:T(128)S(1)} %copy-done.28, f32[16]{0:T(128)S(1)} %copy-done.27, f32[16]{0:T(128)S(1)} %copy-done.26, f32[16]{0:T(128)S(1)} %copy-done.25, f32[16]{0:T(128)S(1)} %copy-done.24, f32[16]{0:T(128)S(1)} %copy-done.23, ...), kind=kOutput, calls=%fused_computation.2085 | convolution fusion | flops 1840250880 | bytes 4458176 | tf_op jit(solution)/shard_map/bij,bkj->bik/dot_general | solution.py:87
  429.9 1.2 copy.29
  431.1 3.2 convolution_convert_fusion
  434.3 5.4 reshape.450
  439.7 5.1 all-to-all-start.1
  445.6 92.5 %all-to-all-done.1 = bf16[8,4,65536]{2,1,0:T(4,128)(2,1)} async-done(((bf16[8,4,65536]{2,1,0:T(4,128)(2,1)}), bf16[8,4,65536]{2,1,0:T(4,128)(2,1)}, u32[]{:S(2)}, u32[]{:S(2)}) %all-to-all-start.1) | async-done | bytes 4194336 | tf_op jit(solution)/shard_map/all_to_all | solution.py:111
  538.1 4.9 fusion.1
  543.2 1.9 collective-permute-start
  545.1 2.4 collective-permute-start.1
  548.2 2.5 collective-permute-done.1
  550.7 1.3 concatenate.3
  552.0 1.1 convert_element_type.46
  553.1 2.2 fusion.1644
  555.4 2.0 add_multiply_fusion.34
  557.8 1.2 broadcast_in_dim_reshape.3
  559.0 18.3 %reduce-scatter.2.cloned.1.call-done = f32[128,1024]{1,0:T(8,128)} async-done(((f32[256,1024]{1,0:T(8,128)}), f32[128,1024]{1,0:T(8,128)}) %reduce-scatter.2.cloned.1.call-update) | async-done | bytes 524304 | tf_op jit(solution)/shard_map/reduce_scatter | solution.py:139
  (73 shorter events, 3.4 us)
Async XLA Ops:
  11.0 428.8 %all-to-all-start = ((bf16[8,4,4]{2,1,0:T(4,128)(2,1)}), bf16[8,4,4]{2,1,0:T(4,128)(2,1)}, u32[]{:S(2)}, u32[]{:S(2)}) async-start(bf16[8,4,4]{2,1,0:T(4,128)(2,1)} %bitcast.5), calls=%async_computation | async-start | bytes 16384 | tf_op jit(solution)/shard_map/all_to_all | solution.py:118
  22.8 227.1 %copy-start.6 = (f32[16]{0:T(128)S(1)}, f32[16]{0:T(128)}, u32[]{:S(2)}) copy-start(f32[16]{0:T(128)} %get-tuple-element.11) | copy-start | bytes 196
  22.8 227.1 %copy-start.7 = (f32[16]{0:T(128)S(1)}, f32[16]{0:T(128)}, u32[]{:S(2)}) copy-start(f32[16]{0:T(128)} %get-tuple-element.12) | copy-start | bytes 196
  22.8 227.1 %copy-start.8 = (f32[16]{0:T(128)S(1)}, f32[16]{0:T(128)}, u32[]{:S(2)}) copy-start(f32[16]{0:T(128)} %get-tuple-element.13) | copy-start | bytes 196
  22.8 227.1 %copy-start.9 = (f32[16]{0:T(128)S(1)}, f32[16]{0:T(128)}, u32[]{:S(2)}) copy-start(f32[16]{0:T(128)} %get-tuple-element.14) | copy-start | bytes 196
  22.8 227.1 %copy-start.10 = (f32[16]{0:T(128)S(1)}, f32[16]{0:T(128)}, u32[]{:S(2)}) copy-start(f32[16]{0:T(128)} %get-tuple-element.15) | copy-start | bytes 196
  22.8 227.1 %copy-start.11 = (f32[16]{0:T(128)S(1)}, f32[16]{0:T(128)}, u32[]{:S(2)}) copy-start(f32[16]{0:T(128)} %get-tuple-element.24) | copy-start | bytes 196
  22.9 227.1 %copy-start.12 = (f32[16]{0:T(128)S(1)}, f32[16]{0:T(128)}, u32[]{:S(2)}) copy-start(f32[16]{0:T(128)} %get-tuple-element.60) | copy-start | bytes 196
  22.9 227.1 %copy-start.13 = (f32[16]{0:T(128)S(1)}, f32[16]{0:T(128)}, u32[]{:S(2)}) copy-start(f32[16]{0:T(128)} %get-tuple-element.58) | copy-start | bytes 196
  22.9 227.1 %copy-start.14 = (f32[16]{0:T(128)S(1)}, f32[16]{0:T(128)}, u32[]{:S(2)}) copy-start(f32[16]{0:T(128)} %get-tuple-element.26) | copy-start | bytes 196
  22.9 227.1 %copy-start.15 = (f32[16]{0:T(128)S(1)}, f32[16]{0:T(128)}, u32[]{:S(2)}) copy-start(f32[16]{0:T(128)} %get-tuple-element.27) | copy-start | bytes 196
  22.9 227.1 %copy-start.16 = (f32[16]{0:T(128)S(1)}, f32[16]{0:T(128)}, u32[]{:S(2)}) copy-start(f32[16]{0:T(128)} %get-tuple-element.28) | copy-start | bytes 196
  22.9 227.1 %copy-start.17 = (f32[16]{0:T(128)S(1)}, f32[16]{0:T(128)}, u32[]{:S(2)}) copy-start(f32[16]{0:T(128)} %get-tuple-element.29) | copy-start | bytes 196
  22.9 227.1 %copy-start.18 = (f32[16]{0:T(128)S(1)}, f32[16]{0:T(128)}, u32[]{:S(2)}) copy-start(f32[16]{0:T(128)} %get-tuple-element.30) | copy-start | bytes 196
  22.9 227.1 %copy-start.19 = (f32[16]{0:T(128)S(1)}, f32[16]{0:T(128)}, u32[]{:S(2)}) copy-start(f32[16]{0:T(128)} %get-tuple-element.31) | copy-start | bytes 196
  22.9 227.1 %copy-start.20 = (f32[16]{0:T(128)S(1)}, f32[16]{0:T(128)}, u32[]{:S(2)}) copy-start(f32[16]{0:T(128)} %get-tuple-element.32) | copy-start | bytes 196
  22.9 227.1 %copy-start.21 = (f32[16]{0:T(128)S(1)}, f32[16]{0:T(128)}, u32[]{:S(2)}) copy-start(f32[16]{0:T(128)} %get-tuple-element.33) | copy-start | bytes 196
  23.0 227.1 %copy-start.22 = (f32[16]{0:T(128)S(1)}, f32[16]{0:T(128)}, u32[]{:S(2)}) copy-start(f32[16]{0:T(128)} %get-tuple-element.34) | copy-start | bytes 196
  23.0 227.1 %copy-start.23 = (f32[16]{0:T(128)S(1)}, f32[16]{0:T(128)}, u32[]{:S(2)}) copy-start(f32[16]{0:T(128)} %get-tuple-element.35) | copy-start | bytes 196
  23.0 227.1 %copy-start.24 = (f32[16]{0:T(128)S(1)}, f32[16]{0:T(128)}, u32[]{:S(2)}) copy-start(f32[16]{0:T(128)} %get-tuple-element.36) | copy-start | bytes 196
  439.7 98.3 %all-to-all-start.1 = ((bf16[8,4,65536]{2,1,0:T(4,128)(2,1)}), bf16[8,4,65536]{2,1,0:T(4,128)(2,1)}, u32[]{:S(2)}, u32[]{:S(2)}) async-start(bf16[8,4,65536]{2,1,0:T(4,128)(2,1)} %reshape.450), calls=%async_computation.1 | async-start | bytes 8388608 | tf_op jit(solution)/shard_map/all_to_all | solution.py:111
  444.8 132.5 %reduce-scatter.2.cloned.1.call-start = ((), (), s32[]{:S(2)}) async-start(), calls=%async_computation.3 | async-start | bytes 1572864 | tf_op jit(solution)/shard_map/reduce_scatter | solution.py:139
  543.2 5.0 collective-permute-start
  545.1 5.6 collective-permute-start.1
  (11 other events, 1833.7 us)
Sparse Core Ops, SparseCore 0:
  557.5 19.7 reduce-scatter.1
where the time goes:
time: 585 us; the launch traced here: 584 us
  matrix products  416 us (71%)
  waiting for transfers between devices  113 us (19%)
  starting transfers between devices  15.8 us (3%)
  between operations  15.2 us (3%)
  local copies, waits for them, and re-layouts  12.3 us (2%)
  other arithmetic  11.9 us (2%)
    dot_general x1, matrix products, local(): jnp.einsum('bij,bjk->bik', row_kernel, images[0], preferred_element_type=...  227 us
    dot_general x1, matrix products, local(): jnp.einsum('bij,bkj->bik', section, col_kernel, preferred_element_type=jn...  180 us
    all_to_all x1, waiting for transfers between devices, local(): lax.all_to_all(packed.reshape(owners, capacity, side * side), ('sect', 's...  92.5 us
    reduce_scatter x1, waiting for transfers between devices, local(): lax.psum_scatter(band_term, 'band', scatter_dimension=0, tiled=True)  18.3 us
  transfers between devices with their start and end apart: 5, of which 3 were waited for; matrix products, arithmetic and copies ran while one was open for 73% of the time, Pallas kernels for 0%

commit v1 on v0

--- a/solution.py
+++ b/solution.py
@@ -31,17 +31,23 @@
 
 
 def block_kernels(shift, spread, side):
-    position = jnp.arange(side, dtype=jnp.float32)
-    spacing = position[:, None] - position[None, :]
+    band = PSF_R + 4
+    spacing = jnp.arange(-band, band + 1, dtype=jnp.float32)
     weight_total = jnp.zeros_like(spread)
-    summed = jnp.zeros((shift.shape[0], side, side), jnp.float32)
+    summed = jnp.zeros((shift.shape[0], 2 * band + 1), jnp.float32)
     for tap_shift in range(-PSF_R, PSF_R + 1):
         tap_weight = jnp.exp(-spread * float(tap_shift * tap_shift))
         weight_total = weight_total + tap_weight
-        summed = summed + tap_weight[:, None, None] * lanczos_tap(
-            spacing[None] + (shift[:, None, None] + float(tap_shift))
+        summed = summed + tap_weight[:, None] * lanczos_tap(
+            spacing[None] + (shift[:, None] + float(tap_shift))
         )
-    return summed / weight_total[:, None, None]
+    values = (summed / weight_total[:, None]).astype(jnp.bfloat16)
+    position = jnp.arange(side, dtype=jnp.int32)
+    lag = position[:, None] - position[None, :]
+    matrix = jnp.zeros((shift.shape[0], side, side), jnp.bfloat16)
+    for index in range(2 * band + 1):
+        matrix = jnp.where((lag == index - band)[None], values[:, index, None, None], matrix)
+    return matrix
 
 
 def filter_taps():
@@ -79,8 +85,8 @@
     owners = sect_count * sub_count
     capacity = max(2, -(-2 * count // owners))
     slot_count = owners * capacity
-    row_kernel = block_kernels(offsets[0, :, 0], widths[0, :, 0], side).astype(jnp.bfloat16)
-    col_kernel = block_kernels(offsets[0, :, 1], widths[0, :, 1], side).astype(jnp.bfloat16)
+    row_kernel = block_kernels(offsets[0, :, 0], widths[0, :, 0], side)
+    col_kernel = block_kernels(offsets[0, :, 1], widths[0, :, 1], side)
     section = jnp.einsum(
         "bij,bjk->bik", row_kernel, images[0], preferred_element_type=jnp.float32
     ).astype(jnp.bfloat16)

time: 585 us -> 193 us (0.33)
  matrix products: 416 us -> 18.4 us
    dot_general x1 -> x0, matrix products: 227 us -> none  [local(): jnp.einsum('bij,bjk->bik', row_kernel, images[0], preferred_element_type=...]
    dot_general x1, matrix products: 180 us -> 9.38 us  [local(): jnp.einsum('bij,bkj->bik', section, col_kernel, preferred_element_type=jn...]
  transfers between devices with their start and end apart: 5 -> 5, of which waited for: 3 -> 3; matrix products, arithmetic and copies ran while one was open for 73% -> 17% of each run, Pallas kernels for 0% -> 0%
where the time goes in v1:
time: 193 us; the launch traced here: 192 us
  waiting for transfers between devices  114 us (59%)
  matrix products  18.4 us (10%)
  starting transfers between devices  15.8 us (8%)
  local copies, waits for them, and re-layouts  15.2 us (8%)
  between operations  14.9 us (8%)
  other arithmetic  13.4 us (7%)
    all_to_all x1, waiting for transfers between devices, local(): lax.all_to_all(packed.reshape(owners, capacity, side * side), ('sect', 's...  93.2 us
    reduce_scatter x1, waiting for transfers between devices, local(): lax.psum_scatter(band_term, 'band', scatter_dimension=0, tiled=True)  18.3 us
    dot_general x1, matrix products, local(): jnp.einsum('bij,bkj->bik', section, col_kernel, preferred_element_type=jn...  9.38 us
    all_to_all x1, starting transfers between devices, local(): lax.all_to_all(packed_weight.reshape(owners, capacity, CELL_DEV), ('sect'...  6.38 us
    reshape x1, local copies, waits for them, and re-layouts, local(): packed.reshape(owners, capacity, side * side)  5.33 us
    all_to_all x1, starting transfers between devices, local(): lax.all_to_all(packed.reshape(owners, capacity, side * side), ('sect', 's...  5.1 us
    dot_general x1, matrix products, local(): jnp.einsum('sc,sp->cp', received_weight, received, preferred_element_type...  4.86 us
  transfers between devices with their start and end apart: 5, of which 3 were waited for; matrix products, arithmetic and copies ran while one was open for 17% of the time, Pallas kernels for 0%

profile of v1, /device:TPU:1, one launch (start us, length us, event | category | flops | bytes accessed | tf_op | source)
XLA Modules:
  0.0 191.7 jit_solution(4671404492673136787)
XLA Ops:
  7.2 1.0 convert_reduce_fusion.1
  8.8 0.9 convolution_convert_fusion.1
  10.5 6.4 %all-to-all-start = ((bf16[8,4,4]{2,1,0:T(4,128)(2,1)}), bf16[8,4,4]{2,1,0:T(4,128)(2,1)S(1)}, u32[]{:S(2)}, u32[]{:S(2)}) async-start(bf16[8,4,4]{2,1,0:T(4,128)(2,1)} %bitcast.5), calls=%async_computation | async-start | bytes 16384 | tf_op jit(solution)/shard_map/all_to_all | solution.py:124
  16.8 0.8 broadcast_add_fusion.31
  17.6 0.8 exponential_bitcast_fusion.17
  18.4 0.8 add_add_fusion.1
  19.9 1.0 divide_convert_fusion
  22.2 1.0 divide_convert_fusion.1
  26.5 9.4 %fusion.136 = bf16[16,256,256]{2,1,0:T(8,128)(2,1)} fusion(pred[256,256]{1,0:T(8,128)(4,1)S(1)} %get-tuple-element.124, pred[256,256]{1,0:T(8,128)(4,1)S(1)} %get-tuple-element.125, pred[256,256]{1,0:T(8,128)(4,1)S(1)} %get-tuple-element.126, pred[256,256]{1,0:T(8,128)(4,1)S(1)} %get-tuple-element.127, pred[256,256]{1,0:T(8,128)(4,1)S(1)} %get-tuple-element.128, ...), kind=kOutput, calls=%fused_computation.83 | convolution fusion | flops 1128267776 | bytes 5834304 | tf_op jit(solution)/shard_map/bij,bkj->bik/dot_general | solution.py:93
  35.9 2.8 %copy.29 = bf16[2,8,256,256]{3,1,2,0:T(8,128)(2,1)S(1)} copy(bf16[2,8,256,256]{3,2,1,0:T(8,128)(2,1)} %bitcast.288) | data formatting | bytes 4194304
  38.7 3.2 %convolution_convert_fusion = bf16[32,65536]{1,0:T(8,128)(2,1)} fusion(bf16[16,65536]{1,0:T(8,128)(2,1)S(1)} %bitcast.283, s32[16]{0:T(128)S(1)} %fusion.1864), kind=kOutput, calls=%fused_computation | convolution fusion | flops 69206528 | bytes 6291520 | tf_op jit(solution)/shard_map/dot_general | solution.py:105
  41.9 5.3 %reshape.745 = bf16[8,4,65536]{2,1,0:T(4,128)(2,1)} reshape(bf16[32,65536]{1,0:T(8,128)(2,1)} %convolution_convert_fusion) | data formatting | bytes 8388608 | tf_op jit(solution)/shard_map/reshape | solution.py:118
  47.3 5.1 %all-to-all-start.1 = ((bf16[8,4,65536]{2,1,0:T(4,128)(2,1)}), bf16[8,4,65536]{2,1,0:T(4,128)(2,1)}, u32[]{:S(2)}, u32[]{:S(2)}) async-start(bf16[8,4,65536]{2,1,0:T(4,128)(2,1)} %reshape.745), calls=%async_computation.1 | async-start | bytes 8388608 | tf_op jit(solution)/shard_map/all_to_all | solution.py:117
  52.4 93.2 %all-to-all-done.1 = bf16[8,4,65536]{2,1,0:T(4,128)(2,1)} async-done(((bf16[8,4,65536]{2,1,0:T(4,128)(2,1)}), bf16[8,4,65536]{2,1,0:T(4,128)(2,1)}, u32[]{:S(2)}, u32[]{:S(2)}) %all-to-all-start.1) | async-done | bytes 4194336 | tf_op jit(solution)/shard_map/all_to_all | solution.py:117
  145.6 4.9 %fusion.1 = bf16[4,65536]{1,0:T(4,128)(2,1)S(1)} fusion(bf16[8,4,4]{2,1,0:T(4,128)(2,1)S(1)} %all-to-all-done, bf16[8,4,65536]{2,1,0:T(4,128)(2,1)} %all-to-all-done.1, f32[4]{0:T(128)S(1)} %broadcast_maximum_fusion), kind=kOutput, calls=%fused_computation.3 | convolution fusion | flops 17301504 | bytes 4718864 | tf_op jit(solution)/shard_map/sc,sp->cp/dot_general | solution.py:134
  150.7 1.9 %collective-permute-start = (bf16[256,4]{1,0:T(8,128)(2,1)S(1)}, bf16[256,4]{1,0:T(8,128)(2,1)S(1)}, u32[]{:S(2)}, u32[]{:S(2)}) collective-permute-start(bf16[256,4]{1,0:T(8,128)(2,1)S(1)} %get-tuple-element.4), channel_id=1, source_target_pairs={{0,1},{1,4},{4,5},{5,8},{8,9},{9,12},{12,13},{2,3},{3,6},{6,7},{7,... | collective-permute-start | bytes 6152 | tf_op jit(solution)/shard_map/ppermute | solution.py:23
  152.6 2.4 %collective-permute-start.1 = (bf16[256,4]{1,0:T(8,128)(2,1)S(1)}, bf16[256,4]{1,0:T(8,128)(2,1)S(1)}, u32[]{:S(2)}, u32[]{:S(2)}) collective-permute-start(bf16[256,4]{1,0:T(8,128)(2,1)S(1)} %get-tuple-element.3), channel_id=1, source_target_pairs={{1,0},{4,1},{5,4},{8,5},{9,8},{12,9},{13,12},{3,2},{6,3},{7,6},{10... | collective-permute-start | bytes 6152 | tf_op jit(solution)/shard_map/ppermute | solution.py:24
  155.7 2.5 %collective-permute-done.1 = bf16[256,4]{1,0:T(8,128)(2,1)S(1)} collective-permute-done((bf16[256,4]{1,0:T(8,128)(2,1)S(1)}, bf16[256,4]{1,0:T(8,128)(2,1)S(1)}, u32[]{:S(2)}, u32[]{:S(2)}) %collective-permute-start.1) | collective-permute-done | bytes 2080 | tf_op jit(solution)/shard_map/ppermute | solution.py:24
  158.2 1.3 concatenate.3
  159.5 1.1 convert_element_type.46
  160.6 2.2 %fusion.145 = f32[256,1024]{1,0:T(8,128)S(1)} fusion(f32[256,1032]{1,0:T(8,128)S(1)} %convert_element_type.46), kind=kLoop, calls=%fused_computation.86 | loop fusion | flops 4456448 | bytes 10485760 | tf_op jit(solution)/shard_map/add | solution.py:66
  162.9 2.1 %add_multiply_fusion = f32[256,1024]{1,0:T(8,128)} fusion(f32[256,1024]{1,0:T(8,128)S(1)} %fusion.145, f32[]{:T(128)} %bitcast.282), kind=kLoop, calls=%fused_computation.102 | loop fusion | flops 4718592 | bytes 2097156 | tf_op jit(solution)/shard_map/mul | solution.py:144
  165.4 1.2 broadcast_in_dim_reshape.3
  166.5 18.3 %reduce-scatter.2.cloned.1.call-done = f32[128,1024]{1,0:T(8,128)} async-done(((f32[256,1024]{1,0:T(8,128)}), f32[128,1024]{1,0:T(8,128)}) %reduce-scatter.2.cloned.1.call-update) | async-done | bytes 524304 | tf_op jit(solution)/shard_map/reduce_scatter | solution.py:145
  (33 shorter events, 7.2 us)
Async XLA Ops:
  7.2 19.4 %copy-start = (bf16[1,16,256,256]{3,2,1,0:T(8,128)(2,1)S(1)}, bf16[1,16,256,256]{3,2,1,0:T(8,128)(2,1)}, u32[]{:S(2)}) copy-start(bf16[1,16,256,256]{3,2,1,0:T(8,128)(2,1)} %param.8) | copy-start | bytes 6291460
  10.5 36.8 %all-to-all-start = ((bf16[8,4,4]{2,1,0:T(4,128)(2,1)}), bf16[8,4,4]{2,1,0:T(4,128)(2,1)S(1)}, u32[]{:S(2)}, u32[]{:S(2)}) async-start(bf16[8,4,4]{2,1,0:T(4,128)(2,1)} %bitcast.5), calls=%async_computation | async-start | bytes 16384 | tf_op jit(solution)/shard_map/all_to_all | solution.py:124
  47.3 98.3 %all-to-all-start.1 = ((bf16[8,4,65536]{2,1,0:T(4,128)(2,1)}), bf16[8,4,65536]{2,1,0:T(4,128)(2,1)}, u32[]{:S(2)}, u32[]{:S(2)}) async-start(bf16[8,4,65536]{2,1,0:T(4,128)(2,1)} %reshape.745), calls=%async_computation.1 | async-start | bytes 8388608 | tf_op jit(solution)/shard_map/all_to_all | solution.py:117
  52.4 132.5 %reduce-scatter.2.cloned.1.call-start = ((), (), s32[]{:S(2)}) async-start(), calls=%async_computation.3 | async-start | bytes 1572864 | tf_op jit(solution)/shard_map/reduce_scatter | solution.py:145
  150.7 5.0 %collective-permute-start = (bf16[256,4]{1,0:T(8,128)(2,1)S(1)}, bf16[256,4]{1,0:T(8,128)(2,1)S(1)}, u32[]{:S(2)}, u32[]{:S(2)}) collective-permute-start(bf16[256,4]{1,0:T(8,128)(2,1)S(1)} %get-tuple-element.4), channel_id=1, source_target_pairs={{0,1},{1,4},{4,5},{5,8},{8,9},{9,12},{12,13},{2,3},{3,6},{6,7},{7,... | collective-permute-start | bytes 6152 | tf_op jit(solution)/shard_map/ppermute | solution.py:23
  152.6 5.6 %collective-permute-start.1 = (bf16[256,4]{1,0:T(8,128)(2,1)S(1)}, bf16[256,4]{1,0:T(8,128)(2,1)S(1)}, u32[]{:S(2)}, u32[]{:S(2)}) collective-permute-start(bf16[256,4]{1,0:T(8,128)(2,1)S(1)} %get-tuple-element.3), channel_id=1, source_target_pairs={{1,0},{4,1},{5,4},{8,5},{9,8},{12,9},{13,12},{3,2},{6,3},{7,6},{10... | collective-permute-start | bytes 6152 | tf_op jit(solution)/shard_map/ppermute | solution.py:24
Sparse Core Ops, SparseCore 0:
  165.1 19.7 reduce-scatter.1

commit v2 on v1

--- a/solution.py
+++ b/solution.py
@@ -67,13 +67,11 @@
     return total
 
 
-def smooth_rows(image):
+def smooth_rows_valid(framed, height):
     taps = filter_taps()
-    height = image.shape[0]
-    padded = jnp.pad(image, ((DET_R, DET_R), (0, 0)))
-    total = jnp.zeros_like(image)
+    total = jnp.zeros((height, framed.shape[1]), jnp.float32)
     for index, tap in enumerate(range(-DET_R, DET_R + 1)):
-        total = total + taps[index] * padded[DET_R + tap : DET_R + tap + height, :]
+        total = total + taps[index] * framed[DET_R + tap : DET_R + tap + height, :]
     return total
 
 
@@ -102,8 +100,8 @@
     placing = (jnp.arange(slot_count, dtype=jnp.int32)[:, None] == slot_index[None, :]).astype(
         jnp.bfloat16
     )
-    packed = jnp.dot(
-        placing, warped.reshape(count, side * side), preferred_element_type=jnp.float32
+    packed = jnp.einsum(
+        "sb,bij->sij", placing, warped, preferred_element_type=jnp.float32
     ).astype(jnp.bfloat16)
     cell_weight = jnp.where(
         cells[0][:, None] == jnp.arange(CELL_DEV, dtype=jnp.int32)[None, :],
@@ -115,7 +113,7 @@
     )
     received, received_weight = (
         lax.all_to_all(
-            packed.reshape(owners, capacity, side * side),
+            packed.reshape(owners, capacity, side, side),
             ("sect", "sub"),
             split_axis=0,
             concat_axis=0,
@@ -129,20 +127,26 @@
             tiled=True,
         ),
     )
-    received = received.reshape(slot_count, side * side)
+    received = received.reshape(slot_count, side, side)
     received_weight = received_weight.reshape(slot_count, CELL_DEV)
     numerator = jnp.einsum(
-        "sc,sp->cp", received_weight, received, preferred_element_type=jnp.float32
+        "sc,sij->cij", received_weight, received, preferred_element_type=jnp.float32
     )
     denominator = jnp.sum(received_weight.astype(jnp.float32), axis=0)
-    cell_mean = (numerator / jnp.maximum(denominator, 1.0)[:, None]).astype(jnp.bfloat16)
+    cell_mean = (numerator / jnp.maximum(denominator, 1.0)[:, None, None]).astype(jnp.bfloat16)
     coadd = (
         cell_mean.reshape(CELL_DEV, side, side).transpose(1, 0, 2).reshape(side, CELL_DEV * side)
     )
     padded = extended(coadd, ((("sect", "sub"), 1),), DET_R)
-    smoothed = smooth_rows(smooth_columns(padded.astype(jnp.float32), CELL_DEV * side))
-    band_term = band_gain[0] * smoothed
-    detection = lax.psum_scatter(band_term, "band", scatter_dimension=0, tiled=True)
+    band_count = lax.axis_size("band")
+    height = side // band_count
+    framed = jnp.pad(band_gain[0] * padded.astype(jnp.float32), ((DET_R, DET_R), (0, 0)))
+    windows = jnp.stack(
+        [framed[k * height : k * height + height + 2 * DET_R] for k in range(band_count)]
+    )
+    gathered = lax.all_to_all(windows, "band", split_axis=0, concat_axis=0, tiled=True)
+    combined = jnp.sum(gathered, axis=0)
+    detection = smooth_rows_valid(smooth_columns(combined, CELL_DEV * side), height)
     return (coadd[None], detection)
 
 

time: 193 us -> 184 us (0.953)
  between operations: 14.9 us -> 1.51 us
  waiting for transfers between devices: 114 us -> 109 us
  starting transfers between devices: 15.8 us -> 20.3 us
  local copies, waits for them, and re-layouts: 15.2 us -> 18.6 us
    reduce_scatter x1 -> x0, waiting for transfers between devices: 18.3 us -> none  [local(): lax.psum_scatter(band_term, 'band', scatter_dimension=0, tiled=True)]
    all_to_all x1 -> x2, waiting for transfers between devices: 93.2 us -> 107 us  [the longest x1 93.2 us: local(): lax.all_to_all(packed.reshape(owners, capacity, side, side), ('sect', 'su...]
    reshape x2, local copies, waits for them, and re-layouts: 5.38 us -> 12.5 us  [local(): packed.reshape(owners, capacity, side, side)]
    all_to_all x1 -> x2, starting transfers between devices: 5.1 us -> 9.62 us  [the longest x1 5.1 us: local(): lax.all_to_all(packed.reshape(owners, capacity, side, side), ('sect', 'su...]
    unnamed x4 -> x7, local copies, waits for them, and re-layouts: 2.85 us -> 0.11 us
    mul x1, other arithmetic: 2.06 us -> 0.08 us  [local(): band_gain[0] * padded.astype(jnp.float32)]
  transfers between devices with their start and end apart: 5 -> 5, of which waited for: 3 -> 3; matrix products, arithmetic and copies ran while one was open for 17% -> 21% of each run, Pallas kernels for 0% -> 0%
where the time goes in v2:
time: 184 us; the launch traced here: 183 us
  waiting for transfers between devices  109 us (59%)
  matrix products  20.3 us (11%)
  starting transfers between devices  20.3 us (11%)
  local copies, waits for them, and re-layouts  18.6 us (10%)
  other arithmetic  13.3 us (7%)
    all_to_all x1, waiting for transfers between devices, local(): lax.all_to_all(packed.reshape(owners, capacity, side, side), ('sect', 'su...  93.2 us
    all_to_all x1, waiting for transfers between devices, local(): lax.all_to_all(windows, 'band', split_axis=0, concat_axis=0, tiled=True)  13.5 us
    reshape x2, local copies, waits for them, and re-layouts, local(): packed.reshape(owners, capacity, side, side)  12.5 us
    dot_general x1, matrix products, local(): jnp.einsum('bij,bkj->bik', section, col_kernel, preferred_element_type=jn...  9.39 us
    all_to_all x1, starting transfers between devices, local(): lax.all_to_all(packed_weight.reshape(owners, capacity, CELL_DEV), ('sect'...  6.38 us
    dot_general x1, matrix products, local(): jnp.einsum('sb,bij->sij', placing, warped, preferred_element_type=jnp.flo...  5.12 us
    all_to_all x1, starting transfers between devices, local(): lax.all_to_all(packed.reshape(owners, capacity, side, side), ('sect', 'su...  5.1 us
    dot_general x1, matrix products, local(): jnp.einsum('sc,sij->cij', received_weight, received, preferred_element_ty...  4.86 us
  transfers between devices with their start and end apart: 5, of which 3 were waited for; matrix products, arithmetic and copies ran while one was open for 21% of the time, Pallas kernels for 0%

profile of v2, /device:TPU:1, one launch (start us, length us, event | category | flops | bytes accessed | tf_op | source)
XLA Modules:
  0.0 183.1 jit_solution(14526151122003138670)
XLA Ops:
  0.6 1.0 convert_reduce_fusion.1
  2.3 0.9 convolution_convert_fusion.1
  3.9 6.4 %all-to-all-start = ((bf16[8,4,4]{2,1,0:T(4,128)(2,1)}), bf16[8,4,4]{2,1,0:T(4,128)(2,1)S(1)}, u32[]{:S(2)}, u32[]{:S(2)}) async-start(bf16[8,4,4]{2,1,0:T(4,128)(2,1)} %bitcast.5), calls=%async_computation | async-start | bytes 16384 | tf_op jit(solution)/shard_map/all_to_all | solution.py:122
  11.1 0.8 exponential_bitcast_fusion.17
  11.8 0.8 add_add_fusion.1
  13.4 1.0 divide_convert_fusion
  15.7 1.0 divide_convert_fusion.1
  20.0 9.4 %fusion.135 = bf16[16,256,256]{2,1,0:T(8,128)(2,1)} fusion(pred[256,256]{1,0:T(8,128)(4,1)S(1)} %get-tuple-element.124, pred[256,256]{1,0:T(8,128)(4,1)S(1)} %get-tuple-element.125, pred[256,256]{1,0:T(8,128)(4,1)S(1)} %get-tuple-element.126, pred[256,256]{1,0:T(8,128)(4,1)S(1)} %get-tuple-element.127, pred[256,256]{1,0:T(8,128)(4,1)S(1)} %get-tuple-element.128, ...), kind=kOutput, calls=%fused_computation.81 | convolution fusion | flops 1128267776 | bytes 5834304 | tf_op jit(solution)/shard_map/bij,bkj->bik/dot_general | solution.py:91
  29.4 5.1 %convolution_convert_fusion = bf16[32,256,256]{2,0,1:T(8,128)(2,1)} fusion(bf16[16,256,256]{2,1,0:T(8,128)(2,1)} %fusion.135, s32[16]{0:T(128)S(1)} %fusion.1873), kind=kOutput, calls=%fused_computation | convolution fusion | flops 69206528 | bytes 6291520 | tf_op jit(solution)/shard_map/sb,bij->sij/dot_general | solution.py:103
  34.5 6.9 %reshape.738 = bf16[8,4,256,256]{3,1,0,2:T(4,128)(2,1)} reshape(bf16[32,256,256]{2,0,1:T(8,128)(2,1)} %convolution_convert_fusion) | data formatting | bytes 8388608 | tf_op jit(solution)/shard_map/reshape | solution.py:116
  41.5 5.6 %copy.20 = bf16[8,4,256,256]{3,1,2,0:T(4,128)(2,1)} copy(bf16[8,4,256,256]{3,1,0,2:T(4,128)(2,1)} %reshape.738) | data formatting | bytes 8388608 | tf_op jit(solution)/shard_map/reshape | solution.py:116
  47.0 5.1 %all-to-all-start.1 = ((bf16[8,4,256,256]{3,1,2,0:T(4,128)(2,1)}), bf16[8,4,256,256]{3,1,2,0:T(4,128)(2,1)}, u32[]{:S(2)}, u32[]{:S(2)}) async-start(bf16[8,4,256,256]{3,1,2,0:T(4,128)(2,1)} %copy.20), calls=%async_computation.1 | async-start | bytes 8388608 | tf_op jit(solution)/shard_map/all_to_all | solution.py:115
  52.2 93.2 %all-to-all-done.1 = bf16[8,4,256,256]{3,1,2,0:T(4,128)(2,1)} async-done(((bf16[8,4,256,256]{3,1,2,0:T(4,128)(2,1)}), bf16[8,4,256,256]{3,1,2,0:T(4,128)(2,1)}, u32[]{:S(2)}, u32[]{:S(2)}) %all-to-all-start.1) | async-done | bytes 4194336 | tf_op jit(solution)/shard_map/all_to_all | solution.py:115
  145.4 4.9 %fusion.145 = bf16[4,256,256]{2,0,1:T(4,128)(2,1)S(1)} fusion(bf16[8,4,256,256]{3,1,2,0:T(4,128)(2,1)} %all-to-all-done.1, f32[4]{0:T(128)S(1)} %broadcast_maximum_fusion, bf16[8,4,4]{2,1,0:T(4,128)(2,1)S(1)} %all-to-all-done), kind=kOutput, calls=%fused_computation.89 | convolution fusion | flops 17301504 | bytes 4718864 | tf_op jit(solution)/shard_map/sc,sij->cij/dot_general | solution.py:132
  150.4 1.9 %collective-permute-start = (bf16[256,4]{1,0:T(8,128)(2,1)S(1)}, bf16[256,4]{1,0:T(8,128)(2,1)S(1)}, u32[]{:S(2)}, u32[]{:S(2)}) collective-permute-start(bf16[256,4]{1,0:T(8,128)(2,1)S(1)} %get-tuple-element.6), channel_id=1, source_target_pairs={{0,1},{1,4},{4,5},{5,8},{8,9},{9,12},{12,13},{2,3},{3,6},{6,7},{7,... | collective-permute-start | bytes 6152 | tf_op jit(solution)/shard_map/ppermute | solution.py:23
  152.4 2.4 %collective-permute-start.1 = (bf16[256,4]{1,0:T(8,128)(2,1)S(1)}, bf16[256,4]{1,0:T(8,128)(2,1)S(1)}, u32[]{:S(2)}, u32[]{:S(2)}) collective-permute-start(bf16[256,4]{1,0:T(8,128)(2,1)S(1)} %get-tuple-element.5), channel_id=1, source_target_pairs={{1,0},{4,1},{5,4},{8,5},{9,8},{12,9},{13,12},{3,2},{6,3},{7,6},{10... | collective-permute-start | bytes 6152 | tf_op jit(solution)/shard_map/ppermute | solution.py:24
  155.5 2.5 %collective-permute-done.1 = bf16[256,4]{1,0:T(8,128)(2,1)S(1)} collective-permute-done((bf16[256,4]{1,0:T(8,128)(2,1)S(1)}, bf16[256,4]{1,0:T(8,128)(2,1)S(1)}, u32[]{:S(2)}, u32[]{:S(2)}) %collective-permute-start.1) | collective-permute-done | bytes 2080 | tf_op jit(solution)/shard_map/ppermute | solution.py:24
  158.8 1.2 pad_maximum_fusion
  160.0 4.5 %all-to-all-start.2 = ((f32[2,136,1032]{2,1,0:T(8,128)}), f32[2,136,1032]{2,1,0:T(8,128)}, u32[]{:S(2)}, u32[]{:S(2)}) async-start(f32[2,136,1032]{2,1,0:T(8,128)} %pad_maximum_fusion), calls=%async_computation.2 | async-start | bytes 2506752 | tf_op jit(solution)/shard_map/all_to_all | solution.py:147
  164.5 1.2 broadcast_in_dim_reshape.3
  165.7 13.5 %all-to-all-done.2 = f32[2,136,1032]{2,1,0:T(8,128)} async-done(((f32[2,136,1032]{2,1,0:T(8,128)}), f32[2,136,1032]{2,1,0:T(8,128)}, u32[]{:S(2)}, u32[]{:S(2)}) %all-to-all-start.2) | async-done | bytes 1122848 | tf_op jit(solution)/shard_map/all_to_all | solution.py:147
  179.2 1.4 reduce_sum.32
  180.6 1.2 fusion.225
  181.8 1.3 fusion.233
  (37 shorter events, 8.3 us)
Async XLA Ops:
  0.6 19.4 %copy-start = (bf16[1,16,256,256]{3,2,1,0:T(8,128)(2,1)S(1)}, bf16[1,16,256,256]{3,2,1,0:T(8,128)(2,1)}, u32[]{:S(2)}) copy-start(bf16[1,16,256,256]{3,2,1,0:T(8,128)(2,1)} %param.8) | copy-start | bytes 6291460
  3.9 43.1 %all-to-all-start = ((bf16[8,4,4]{2,1,0:T(4,128)(2,1)}), bf16[8,4,4]{2,1,0:T(4,128)(2,1)S(1)}, u32[]{:S(2)}, u32[]{:S(2)}) async-start(bf16[8,4,4]{2,1,0:T(4,128)(2,1)} %bitcast.5), calls=%async_computation | async-start | bytes 16384 | tf_op jit(solution)/shard_map/all_to_all | solution.py:122
  47.0 98.4 %all-to-all-start.1 = ((bf16[8,4,256,256]{3,1,2,0:T(4,128)(2,1)}), bf16[8,4,256,256]{3,1,2,0:T(4,128)(2,1)}, u32[]{:S(2)}, u32[]{:S(2)}) async-start(bf16[8,4,256,256]{3,1,2,0:T(4,128)(2,1)} %copy.20), calls=%async_computation.1 | async-start | bytes 8388608 | tf_op jit(solution)/shard_map/all_to_all | solution.py:115
  150.2 5.2 %copy-start.1 = (bf16[4,256,256]{2,0,1:T(4,128)(2,1)}, bf16[4,256,256]{2,0,1:T(4,128)(2,1)S(1)}, u32[]{:S(2)}) copy-start(bf16[4,256,256]{2,0,1:T(4,128)(2,1)S(1)} %fusion.145) | copy-start | bytes 1572868
  150.4 5.0 %collective-permute-start = (bf16[256,4]{1,0:T(8,128)(2,1)S(1)}, bf16[256,4]{1,0:T(8,128)(2,1)S(1)}, u32[]{:S(2)}, u32[]{:S(2)}) collective-permute-start(bf16[256,4]{1,0:T(8,128)(2,1)S(1)} %get-tuple-element.6), channel_id=1, source_target_pairs={{0,1},{1,4},{4,5},{5,8},{8,9},{9,12},{12,13},{2,3},{3,6},{6,7},{7,... | collective-permute-start | bytes 6152 | tf_op jit(solution)/shard_map/ppermute | solution.py:23
  152.4 5.6 %collective-permute-start.1 = (bf16[256,4]{1,0:T(8,128)(2,1)S(1)}, bf16[256,4]{1,0:T(8,128)(2,1)S(1)}, u32[]{:S(2)}, u32[]{:S(2)}) collective-permute-start(bf16[256,4]{1,0:T(8,128)(2,1)S(1)} %get-tuple-element.5), channel_id=1, source_target_pairs={{1,0},{4,1},{5,4},{8,5},{9,8},{12,9},{13,12},{3,2},{6,3},{7,6},{10... | collective-permute-start | bytes 6152 | tf_op jit(solution)/shard_map/ppermute | solution.py:24
  158.8 5.8 %copy-start.2 = (bf16[4,256,256]{2,0,1:T(4,128)(2,1)S(1)}, bf16[4,256,256]{2,0,1:T(4,128)(2,1)}, u32[]{:S(2)}) copy-start(bf16[4,256,256]{2,0,1:T(4,128)(2,1)} %copy-done.1) | copy-start | bytes 1572868
  160.0 19.2 %all-to-all-start.2 = ((f32[2,136,1032]{2,1,0:T(8,128)}), f32[2,136,1032]{2,1,0:T(8,128)}, u32[]{:S(2)}, u32[]{:S(2)}) async-start(f32[2,136,1032]{2,1,0:T(8,128)} %pad_maximum_fusion), calls=%async_computation.2 | async-start | bytes 2506752 | tf_op jit(solution)/shard_map/all_to_all | solution.py:147

commit v3 on v2

--- a/solution.py
+++ b/solution.py
@@ -97,12 +97,10 @@
     earlier = block_order[None, :] < block_order[:, None]
     rank_within = jnp.sum(jnp.logical_and(same_owner, earlier), axis=1)
     slot_index = target * capacity + rank_within
-    placing = (jnp.arange(slot_count, dtype=jnp.int32)[:, None] == slot_index[None, :]).astype(
-        jnp.bfloat16
-    )
-    packed = jnp.einsum(
-        "sb,bij->sij", placing, warped, preferred_element_type=jnp.float32
-    ).astype(jnp.bfloat16)
+    matching = jnp.arange(slot_count, dtype=jnp.int32)[:, None] == slot_index[None, :]
+    source = jnp.sum(jnp.where(matching, block_order[None, :], 0), axis=1)
+    placing = matching.astype(jnp.bfloat16)
+    packed = jnp.take(warped, source, axis=0, mode="clip")
     cell_weight = jnp.where(
         cells[0][:, None] == jnp.arange(CELL_DEV, dtype=jnp.int32)[None, :],
         weights[0][:, None],
@@ -113,7 +111,7 @@
     )
     received, received_weight = (
         lax.all_to_all(
-            packed.reshape(owners, capacity, side, side),
+            packed.reshape(owners, capacity * side, side),
             ("sect", "sub"),
             split_axis=0,
             concat_axis=0,
@@ -129,8 +127,10 @@
     )
     received = received.reshape(slot_count, side, side)
     received_weight = received_weight.reshape(slot_count, CELL_DEV)
-    numerator = jnp.einsum(
-        "sc,sij->cij", received_weight, received, preferred_element_type=jnp.float32
+    numerator = jnp.sum(
+        received_weight.astype(jnp.float32)[:, :, None, None]
+        * received.astype(jnp.float32)[:, None],
+        axis=0,
     )
     denominator = jnp.sum(received_weight.astype(jnp.float32), axis=0)
     cell_mean = (numerator / jnp.maximum(denominator, 1.0)[:, None, None]).astype(jnp.bfloat16)

time: 184 us -> 216 us (1.17)
  local copies, waits for them, and re-layouts: 18.6 us -> 40.4 us
  other arithmetic: 13.3 us -> 32.9 us
  matrix products: 20.3 us -> 10.4 us
    unnamed x7 -> x15, local copies, waits for them, and re-layouts: 0.11 us -> 23 us
    reshape x2 -> x0, local copies, waits for them, and re-layouts: 12.5 us -> none  [local(): packed.reshape(owners, capacity, side, side)]
    dot_general x2 -> x0, matrix products: 9.98 us -> none  [the longest x1 5.12 us: local(): jnp.einsum('sb,bij->sij', placing, warped, preferred_element_type=jnp.flo...]
    reduce_sum x0 -> x2, other arithmetic: none -> 8.41 us  [the longest x1 7.13 us: local(): jnp.sum(received_weight.astype(jnp.float32)[:, :, None, None] * received....]
    convert_element_type x0 -> x2, other arithmetic: none -> 7.42 us  [the longest x1 6.48 us: local(): received.astype(jnp.float32)[:, None]]
    gather x0 -> x1, local copies, waits for them, and re-layouts: none -> 4.36 us  [local(): packed = jnp.take(warped, source, axis=0, mode='clip')]
    slice x0 -> x1, local copies, waits for them, and re-layouts: none -> 3.47 us  [smooth_columns(): total = total + taps[index] * padded[:, DET_R + tap:DET_R + tap + width]]
    another operation x1 -> x2, local copies, waits for them, and re-layouts: 0.09 us -> 3.35 us  [local(): jnp.stack([framed[k * height:k * height + height + 2 * DET_R] for k in ra...]
  transfers between devices with their start and end apart: 5 -> 5, of which waited for: 3 -> 3; matrix products, arithmetic and copies ran while one was open for 21% -> 12% of each run, Pallas kernels for 0% -> 0%
where the time goes in v3:
time: 216 us; the launch traced here: 215 us
  waiting for transfers between devices  109 us (50%)
  local copies, waits for them, and re-layouts  40.4 us (19%)
  other arithmetic  32.9 us (15%)
  starting transfers between devices  20.3 us (9%)
  matrix products  10.4 us (5%)
    all_to_all x1, waiting for transfers between devices, local(): lax.all_to_all(packed.reshape(owners, capacity * side, side), ('sect', 's...  93 us
    unnamed x15, local copies, waits for them, and re-layouts  23 us
    all_to_all x1, waiting for transfers between devices, local(): lax.all_to_all(windows, 'band', split_axis=0, concat_axis=0, tiled=True)  14.2 us
    dot_general x1, matrix products, local(): jnp.einsum('bij,bkj->bik', section, col_kernel, preferred_element_type=jn...  9.49 us
    reduce_sum x1, other arithmetic, local(): jnp.sum(received_weight.astype(jnp.float32)[:, :, None, None] * received....  7.13 us
    convert_element_type x1, other arithmetic, local(): received.astype(jnp.float32)[:, None]  6.48 us
    all_to_all x1, starting transfers between devices, local(): lax.all_to_all(packed_weight.reshape(owners, capacity, CELL_DEV), ('sect'...  6.38 us
    all_to_all x1, starting transfers between devices, local(): lax.all_to_all(packed.reshape(owners, capacity * side, side), ('sect', 's...  5.1 us
  transfers between devices with their start and end apart: 5, of which 3 were waited for; matrix products, arithmetic and copies ran while one was open for 12% of the time, Pallas kernels for 0%

profile of v3, /device:TPU:1, one launch (start us, length us, event | category | flops | bytes accessed | tf_op | source)
XLA Modules:
  0.0 214.5 jit_solution(9942672244250965511)
XLA Ops:
  4.4 6.4 %all-to-all-start = ((bf16[8,4,4]{1,2,0:T(4,128)(2,1)}), bf16[8,4,4]{1,2,0:T(4,128)(2,1)S(1)}, u32[]{:S(2)}, u32[]{:S(2)}) async-start(bf16[8,4,4]{1,2,0:T(4,128)(2,1)} %copy.23), calls=%async_computation | async-start | bytes 16384 | tf_op jit(solution)/shard_map/all_to_all | solution.py:120
  21.8 9.5 %fusion.134 = bf16[16,256,256]{2,1,0:T(8,128)(2,1)} fusion(pred[256,256]{1,0:T(8,128)(4,1)S(1)} %get-tuple-element.137, pred[256,256]{1,0:T(8,128)(4,1)S(1)} %get-tuple-element.138, pred[256,256]{1,0:T(8,128)(4,1)S(1)} %get-tuple-element.139, pred[256,256]{1,0:T(8,128)(4,1)S(1)} %get-tuple-element.140, pred[256,256]{1,0:T(8,128)(4,1)S(1)} %get-tuple-element.141, ...), kind=kOutput, calls=%fused_computation.82 | convolution fusion | flops 1128267776 | bytes 5834304 | tf_op jit(solution)/shard_map/bij,bkj->bik/dot_general | solution.py:91
  31.9 4.4 %gather_fusion = bf16[32,256,256]{2,1,0:T(8,128)(2,1)} fusion(bf16[16,256,256]{2,1,0:T(8,128)(2,1)} %fusion.134, s32[1024]{0:T(1024)S(1)} %pad_clamp_fusion), kind=kCustom, calls=%fused_computation | custom fusion | bytes 8388736 | tf_op jit(solution)/shard_map/jit(_take)/gather | solution.py:103
  36.3 5.1 %all-to-all-start.1 = ((bf16[8,1024,256]{2,1,0:T(8,128)(2,1)}), bf16[8,1024,256]{2,1,0:T(8,128)(2,1)}, u32[]{:S(2)}, u32[]{:S(2)}) async-start(bf16[8,1024,256]{2,1,0:T(8,128)(2,1)} %bitcast.274), calls=%async_computation.1 | async-start | bytes 8388608 | tf_op jit(solution)/shard_map/all_to_all | solution.py:113
  41.7 93.0 %all-to-all-done.1 = bf16[8,1024,256]{2,1,0:T(8,128)(2,1)} async-done(((bf16[8,1024,256]{2,1,0:T(8,128)(2,1)}), bf16[8,1024,256]{2,1,0:T(8,128)(2,1)}, u32[]{:S(2)}, u32[]{:S(2)}) %all-to-all-start.1) | async-done | bytes 4194336 | tf_op jit(solution)/shard_map/all_to_all | solution.py:113
  134.7 6.5 %convert.2 = f32[32,256,256]{2,1,0:T(8,128)} convert(bf16[32,256,256]{2,1,0:T(8,128)(2,1)} %bitcast.85) | non-fusion elementwise | flops 2097152 | bytes 12582912 | tf_op jit(solution)/shard_map/convert_element_type | solution.py:132
  141.1 7.1 %multiply_reduce_fusion = f32[4,256,256]{2,1,0:T(8,128)S(1)} fusion(f32[32,256,256]{2,1,0:T(8,128)} %convert.2, f32[32,4]{1,0:T(8,128)S(1)} %bitcast.278), kind=kLoop, calls=%fused_computation.1 | loop fusion | flops 16515072 | bytes 9437696 | tf_op jit(solution)/shard_map/reduce_sum | solution.py:130
  150.5 1.9 collective-permute-start
  152.4 2.4 %collective-permute-start.1 = (bf16[256,4]{0,1:T(4,128)(2,1)S(1)}, bf16[256,4]{0,1:T(4,128)(2,1)S(1)}, u32[]{:S(2)}, u32[]{:S(2)}) collective-permute-start(bf16[256,4]{0,1:T(4,128)(2,1)S(1)} %get-tuple-element.18), channel_id=1, source_target_pairs={{1,0},{4,1},{5,4},{8,5},{9,8},{12,9},{13,12},{3,2},{6,3},{7,6},{10... | collective-permute-start | bytes 6152 | tf_op jit(solution)/shard_map/ppermute | solution.py:24
  155.5 1.8 collective-permute-done.1
  158.9 1.6 pad_maximum_fusion
  160.5 2.7 %copy.28 = f32[2,136,1032]{2,1,0:T(8,128)} copy(f32[2,136,1032]{1,2,0:T(8,128)} %pad_maximum_fusion) | data formatting | bytes 2245632 | tf_op jit(solution)/shard_map/stack | solution.py:144
  163.2 4.5 %all-to-all-start.2 = ((f32[2,136,1032]{2,1,0:T(8,128)}), f32[2,136,1032]{2,1,0:T(8,128)}, u32[]{:S(2)}, u32[]{:S(2)}) async-start(f32[2,136,1032]{2,1,0:T(8,128)} %copy.28), calls=%async_computation.2 | async-start | bytes 2506752 | tf_op jit(solution)/shard_map/all_to_all | solution.py:147
  168.7 14.2 %all-to-all-done.2 = f32[2,136,1032]{2,1,0:T(8,128)} async-done(((f32[2,136,1032]{2,1,0:T(8,128)}), f32[2,136,1032]{2,1,0:T(8,128)}, u32[]{:S(2)}, u32[]{:S(2)}) %all-to-all-start.2) | async-done | bytes 1122848 | tf_op jit(solution)/shard_map/all_to_all | solution.py:147
  184.4 3.5 %fusion.1863 = (f32[136,1024]{1,0:T(8,128)}, f32[136,1024]{1,0:T(8,128)}, f32[136,1024]{1,0:T(8,128)}, f32[136,1024]{1,0:T(8,128)}, f32[136,1024]{1,0:T(8,128)},...) fusion(f32[136,1032]{1,0:T(8,128)S(1)} %reduce_sum.52), kind=kLoop, calls=%fused_computation.2385 | loop fusion | bytes 10027008 | tf_op jit(solution)/shard_map/slice | solution.py:66
  189.3 2.4 %copy.36 = f32[136,1024]{0,1:T(8,128)} copy(f32[136,1024]{1,0:T(8,128)} %get-tuple-element.16) | data formatting | bytes 1114112
  191.6 2.4 %copy.37 = f32[136,1024]{0,1:T(8,128)} copy(f32[136,1024]{1,0:T(8,128)} %get-tuple-element.15) | data formatting | bytes 1114112
  194.0 2.4 %copy.38 = f32[136,1024]{0,1:T(8,128)} copy(f32[136,1024]{1,0:T(8,128)} %get-tuple-element.14) | data formatting | bytes 1114112
  196.4 2.4 %copy.39 = f32[136,1024]{0,1:T(8,128)} copy(f32[136,1024]{1,0:T(8,128)} %get-tuple-element.13) | data formatting | bytes 1114112
  198.8 2.4 %copy.40 = f32[136,1024]{0,1:T(8,128)} copy(f32[136,1024]{1,0:T(8,128)} %get-tuple-element.12) | data formatting | bytes 1114112
  201.1 2.4 %copy.41 = f32[136,1024]{0,1:T(8,128)} copy(f32[136,1024]{1,0:T(8,128)} %get-tuple-element.11) | data formatting | bytes 1114112
  203.5 2.4 %copy.42 = f32[136,1024]{0,1:T(8,128)} copy(f32[136,1024]{1,0:T(8,128)} %get-tuple-element.10) | data formatting | bytes 1114112
  205.9 2.4 %copy.43 = f32[136,1024]{0,1:T(8,128)} copy(f32[136,1024]{1,0:T(8,128)} %get-tuple-element.17) | data formatting | bytes 1114112
  208.3 4.1 %multiply_add_fusion = f32[136,1024]{0,1:T(8,128)S(1)} fusion(f32[136,1024]{0,1:T(8,128)} %copy.43, f32[136,1024]{0,1:T(8,128)} %copy.42, f32[136,1024]{0,1:T(8,128)} %copy.41, f32[136,1024]{0,1:T(8,128)} %copy.40, f32[136,1024]{0,1:T(8,128)} %copy.39, f32[136,1024]{0,1:T(8,128)} %copy.38, f32[136,1024]{0,1:T(8,128)} %copy.37, f32[136,1024]{0,1:T(8,128)} %copy.36, ...), kind=kLoop, calls=%fused_computation.89 | loop fusion | flops 2367488 | bytes 5570560 | tf_op jit(solution)/shard_map/add | solution.py:66
  (51 shorter events, 25.4 us)
Async XLA Ops:
  0.6 21.2 %copy-start = (bf16[1,16,256,256]{3,2,1,0:T(8,128)(2,1)S(1)}, bf16[1,16,256,256]{3,2,1,0:T(8,128)(2,1)}, u32[]{:S(2)}) copy-start(bf16[1,16,256,256]{3,2,1,0:T(8,128)(2,1)} %param.8) | copy-start | bytes 6291460
  2.3 0.5 copy-start.1
  4.4 31.9 %all-to-all-start = ((bf16[8,4,4]{1,2,0:T(4,128)(2,1)}), bf16[8,4,4]{1,2,0:T(4,128)(2,1)S(1)}, u32[]{:S(2)}, u32[]{:S(2)}) async-start(bf16[8,4,4]{1,2,0:T(4,128)(2,1)} %copy.23), calls=%async_computation | async-start | bytes 16384 | tf_op jit(solution)/shard_map/all_to_all | solution.py:120
  36.3 98.3 %all-to-all-start.1 = ((bf16[8,1024,256]{2,1,0:T(8,128)(2,1)}), bf16[8,1024,256]{2,1,0:T(8,128)(2,1)}, u32[]{:S(2)}, u32[]{:S(2)}) async-start(bf16[8,1024,256]{2,1,0:T(8,128)(2,1)} %bitcast.274), calls=%async_computation.1 | async-start | bytes 8388608 | tf_op jit(solution)/shard_map/all_to_all | solution.py:113
  150.5 5.0 %collective-permute-start = (bf16[256,4]{0,1:T(4,128)(2,1)S(1)}, bf16[256,4]{0,1:T(4,128)(2,1)S(1)}, u32[]{:S(2)}, u32[]{:S(2)}) collective-permute-start(bf16[256,4]{0,1:T(4,128)(2,1)S(1)} %get-tuple-element.19), channel_id=1, source_target_pairs={{0,1},{1,4},{4,5},{5,8},{8,9},{9,12},{12,13},{2,3},{3,6},{6,7},{7,... | collective-permute-start | bytes 6152 | tf_op jit(solution)/shard_map/ppermute | solution.py:23
  152.4 4.9 %collective-permute-start.1 = (bf16[256,4]{0,1:T(4,128)(2,1)S(1)}, bf16[256,4]{0,1:T(4,128)(2,1)S(1)}, u32[]{:S(2)}, u32[]{:S(2)}) collective-permute-start(bf16[256,4]{0,1:T(4,128)(2,1)S(1)} %get-tuple-element.18), channel_id=1, source_target_pairs={{1,0},{4,1},{5,4},{8,5},{9,8},{12,9},{13,12},{3,2},{6,3},{7,6},{10... | collective-permute-start | bytes 6152 | tf_op jit(solution)/shard_map/ppermute | solution.py:24
  163.2 19.7 %all-to-all-start.2 = ((f32[2,136,1032]{2,1,0:T(8,128)}), f32[2,136,1032]{2,1,0:T(8,128)}, u32[]{:S(2)}, u32[]{:S(2)}) async-start(f32[2,136,1032]{2,1,0:T(8,128)} %copy.28), calls=%async_computation.2 | async-start | bytes 2506752 | tf_op jit(solution)/shard_map/all_to_all | solution.py:147

commit v4 on v3

--- a/solution.py
+++ b/solution.py
@@ -127,10 +127,8 @@
     )
     received = received.reshape(slot_count, side, side)
     received_weight = received_weight.reshape(slot_count, CELL_DEV)
-    numerator = jnp.sum(
-        received_weight.astype(jnp.float32)[:, :, None, None]
-        * received.astype(jnp.float32)[:, None],
-        axis=0,
+    numerator = jnp.einsum(
+        "sc,sij->cij", received_weight, received, preferred_element_type=jnp.float32
     )
     denominator = jnp.sum(received_weight.astype(jnp.float32), axis=0)
     cell_mean = (numerator / jnp.maximum(denominator, 1.0)[:, None, None]).astype(jnp.bfloat16)

time: 216 us -> 173 us (0.80)
  local copies, waits for them, and re-layouts: 40.4 us -> 11 us
  other arithmetic: 32.9 us -> 15.2 us
  matrix products: 10.4 us -> 15 us
    unnamed x15 -> x9, local copies, waits for them, and re-layouts: 23 us -> 0.65 us
    convert_element_type x2 -> x0, other arithmetic: 7.42 us -> none  [the longest x1 6.48 us: local(): received.astype(jnp.float32)[:, None]]
    reduce_sum x1 -> x0, other arithmetic: 7.13 us -> none  [local(): jnp.sum(received_weight.astype(jnp.float32)[:, :, None, None] * received....]
    dot_general x0 -> x1, matrix products: none -> 4.63 us  [local(): jnp.einsum('sc,sij->cij', received_weight, received, preferred_element_ty...]
    slice x1 -> x0, local copies, waits for them, and re-layouts: 3.47 us -> none  [smooth_columns(): total = total + taps[index] * padded[:, DET_R + tap:DET_R + tap + width]]
    another operation x2 -> x1, local copies, waits for them, and re-layouts: 3.35 us -> 0.09 us  [local(): jnp.stack([framed[k * height:k * height + height + 2 * DET_R] for k in ra...]
    add x1, other arithmetic: 4.07 us -> 1.21 us  [smooth_columns(): total = total + taps[index] * padded[:, DET_R + tap:DET_R + tap + width]]
  transfers between devices with their start and end apart: 5 -> 5, of which waited for: 3 -> 3; matrix products, arithmetic and copies ran while one was open for 12% -> 15% of each run, Pallas kernels for 0% -> 0%
where the time goes in v4:
time: 173 us; the launch traced here: 172 us
  waiting for transfers between devices  109 us (63%)
  starting transfers between devices  20.3 us (12%)
  other arithmetic  15.2 us (9%)
  matrix products  15 us (9%)
  local copies, waits for them, and re-layouts  11 us (6%)
    all_to_all x1, waiting for transfers between devices, local(): lax.all_to_all(packed.reshape(owners, capacity * side, side), ('sect', 's...  93 us
    all_to_all x1, waiting for transfers between devices, local(): lax.all_to_all(windows, 'band', split_axis=0, concat_axis=0, tiled=True)  13.5 us
    dot_general x1, matrix products, local(): jnp.einsum('bij,bkj->bik', section, col_kernel, preferred_element_type=jn...  9.48 us
    all_to_all x1, starting transfers between devices, local(): lax.all_to_all(packed_weight.reshape(owners, capacity, CELL_DEV), ('sect'...  6.38 us
    all_to_all x1, starting transfers between devices, local(): lax.all_to_all(packed.reshape(owners, capacity * side, side), ('sect', 's...  5.1 us
    dot_general x1, matrix products, local(): jnp.einsum('sc,sij->cij', received_weight, received, preferred_element_ty...  4.63 us
    all_to_all x1, starting transfers between devices, local(): lax.all_to_all(windows, 'band', split_axis=0, concat_axis=0, tiled=True)  4.49 us
    gather x1, local copies, waits for them, and re-layouts, local(): packed = jnp.take(warped, source, axis=0, mode='clip')  4.34 us
  transfers between devices with their start and end apart: 5, of which 3 were waited for; matrix products, arithmetic and copies ran while one was open for 15% of the time, Pallas kernels for 0%

profile of v4, /device:TPU:1, one launch (start us, length us, event | category | flops | bytes accessed | tf_op | source)
XLA Modules:
  0.0 172.0 jit_solution(8993266516749827027)
XLA Ops:
  0.6 1.0 convert_reduce_fusion.1
  2.8 0.9 convolution_convert_fusion
  4.5 6.4 %all-to-all-start = ((bf16[8,4,4]{1,2,0:T(4,128)(2,1)}), bf16[8,4,4]{1,2,0:T(4,128)(2,1)S(1)}, u32[]{:S(2)}, u32[]{:S(2)}) async-start(bf16[8,4,4]{1,2,0:T(4,128)(2,1)} %copy.13), calls=%async_computation | async-start | bytes 16384 | tf_op jit(solution)/shard_map/all_to_all | solution.py:120
  10.8 0.8 broadcast_add_fusion.31
  11.6 0.8 exponential_bitcast_fusion.17
  12.4 0.8 add_add_fusion.1
  13.9 1.0 divide_convert_fusion.1
  16.2 1.0 divide_convert_fusion.2
  20.5 1.2 select_reduce_fusion
  21.7 9.5 %fusion.136 = bf16[16,256,256]{2,1,0:T(8,128)(2,1)} fusion(pred[256,256]{1,0:T(8,128)(4,1)S(1)} %get-tuple-element.124, pred[256,256]{1,0:T(8,128)(4,1)S(1)} %get-tuple-element.125, pred[256,256]{1,0:T(8,128)(4,1)S(1)} %get-tuple-element.126, pred[256,256]{1,0:T(8,128)(4,1)S(1)} %get-tuple-element.127, pred[256,256]{1,0:T(8,128)(4,1)S(1)} %get-tuple-element.128, ...), kind=kOutput, calls=%fused_computation.82 | convolution fusion | flops 1128267776 | bytes 5834304 | tf_op jit(solution)/shard_map/bij,bkj->bik/dot_general | solution.py:91
  31.8 4.3 %gather_fusion = bf16[32,256,256]{2,1,0:T(8,128)(2,1)} fusion(bf16[16,256,256]{2,1,0:T(8,128)(2,1)} %fusion.136, s32[1024]{0:T(1024)S(1)} %pad_clamp_fusion), kind=kCustom, calls=%fused_computation | custom fusion | bytes 8388736 | tf_op jit(solution)/shard_map/jit(_take)/gather | solution.py:103
  36.2 5.1 %all-to-all-start.1 = ((bf16[8,1024,256]{2,1,0:T(8,128)(2,1)}), bf16[8,1024,256]{2,1,0:T(8,128)(2,1)}, u32[]{:S(2)}, u32[]{:S(2)}) async-start(bf16[8,1024,256]{2,1,0:T(8,128)(2,1)} %bitcast.274), calls=%async_computation.1 | async-start | bytes 8388608 | tf_op jit(solution)/shard_map/all_to_all | solution.py:113
  41.5 93.0 %all-to-all-done.1 = bf16[8,1024,256]{2,1,0:T(8,128)(2,1)} async-done(((bf16[8,1024,256]{2,1,0:T(8,128)(2,1)}), bf16[8,1024,256]{2,1,0:T(8,128)(2,1)}, u32[]{:S(2)}, u32[]{:S(2)}) %all-to-all-start.1) | async-done | bytes 4194336 | tf_op jit(solution)/shard_map/all_to_all | solution.py:113
  134.5 4.6 %divide_convert_fusion = bf16[4,256,256]{2,0,1:T(4,128)(2,1)S(1)} fusion(bf16[32,4,1]{0,1,2:T(4,128)(2,1)S(1)} %reshape.755, bf16[32,256,256]{2,1,0:T(8,128)(2,1)} %bitcast.77, f32[4]{0:T(128)S(1)} %broadcast_maximum_fusion), kind=kOutput, calls=%fused_computation.139 | convolution fusion | flops 17301504 | bytes 4718864 | tf_op jit(solution)/shard_map/sc,sij->cij/dot_general | solution.py:130
  139.3 1.9 %collective-permute-start = (bf16[256,4]{1,0:T(8,128)(2,1)S(1)}, bf16[256,4]{1,0:T(8,128)(2,1)S(1)}, u32[]{:S(2)}, u32[]{:S(2)}) collective-permute-start(bf16[256,4]{1,0:T(8,128)(2,1)S(1)} %get-tuple-element.6), channel_id=1, source_target_pairs={{0,1},{1,4},{4,5},{5,8},{8,9},{9,12},{12,13},{2,3},{3,6},{6,7},{7,... | collective-permute-start | bytes 6152 | tf_op jit(solution)/shard_map/ppermute | solution.py:23
  141.3 2.4 %collective-permute-start.1 = (bf16[256,4]{1,0:T(8,128)(2,1)S(1)}, bf16[256,4]{1,0:T(8,128)(2,1)S(1)}, u32[]{:S(2)}, u32[]{:S(2)}) collective-permute-start(bf16[256,4]{1,0:T(8,128)(2,1)S(1)} %get-tuple-element.5), channel_id=1, source_target_pairs={{1,0},{4,1},{5,4},{8,5},{9,8},{12,9},{13,12},{3,2},{6,3},{7,6},{10... | collective-permute-start | bytes 6152 | tf_op jit(solution)/shard_map/ppermute | solution.py:24
  144.3 2.5 %collective-permute-done.1 = bf16[256,4]{1,0:T(8,128)(2,1)S(1)} collective-permute-done((bf16[256,4]{1,0:T(8,128)(2,1)S(1)}, bf16[256,4]{1,0:T(8,128)(2,1)S(1)}, u32[]{:S(2)}, u32[]{:S(2)}) %collective-permute-start.1) | collective-permute-done | bytes 2080 | tf_op jit(solution)/shard_map/ppermute | solution.py:24
  147.7 1.2 pad_maximum_fusion
  148.9 4.5 %all-to-all-start.2 = ((f32[2,136,1032]{2,1,0:T(8,128)}), f32[2,136,1032]{2,1,0:T(8,128)}, u32[]{:S(2)}, u32[]{:S(2)}) async-start(f32[2,136,1032]{2,1,0:T(8,128)} %pad_maximum_fusion), calls=%async_computation.2 | async-start | bytes 2506752 | tf_op jit(solution)/shard_map/all_to_all | solution.py:145
  153.4 1.2 broadcast_in_dim_reshape.3
  154.6 13.5 %all-to-all-done.2 = f32[2,136,1032]{2,1,0:T(8,128)} async-done(((f32[2,136,1032]{2,1,0:T(8,128)}), f32[2,136,1032]{2,1,0:T(8,128)}, u32[]{:S(2)}, u32[]{:S(2)}) %all-to-all-start.2) | async-done | bytes 1122848 | tf_op jit(solution)/shard_map/all_to_all | solution.py:145
  168.1 1.5 reduce_sum.42
  169.5 1.2 fusion.226
  170.7 1.3 fusion.234
  (42 shorter events, 8.9 us)
Async XLA Ops:
  0.6 21.1 %copy-start = (bf16[1,16,256,256]{3,2,1,0:T(8,128)(2,1)S(1)}, bf16[1,16,256,256]{3,2,1,0:T(8,128)(2,1)}, u32[]{:S(2)}) copy-start(bf16[1,16,256,256]{3,2,1,0:T(8,128)(2,1)} %param.8) | copy-start | bytes 6291460
  2.3 0.5 copy-start.3
  4.5 31.7 %all-to-all-start = ((bf16[8,4,4]{1,2,0:T(4,128)(2,1)}), bf16[8,4,4]{1,2,0:T(4,128)(2,1)S(1)}, u32[]{:S(2)}, u32[]{:S(2)}) async-start(bf16[8,4,4]{1,2,0:T(4,128)(2,1)} %copy.13), calls=%async_computation | async-start | bytes 16384 | tf_op jit(solution)/shard_map/all_to_all | solution.py:120
  36.2 98.3 %all-to-all-start.1 = ((bf16[8,1024,256]{2,1,0:T(8,128)(2,1)}), bf16[8,1024,256]{2,1,0:T(8,128)(2,1)}, u32[]{:S(2)}, u32[]{:S(2)}) async-start(bf16[8,1024,256]{2,1,0:T(8,128)(2,1)} %bitcast.274), calls=%async_computation.1 | async-start | bytes 8388608 | tf_op jit(solution)/shard_map/all_to_all | solution.py:113
  139.1 5.2 %copy-start.1 = (bf16[4,256,256]{2,0,1:T(4,128)(2,1)}, bf16[4,256,256]{2,0,1:T(4,128)(2,1)S(1)}, u32[]{:S(2)}) copy-start(bf16[4,256,256]{2,0,1:T(4,128)(2,1)S(1)} %divide_convert_fusion) | copy-start | bytes 1572868
  139.3 5.0 %collective-permute-start = (bf16[256,4]{1,0:T(8,128)(2,1)S(1)}, bf16[256,4]{1,0:T(8,128)(2,1)S(1)}, u32[]{:S(2)}, u32[]{:S(2)}) collective-permute-start(bf16[256,4]{1,0:T(8,128)(2,1)S(1)} %get-tuple-element.6), channel_id=1, source_target_pairs={{0,1},{1,4},{4,5},{5,8},{8,9},{9,12},{12,13},{2,3},{3,6},{6,7},{7,... | collective-permute-start | bytes 6152 | tf_op jit(solution)/shard_map/ppermute | solution.py:23
  141.3 5.6 %collective-permute-start.1 = (bf16[256,4]{1,0:T(8,128)(2,1)S(1)}, bf16[256,4]{1,0:T(8,128)(2,1)S(1)}, u32[]{:S(2)}, u32[]{:S(2)}) collective-permute-start(bf16[256,4]{1,0:T(8,128)(2,1)S(1)} %get-tuple-element.5), channel_id=1, source_target_pairs={{1,0},{4,1},{5,4},{8,5},{9,8},{12,9},{13,12},{3,2},{6,3},{7,6},{10... | collective-permute-start | bytes 6152 | tf_op jit(solution)/shard_map/ppermute | solution.py:24
  147.7 5.7 %copy-start.2 = (bf16[4,256,256]{2,0,1:T(4,128)(2,1)S(1)}, bf16[4,256,256]{2,0,1:T(4,128)(2,1)}, u32[]{:S(2)}) copy-start(bf16[4,256,256]{2,0,1:T(4,128)(2,1)} %copy-done.1) | copy-start | bytes 1572868
  148.9 19.2 %all-to-all-start.2 = ((f32[2,136,1032]{2,1,0:T(8,128)}), f32[2,136,1032]{2,1,0:T(8,128)}, u32[]{:S(2)}, u32[]{:S(2)}) async-start(f32[2,136,1032]{2,1,0:T(8,128)} %pad_maximum_fusion), calls=%async_computation.2 | async-start | bytes 2506752 | tf_op jit(solution)/shard_map/all_to_all | solution.py:145

commit v5 on v4

--- a/solution.py
+++ b/solution.py
@@ -33,21 +33,26 @@
 def block_kernels(shift, spread, side):
     band = PSF_R + 4
     spacing = jnp.arange(-band, band + 1, dtype=jnp.float32)
-    weight_total = jnp.zeros_like(spread)
-    summed = jnp.zeros((shift.shape[0], 2 * band + 1), jnp.float32)
-    for tap_shift in range(-PSF_R, PSF_R + 1):
-        tap_weight = jnp.exp(-spread * float(tap_shift * tap_shift))
-        weight_total = weight_total + tap_weight
-        summed = summed + tap_weight[:, None] * lanczos_tap(
-            spacing[None] + (shift[:, None] + float(tap_shift))
-        )
-    values = (summed / weight_total[:, None]).astype(jnp.bfloat16)
+    tap = jnp.arange(-PSF_R, PSF_R + 1, dtype=jnp.float32)
+    tap_weight = jnp.exp(-spread[..., None] * (tap * tap))
+    weight_total = jnp.sum(tap_weight, axis=-1)
+    taps = lanczos_tap(spacing + (shift[..., None, None] + tap[:, None]))
+    summed = jnp.sum(tap_weight[..., None] * taps, axis=-2)
+    values = (summed / weight_total[..., None]).astype(jnp.bfloat16)
     position = jnp.arange(side, dtype=jnp.int32)
     lag = position[:, None] - position[None, :]
-    matrix = jnp.zeros((shift.shape[0], side, side), jnp.bfloat16)
+    matrix = jnp.zeros(shift.shape + (side, side), jnp.bfloat16)
     for index in range(2 * band + 1):
-        matrix = jnp.where((lag == index - band)[None], values[:, index, None, None], matrix)
+        matrix = jnp.where(lag == index - band, values[..., index, None, None], matrix)
     return matrix
+
+
+def gain_pieces(gain):
+    high = lax.reduce_precision(gain, exponent_bits=8, mantissa_bits=7)
+    rest = gain - high
+    middle = lax.reduce_precision(rest, exponent_bits=8, mantissa_bits=7)
+    low = lax.reduce_precision(rest - middle, exponent_bits=8, mantissa_bits=7)
+    return jnp.stack([high, middle, low]).astype(jnp.bfloat16)
 
 
 def filter_taps():
@@ -83,8 +88,9 @@
     owners = sect_count * sub_count
     capacity = max(2, -(-2 * count // owners))
     slot_count = owners * capacity
-    row_kernel = block_kernels(offsets[0, :, 0], widths[0, :, 0], side)
-    col_kernel = block_kernels(offsets[0, :, 1], widths[0, :, 1], side)
+    kernels = block_kernels(offsets[0], widths[0], side)
+    row_kernel = kernels[:, 0]
+    col_kernel = kernels[:, 1]
     section = jnp.einsum(
         "bij,bjk->bik", row_kernel, images[0], preferred_element_type=jnp.float32
     ).astype(jnp.bfloat16)
@@ -138,12 +144,20 @@
     padded = extended(coadd, ((("sect", "sub"), 1),), DET_R)
     band_count = lax.axis_size("band")
     height = side // band_count
-    framed = jnp.pad(band_gain[0] * padded.astype(jnp.float32), ((DET_R, DET_R), (0, 0)))
+    framed = jnp.pad(padded, ((DET_R, DET_R), (0, 0)))
+    gain_row = jnp.zeros((1, padded.shape[1]), jnp.bfloat16).at[0, :3].set(gain_pieces(band_gain[0]))
     windows = jnp.stack(
-        [framed[k * height : k * height + height + 2 * DET_R] for k in range(band_count)]
+        [
+            jnp.concatenate([framed[k * height : k * height + height + 2 * DET_R], gain_row])
+            for k in range(band_count)
+        ]
     )
     gathered = lax.all_to_all(windows, "band", split_axis=0, concat_axis=0, tiled=True)
-    combined = jnp.sum(gathered, axis=0)
+    span = height + 2 * DET_R
+    gains = jnp.sum(gathered[:, span, :3].astype(jnp.float32), axis=1)
+    combined = jnp.zeros((span, padded.shape[1]), jnp.float32)
+    for k in range(band_count):
+        combined = combined + gains[k] * gathered[k, :span].astype(jnp.float32)
     detection = smooth_rows_valid(smooth_columns(combined, CELL_DEV * side), height)
     return (coadd[None], detection)
 

time: 173 us -> 169 us (0.977)
  other arithmetic: 15.2 us -> 28 us
  waiting for transfers between devices: 109 us -> 96.6 us
  matrix products: 15 us -> 10.4 us
  between operations: 1.5 us -> 5.61 us
  local copies, waits for them, and re-layouts: 11 us -> 8.46 us
    select_n x0 -> x1, other arithmetic: none -> 16 us  [block_kernels(): jnp.where(lag == index - band, values[..., index, None, None], matrix)]
    all_to_all x1, waiting for transfers between devices: 13.5 us -> 7.07 us  [local(): lax.all_to_all(windows, 'band', split_axis=0, concat_axis=0, tiled=True)]
    all_to_all x1, waiting for transfers between devices: 93 us -> 87.6 us  [local(): lax.all_to_all(packed.reshape(owners, capacity * side, side), ('sect', 's...]
    dot_general x1, matrix products: 9.48 us -> 4.84 us  [local(): jnp.einsum('bij,bkj->bik', section, col_kernel, preferred_element_type=jn...]
    broadcast_in_dim x4 -> x0, local copies, waits for them, and re-layouts: 2.51 us -> none  [block_kernels(): jnp.where((lag == index - band)[None], values[:, index, None, None], matrix)]
    convert_element_type x2 -> x1, other arithmetic: 2.06 us -> 0.08 us  [block_kernels(): values = (summed / weight_total[..., None]).astype(jnp.bfloat16)]
  transfers between devices with their start and end apart: 5 -> 5, of which waited for: 3 -> 3; matrix products, arithmetic and copies ran while one was open for 15% -> 19% of each run, Pallas kernels for 0% -> 0%
where the time goes in v5:
time: 169 us; the launch traced here: 168 us
  waiting for transfers between devices  96.6 us (57%)
  other arithmetic  28 us (17%)
  starting transfers between devices  19.3 us (11%)
  matrix products  10.4 us (6%)
  local copies, waits for them, and re-layouts  8.46 us (5%)
  between operations  5.61 us (3%)
    all_to_all x1, waiting for transfers between devices, local(): lax.all_to_all(packed.reshape(owners, capacity * side, side), ('sect', 's...  87.6 us
    select_n x1, other arithmetic, block_kernels(): jnp.where(lag == index - band, values[..., index, None, None], matrix)  16 us
    all_to_all x1, waiting for transfers between devices, local(): lax.all_to_all(windows, 'band', split_axis=0, concat_axis=0, tiled=True)  7.07 us
    all_to_all x1, starting transfers between devices, local(): lax.all_to_all(packed_weight.reshape(owners, capacity, CELL_DEV), ('sect'...  6.38 us
    all_to_all x1, starting transfers between devices, local(): lax.all_to_all(packed.reshape(owners, capacity * side, side), ('sect', 's...  5.1 us
    dot_general x1, matrix products, local(): jnp.einsum('bij,bkj->bik', section, col_kernel, preferred_element_type=jn...  4.84 us
    dot_general x1, matrix products, local(): jnp.einsum('sc,sij->cij', received_weight, received, preferred_element_ty...  4.63 us
    gather x1, local copies, waits for them, and re-layouts, local(): packed = jnp.take(warped, source, axis=0, mode='clip')  4.33 us
  transfers between devices with their start and end apart: 5, of which 3 were waited for; matrix products, arithmetic and copies ran while one was open for 19% of the time, Pallas kernels for 0%

profile of v5, /device:TPU:1, one launch (start us, length us, event | category | flops | bytes accessed | tf_op | source)
XLA Modules:
  0.0 168.4 jit_solution(10428878472129889381)
XLA Ops:
  0.6 1.0 convert_reduce_fusion.1
  2.3 0.9 convolution_convert_fusion
  3.9 6.4 %all-to-all-start = ((bf16[8,4,4]{1,2,0:T(4,128)(2,1)}), bf16[8,4,4]{1,2,0:T(4,128)(2,1)S(1)}, u32[]{:S(2)}, u32[]{:S(2)}) async-start(bf16[8,4,4]{1,2,0:T(4,128)(2,1)} %copy.23), calls=%async_computation | async-start | bytes 16384 | tf_op jit(solution)/shard_map/all_to_all | solution.py:126
  10.3 0.7 negate_bitcast_fusion
  11.3 0.8 broadcast_add_fusion
  12.0 0.8 multiply_reduce_fusion
  14.2 16.0 %select_select_fusion = bf16[16,2,256,256]{3,2,0,1:T(8,128)(2,1)} fusion(pred[256,256]{1,0:T(8,128)(4,1)S(1)} %get-tuple-element.50, pred[256,256]{1,0:T(8,128)(4,1)S(1)} %get-tuple-element.51, pred[256,256]{1,0:T(8,128)(4,1)S(1)} %get-tuple-element.52, pred[256,256]{1,0:T(8,128)(4,1)S(1)} %get-tuple-element.53, pred[256,256]{1,0:T(8,128)(4,1)S(1)} %get-tuple-element.54, ...), kind=kLoop, calls=%fused_computation.3 | loop fusion | flops 52428800 | bytes 5834304 | tf_op jit(solution)/shard_map/jit(_where)/select_n | solution.py:46
  30.2 4.8 %fusion.10 = bf16[16,256,256]{2,1,0:T(8,128)(2,1)} fusion(bf16[16,2,256,256]{3,2,0,1:T(8,128)(2,1)} %select_select_fusion, bf16[1,16,256,256]{3,2,1,0:T(8,128)(2,1)S(1)} %copy-done), kind=kOutput, calls=%fused_computation.10 | convolution fusion | flops 1075838976 | bytes 8388608 | tf_op jit(solution)/shard_map/bij,bkj->bik/dot_general | solution.py:97
  35.1 4.3 %gather_fusion = bf16[32,256,256]{2,1,0:T(8,128)(2,1)} fusion(bf16[16,256,256]{2,1,0:T(8,128)(2,1)} %fusion.10, s32[1024]{0:T(1024)S(1)} %pad_clamp_fusion), kind=kCustom, calls=%fused_computation | custom fusion | bytes 8388736 | tf_op jit(solution)/shard_map/jit(_take)/gather | solution.py:109
  39.4 5.1 %all-to-all-start.1 = ((bf16[8,1024,256]{2,1,0:T(8,128)(2,1)}), bf16[8,1024,256]{2,1,0:T(8,128)(2,1)}, u32[]{:S(2)}, u32[]{:S(2)}) async-start(bf16[8,1024,256]{2,1,0:T(8,128)(2,1)} %bitcast.59), calls=%async_computation.1 | async-start | bytes 8388608 | tf_op jit(solution)/shard_map/all_to_all | solution.py:119
  50.1 87.6 %all-to-all-done.1 = bf16[8,1024,256]{2,1,0:T(8,128)(2,1)} async-done(((bf16[8,1024,256]{2,1,0:T(8,128)(2,1)}), bf16[8,1024,256]{2,1,0:T(8,128)(2,1)}, u32[]{:S(2)}, u32[]{:S(2)}) %all-to-all-start.1) | async-done | bytes 4194336 | tf_op jit(solution)/shard_map/all_to_all | solution.py:119
  137.8 4.6 %divide_convert_fusion = bf16[4,256,256]{2,0,1:T(4,128)(2,1)S(1)} fusion(bf16[32,4,1]{0,1,2:T(4,128)(2,1)S(1)} %reshape.169, bf16[32,256,256]{2,1,0:T(8,128)(2,1)} %bitcast.11, f32[4]{0:T(128)S(1)} %broadcast_maximum_fusion), kind=kOutput, calls=%fused_computation.12 | convolution fusion | flops 17301504 | bytes 4718864 | tf_op jit(solution)/shard_map/sc,sij->cij/dot_general | solution.py:136
  142.6 1.9 %collective-permute-start = (bf16[256,4]{1,0:T(8,128)(2,1)S(1)}, bf16[256,4]{1,0:T(8,128)(2,1)S(1)}, u32[]{:S(2)}, u32[]{:S(2)}) collective-permute-start(bf16[256,4]{1,0:T(8,128)(2,1)S(1)} %get-tuple-element.43), channel_id=1, source_target_pairs={{0,1},{1,4},{4,5},{5,8},{8,9},{9,12},{12,13},{2,3},{3,6},{6,7},{7,... | collective-permute-start | bytes 6152 | tf_op jit(solution)/shard_map/ppermute | solution.py:23
  144.5 2.4 %collective-permute-start.1 = (bf16[256,4]{1,0:T(8,128)(2,1)S(1)}, bf16[256,4]{1,0:T(8,128)(2,1)S(1)}, u32[]{:S(2)}, u32[]{:S(2)}) collective-permute-start(bf16[256,4]{1,0:T(8,128)(2,1)S(1)} %get-tuple-element.42), channel_id=1, source_target_pairs={{1,0},{4,1},{5,4},{8,5},{9,8},{12,9},{13,12},{3,2},{6,3},{7,6},{10... | collective-permute-start | bytes 6152 | tf_op jit(solution)/shard_map/ppermute | solution.py:24
  146.9 1.3 broadcast_select_fusion
  148.2 1.9 %collective-permute-done.1 = bf16[256,4]{1,0:T(8,128)(2,1)S(1)} collective-permute-done((bf16[256,4]{1,0:T(8,128)(2,1)S(1)}, bf16[256,4]{1,0:T(8,128)(2,1)S(1)}, u32[]{:S(2)}, u32[]{:S(2)}) %collective-permute-start.1) | collective-permute-done | bytes 2080 | tf_op jit(solution)/shard_map/ppermute | solution.py:24
  151.0 0.9 pad_maximum_fusion
  151.9 3.5 %all-to-all-start.2 = ((bf16[2,137,1032]{2,1,0:T(8,128)(2,1)}), bf16[2,137,1032]{2,1,0:T(8,128)(2,1)S(1)}, u32[]{:S(2)}, u32[]{:S(2)}) async-start(bf16[2,137,1032]{2,1,0:T(8,128)(2,1)} %pad_maximum_fusion), calls=%async_computation.2 | async-start | bytes 1327104 | tf_op jit(solution)/shard_map/all_to_all | solution.py:155
  155.4 1.2 broadcast_in_dim_reshape.3
  156.6 7.1 %all-to-all-done.2 = bf16[2,137,1032]{2,1,0:T(8,128)(2,1)S(1)} async-done(((bf16[2,137,1032]{2,1,0:T(8,128)(2,1)}), bf16[2,137,1032]{2,1,0:T(8,128)(2,1)S(1)}, u32[]{:S(2)}, u32[]{:S(2)}) %all-to-all-start.2) | async-done | bytes 565568 | tf_op jit(solution)/shard_map/all_to_all | solution.py:155
  163.7 0.7 fusion.121
  164.4 1.4 add_bitcast_fusion
  165.9 1.2 fusion.26
  167.1 1.3 fusion.37
  (45 shorter events, 4.9 us)
Async XLA Ops:
  0.6 29.6 %copy-start = (bf16[1,16,256,256]{3,2,1,0:T(8,128)(2,1)S(1)}, bf16[1,16,256,256]{3,2,1,0:T(8,128)(2,1)}, u32[]{:S(2)}) copy-start(bf16[1,16,256,256]{3,2,1,0:T(8,128)(2,1)} %param.10) | copy-start | bytes 6291460
  3.9 35.5 %all-to-all-start = ((bf16[8,4,4]{1,2,0:T(4,128)(2,1)}), bf16[8,4,4]{1,2,0:T(4,128)(2,1)S(1)}, u32[]{:S(2)}, u32[]{:S(2)}) async-start(bf16[8,4,4]{1,2,0:T(4,128)(2,1)} %copy.23), calls=%async_computation | async-start | bytes 16384 | tf_op jit(solution)/shard_map/all_to_all | solution.py:126
  39.4 98.3 %all-to-all-start.1 = ((bf16[8,1024,256]{2,1,0:T(8,128)(2,1)}), bf16[8,1024,256]{2,1,0:T(8,128)(2,1)}, u32[]{:S(2)}, u32[]{:S(2)}) async-start(bf16[8,1024,256]{2,1,0:T(8,128)(2,1)} %bitcast.59), calls=%async_computation.1 | async-start | bytes 8388608 | tf_op jit(solution)/shard_map/all_to_all | solution.py:119
  142.4 5.8 %copy-start.1 = (bf16[4,256,256]{2,0,1:T(4,128)(2,1)}, bf16[4,256,256]{2,0,1:T(4,128)(2,1)S(1)}, u32[]{:S(2)}) copy-start(bf16[4,256,256]{2,0,1:T(4,128)(2,1)S(1)} %divide_convert_fusion) | copy-start | bytes 1572868
  142.6 5.6 %collective-permute-start = (bf16[256,4]{1,0:T(8,128)(2,1)S(1)}, bf16[256,4]{1,0:T(8,128)(2,1)S(1)}, u32[]{:S(2)}, u32[]{:S(2)}) collective-permute-start(bf16[256,4]{1,0:T(8,128)(2,1)S(1)} %get-tuple-element.43), channel_id=1, source_target_pairs={{0,1},{1,4},{4,5},{5,8},{8,9},{9,12},{12,13},{2,3},{3,6},{6,7},{7,... | collective-permute-start | bytes 6152 | tf_op jit(solution)/shard_map/ppermute | solution.py:23
  144.5 5.6 %collective-permute-start.1 = (bf16[256,4]{1,0:T(8,128)(2,1)S(1)}, bf16[256,4]{1,0:T(8,128)(2,1)S(1)}, u32[]{:S(2)}, u32[]{:S(2)}) collective-permute-start(bf16[256,4]{1,0:T(8,128)(2,1)S(1)} %get-tuple-element.42), channel_id=1, source_target_pairs={{1,0},{4,1},{5,4},{8,5},{9,8},{12,9},{13,12},{3,2},{6,3},{7,6},{10... | collective-permute-start | bytes 6152 | tf_op jit(solution)/shard_map/ppermute | solution.py:24
  150.9 4.5 %copy-start.2 = (bf16[4,256,256]{2,0,1:T(4,128)(2,1)S(1)}, bf16[4,256,256]{2,0,1:T(4,128)(2,1)}, u32[]{:S(2)}) copy-start(bf16[4,256,256]{2,0,1:T(4,128)(2,1)} %copy-done.1) | copy-start | bytes 1572868
  151.9 11.8 %all-to-all-start.2 = ((bf16[2,137,1032]{2,1,0:T(8,128)(2,1)}), bf16[2,137,1032]{2,1,0:T(8,128)(2,1)S(1)}, u32[]{:S(2)}, u32[]{:S(2)}) async-start(bf16[2,137,1032]{2,1,0:T(8,128)(2,1)} %pad_maximum_fusion), calls=%async_computation.2 | async-start | bytes 1327104 | tf_op jit(solution)/shard_map/all_to_all | solution.py:155

commit v6 on v5

--- a/solution.py
+++ b/solution.py
@@ -30,7 +30,7 @@
     return jnp.where(jnp.abs(spacing) < 3.0, jnp.sinc(spacing) * jnp.sinc(spacing / 3.0), 0.0)
 
 
-def block_kernels(shift, spread, side):
+def band_values(shift, spread):
     band = PSF_R + 4
     spacing = jnp.arange(-band, band + 1, dtype=jnp.float32)
     tap = jnp.arange(-PSF_R, PSF_R + 1, dtype=jnp.float32)
@@ -38,10 +38,14 @@
     weight_total = jnp.sum(tap_weight, axis=-1)
     taps = lanczos_tap(spacing + (shift[..., None, None] + tap[:, None]))
     summed = jnp.sum(tap_weight[..., None] * taps, axis=-2)
-    values = (summed / weight_total[..., None]).astype(jnp.bfloat16)
+    return (summed / weight_total[..., None]).astype(jnp.bfloat16)
+
+
+def toeplitz(values, side):
+    band = PSF_R + 4
     position = jnp.arange(side, dtype=jnp.int32)
     lag = position[:, None] - position[None, :]
-    matrix = jnp.zeros(shift.shape + (side, side), jnp.bfloat16)
+    matrix = jnp.zeros(values.shape[:-1] + (side, side), jnp.bfloat16)
     for index in range(2 * band + 1):
         matrix = jnp.where(lag == index - band, values[..., index, None, None], matrix)
     return matrix
@@ -88,9 +92,9 @@
     owners = sect_count * sub_count
     capacity = max(2, -(-2 * count // owners))
     slot_count = owners * capacity
-    kernels = block_kernels(offsets[0], widths[0], side)
-    row_kernel = kernels[:, 0]
-    col_kernel = kernels[:, 1]
+    values = band_values(offsets[0], widths[0])
+    row_kernel = toeplitz(values[:, 0], side)
+    col_kernel = toeplitz(values[:, 1], side)
     section = jnp.einsum(
         "bij,bjk->bik", row_kernel, images[0], preferred_element_type=jnp.float32
     ).astype(jnp.bfloat16)

time: 169 us -> 163 us (0.964)
  other arithmetic: 28 us -> 15.1 us
  matrix products: 10.4 us -> 15 us
  local copies, waits for them, and re-layouts: 8.46 us -> 11.2 us
    select_n x1 -> x0, other arithmetic: 16 us -> none  [block_kernels(): jnp.where(lag == index - band, values[..., index, None, None], matrix)]
    dot_general x1, matrix products: 4.84 us -> 9.46 us  [local(): jnp.einsum('bij,bkj->bik', section, col_kernel, preferred_element_type=jn...]
    slice x2 -> x3, local copies, waits for them, and re-layouts: 0.46 us -> 2.7 us  [toeplitz(): values[..., index, None, None]]
  transfers between devices with their start and end apart: 5 -> 5, of which waited for: 3 -> 3; matrix products, arithmetic and copies ran while one was open for 19% -> 16% of each run, Pallas kernels for 0% -> 0%
where the time goes in v6:
time: 163 us
  waiting for transfers between devices  96.6 us (59%)
  starting transfers between devices  19.3 us (12%)
  other arithmetic  15.1 us (9%)
  matrix products  15 us (9%)
  local copies, waits for them, and re-layouts  11.2 us (7%)
  between operations  5.58 us (3%)
    all_to_all x1, waiting for transfers between devices, local(): lax.all_to_all(packed.reshape(owners, capacity * side, side), ('sect', 's...  87.6 us
    dot_general x1, matrix products, local(): jnp.einsum('bij,bkj->bik', section, col_kernel, preferred_element_type=jn...  9.46 us
    all_to_all x1, waiting for transfers between devices, local(): lax.all_to_all(windows, 'band', split_axis=0, concat_axis=0, tiled=True)  7.07 us
    all_to_all x1, starting transfers between devices, local(): lax.all_to_all(packed_weight.reshape(owners, capacity, CELL_DEV), ('sect'...  6.38 us
    all_to_all x1, starting transfers between devices, local(): lax.all_to_all(packed.reshape(owners, capacity * side, side), ('sect', 's...  5.1 us
    dot_general x1, matrix products, local(): jnp.einsum('sc,sij->cij', received_weight, received, preferred_element_ty...  4.63 us
    gather x1, local copies, waits for them, and re-layouts, local(): packed = jnp.take(warped, source, axis=0, mode='clip')  4.33 us
    all_to_all x1, starting transfers between devices, local(): lax.all_to_all(windows, 'band', split_axis=0, concat_axis=0, tiled=True)  3.51 us
  transfers between devices with their start and end apart: 5, of which 3 were waited for; matrix products, arithmetic and copies ran while one was open for 16% of the time, Pallas kernels for 0%

profile of v6, /device:TPU:1, one launch (start us, length us, event | category | flops | bytes accessed | tf_op | source)
XLA Modules:
  0.0 162.8 jit_solution(2371167981775269380)
XLA Ops:
  0.6 1.0 convert_reduce_fusion.1
  2.8 0.9 convolution_convert_fusion
  4.5 6.4 %all-to-all-start = ((bf16[8,4,4]{1,2,0:T(4,128)(2,1)}), bf16[8,4,4]{1,2,0:T(4,128)(2,1)S(1)}, u32[]{:S(2)}, u32[]{:S(2)}) async-start(bf16[8,4,4]{1,2,0:T(4,128)(2,1)} %copy.23), calls=%async_computation | async-start | bytes 16384 | tf_op jit(solution)/shard_map/all_to_all | solution.py:130
  12.6 0.8 multiply_reduce_fusion
  13.4 0.9 slice_reduce_fusion.49
  14.3 0.9 slice_reduce_fusion.24
  15.3 0.9 slice_reduce_fusion.23
  18.1 1.3 select_reduce_fusion
  19.4 9.5 %fusion.136 = bf16[16,256,256]{2,1,0:T(8,128)(2,1)} fusion(pred[256,256]{1,0:T(8,128)(4,1)S(1)} %get-tuple-element.83, pred[256,256]{1,0:T(8,128)(4,1)S(1)} %get-tuple-element.84, pred[256,256]{1,0:T(8,128)(4,1)S(1)} %get-tuple-element.85, pred[256,256]{1,0:T(8,128)(4,1)S(1)} %get-tuple-element.86, pred[256,256]{1,0:T(8,128)(4,1)S(1)} %get-tuple-element.87, ...), kind=kOutput, calls=%fused_computation.82 | convolution fusion | flops 1128267776 | bytes 5834304 | tf_op jit(solution)/shard_map/bij,bkj->bik/dot_general | solution.py:101
  29.5 4.3 %gather_fusion = bf16[32,256,256]{2,1,0:T(8,128)(2,1)} fusion(bf16[16,256,256]{2,1,0:T(8,128)(2,1)} %fusion.136, s32[1024]{0:T(1024)S(1)} %pad_clamp_fusion), kind=kCustom, calls=%fused_computation | custom fusion | bytes 8388736 | tf_op jit(solution)/shard_map/jit(_take)/gather | solution.py:113
  33.8 5.1 %all-to-all-start.1 = ((bf16[8,1024,256]{2,1,0:T(8,128)(2,1)}), bf16[8,1024,256]{2,1,0:T(8,128)(2,1)}, u32[]{:S(2)}, u32[]{:S(2)}) async-start(bf16[8,1024,256]{2,1,0:T(8,128)(2,1)} %bitcast.49), calls=%async_computation.1 | async-start | bytes 8388608 | tf_op jit(solution)/shard_map/all_to_all | solution.py:123
  44.5 87.6 %all-to-all-done.1 = bf16[8,1024,256]{2,1,0:T(8,128)(2,1)} async-done(((bf16[8,1024,256]{2,1,0:T(8,128)(2,1)}), bf16[8,1024,256]{2,1,0:T(8,128)(2,1)}, u32[]{:S(2)}, u32[]{:S(2)}) %all-to-all-start.1) | async-done | bytes 4194336 | tf_op jit(solution)/shard_map/all_to_all | solution.py:123
  132.2 4.6 %divide_convert_fusion = bf16[4,256,256]{2,0,1:T(4,128)(2,1)S(1)} fusion(bf16[32,4,1]{0,1,2:T(4,128)(2,1)S(1)} %reshape.194, bf16[32,256,256]{2,1,0:T(8,128)(2,1)} %bitcast.11, f32[4]{0:T(128)S(1)} %broadcast_maximum_fusion), kind=kOutput, calls=%fused_computation.135 | convolution fusion | flops 17301504 | bytes 4718864 | tf_op jit(solution)/shard_map/sc,sij->cij/dot_general | solution.py:140
  137.0 1.9 %collective-permute-start = (bf16[256,4]{1,0:T(8,128)(2,1)S(1)}, bf16[256,4]{1,0:T(8,128)(2,1)S(1)}, u32[]{:S(2)}, u32[]{:S(2)}) collective-permute-start(bf16[256,4]{1,0:T(8,128)(2,1)S(1)} %get-tuple-element.68), channel_id=1, source_target_pairs={{0,1},{1,4},{4,5},{5,8},{8,9},{9,12},{12,13},{2,3},{3,6},{6,7},{7,... | collective-permute-start | bytes 6152 | tf_op jit(solution)/shard_map/ppermute | solution.py:23
  138.9 2.4 %collective-permute-start.1 = (bf16[256,4]{1,0:T(8,128)(2,1)S(1)}, bf16[256,4]{1,0:T(8,128)(2,1)S(1)}, u32[]{:S(2)}, u32[]{:S(2)}) collective-permute-start(bf16[256,4]{1,0:T(8,128)(2,1)S(1)} %get-tuple-element.67), channel_id=1, source_target_pairs={{1,0},{4,1},{5,4},{8,5},{9,8},{12,9},{13,12},{3,2},{6,3},{7,6},{10... | collective-permute-start | bytes 6152 | tf_op jit(solution)/shard_map/ppermute | solution.py:24
  141.3 1.3 broadcast_select_fusion
  142.6 1.9 %collective-permute-done.1 = bf16[256,4]{1,0:T(8,128)(2,1)S(1)} collective-permute-done((bf16[256,4]{1,0:T(8,128)(2,1)S(1)}, bf16[256,4]{1,0:T(8,128)(2,1)S(1)}, u32[]{:S(2)}, u32[]{:S(2)}) %collective-permute-start.1) | collective-permute-done | bytes 2080 | tf_op jit(solution)/shard_map/ppermute | solution.py:24
  145.4 0.9 pad_maximum_fusion
  146.3 3.5 %all-to-all-start.2 = ((bf16[2,137,1032]{2,1,0:T(8,128)(2,1)}), bf16[2,137,1032]{2,1,0:T(8,128)(2,1)S(1)}, u32[]{:S(2)}, u32[]{:S(2)}) async-start(bf16[2,137,1032]{2,1,0:T(8,128)(2,1)} %pad_maximum_fusion), calls=%async_computation.2 | async-start | bytes 1327104 | tf_op jit(solution)/shard_map/all_to_all | solution.py:159
  149.8 1.2 broadcast_in_dim_reshape.3
  151.0 7.1 %all-to-all-done.2 = bf16[2,137,1032]{2,1,0:T(8,128)(2,1)S(1)} async-done(((bf16[2,137,1032]{2,1,0:T(8,128)(2,1)}), bf16[2,137,1032]{2,1,0:T(8,128)(2,1)S(1)}, u32[]{:S(2)}, u32[]{:S(2)}) %all-to-all-start.2) | async-done | bytes 565568 | tf_op jit(solution)/shard_map/all_to_all | solution.py:159
  158.8 1.4 add_bitcast_fusion
  160.3 1.2 fusion.233
  161.5 1.3 fusion.244
  (48 shorter events, 8.9 us)
Async XLA Ops:
  0.6 18.7 %copy-start = (bf16[1,16,256,256]{3,2,1,0:T(8,128)(2,1)S(1)}, bf16[1,16,256,256]{3,2,1,0:T(8,128)(2,1)}, u32[]{:S(2)}) copy-start(bf16[1,16,256,256]{3,2,1,0:T(8,128)(2,1)} %param.10) | copy-start | bytes 6291460
  2.3 0.5 copy-start.3
  4.5 29.4 %all-to-all-start = ((bf16[8,4,4]{1,2,0:T(4,128)(2,1)}), bf16[8,4,4]{1,2,0:T(4,128)(2,1)S(1)}, u32[]{:S(2)}, u32[]{:S(2)}) async-start(bf16[8,4,4]{1,2,0:T(4,128)(2,1)} %copy.23), calls=%async_computation | async-start | bytes 16384 | tf_op jit(solution)/shard_map/all_to_all | solution.py:130
  33.8 98.3 %all-to-all-start.1 = ((bf16[8,1024,256]{2,1,0:T(8,128)(2,1)}), bf16[8,1024,256]{2,1,0:T(8,128)(2,1)}, u32[]{:S(2)}, u32[]{:S(2)}) async-start(bf16[8,1024,256]{2,1,0:T(8,128)(2,1)} %bitcast.49), calls=%async_computation.1 | async-start | bytes 8388608 | tf_op jit(solution)/shard_map/all_to_all | solution.py:123
  136.8 5.8 %copy-start.1 = (bf16[4,256,256]{2,0,1:T(4,128)(2,1)}, bf16[4,256,256]{2,0,1:T(4,128)(2,1)S(1)}, u32[]{:S(2)}) copy-start(bf16[4,256,256]{2,0,1:T(4,128)(2,1)S(1)} %divide_convert_fusion) | copy-start | bytes 1572868
  137.0 5.6 %collective-permute-start = (bf16[256,4]{1,0:T(8,128)(2,1)S(1)}, bf16[256,4]{1,0:T(8,128)(2,1)S(1)}, u32[]{:S(2)}, u32[]{:S(2)}) collective-permute-start(bf16[256,4]{1,0:T(8,128)(2,1)S(1)} %get-tuple-element.68), channel_id=1, source_target_pairs={{0,1},{1,4},{4,5},{5,8},{8,9},{9,12},{12,13},{2,3},{3,6},{6,7},{7,... | collective-permute-start | bytes 6152 | tf_op jit(solution)/shard_map/ppermute | solution.py:23
  138.9 5.6 %collective-permute-start.1 = (bf16[256,4]{1,0:T(8,128)(2,1)S(1)}, bf16[256,4]{1,0:T(8,128)(2,1)S(1)}, u32[]{:S(2)}, u32[]{:S(2)}) collective-permute-start(bf16[256,4]{1,0:T(8,128)(2,1)S(1)} %get-tuple-element.67), channel_id=1, source_target_pairs={{1,0},{4,1},{5,4},{8,5},{9,8},{12,9},{13,12},{3,2},{6,3},{7,6},{10... | collective-permute-start | bytes 6152 | tf_op jit(solution)/shard_map/ppermute | solution.py:24
  145.3 4.5 %copy-start.2 = (bf16[4,256,256]{2,0,1:T(4,128)(2,1)S(1)}, bf16[4,256,256]{2,0,1:T(4,128)(2,1)}, u32[]{:S(2)}) copy-start(bf16[4,256,256]{2,0,1:T(4,128)(2,1)} %copy-done.1) | copy-start | bytes 1572868
  146.3 11.8 %all-to-all-start.2 = ((bf16[2,137,1032]{2,1,0:T(8,128)(2,1)}), bf16[2,137,1032]{2,1,0:T(8,128)(2,1)S(1)}, u32[]{:S(2)}, u32[]{:S(2)}) async-start(bf16[2,137,1032]{2,1,0:T(8,128)(2,1)} %pad_maximum_fusion), calls=%async_computation.2 | async-start | bytes 1327104 | tf_op jit(solution)/shard_map/all_to_all | solution.py:159

commit v7 on v6

--- a/solution.py
+++ b/solution.py
@@ -150,18 +150,19 @@
     height = side // band_count
     framed = jnp.pad(padded, ((DET_R, DET_R), (0, 0)))
     gain_row = jnp.zeros((1, padded.shape[1]), jnp.bfloat16).at[0, :3].set(gain_pieces(band_gain[0]))
-    windows = jnp.stack(
-        [
-            jnp.concatenate([framed[k * height : k * height + height + 2 * DET_R], gain_row])
-            for k in range(band_count)
-        ]
-    )
-    gathered = lax.all_to_all(windows, "band", split_axis=0, concat_axis=0, tiled=True)
     span = height + 2 * DET_R
-    gains = jnp.sum(gathered[:, span, :3].astype(jnp.float32), axis=1)
-    combined = jnp.zeros((span, padded.shape[1]), jnp.float32)
-    for k in range(band_count):
-        combined = combined + gains[k] * gathered[k, :span].astype(jnp.float32)
+    me = lax.axis_index("band")
+    own = lax.dynamic_slice_in_dim(framed, me * height, span, axis=0)
+    combined = band_gain[0] * own.astype(jnp.float32)
+    for shift in range(1, band_count):
+        outgoing = jnp.concatenate(
+            [lax.dynamic_slice_in_dim(framed, ((me + shift) % band_count) * height, span, axis=0), gain_row]
+        )
+        incoming = lax.ppermute(
+            outgoing, "band", [(i, (i + shift) % band_count) for i in range(band_count)]
+        )
+        gain = jnp.sum(incoming[span, :3].astype(jnp.float32))
+        combined = combined + gain * incoming[:span].astype(jnp.float32)
     detection = smooth_rows_valid(smooth_columns(combined, CELL_DEV * side), height)
     return (coadd[None], detection)
 

time: 163 us -> 159 us (0.975)
  waiting for transfers between devices: 96.6 us -> 94.1 us
  starting transfers between devices: 19.3 us -> 17.1 us
    all_to_all x1 -> x0, waiting for transfers between devices: 7.07 us -> none  [local(): lax.all_to_all(windows, 'band', split_axis=0, concat_axis=0, tiled=True)]
    ppermute x0 -> x1, waiting for transfers between devices: none -> 4.64 us  [local(): lax.ppermute(outgoing, 'band', [(i, (i + shift) % band_count) for i in ra...]
    all_to_all x1 -> x0, starting transfers between devices: 3.51 us -> none  [local(): lax.all_to_all(windows, 'band', split_axis=0, concat_axis=0, tiled=True)]
  transfers between devices with their start and end apart: 5 -> 5, of which waited for: 3 -> 3; matrix products, arithmetic and copies ran while one was open for 16% -> 17% of each run, Pallas kernels for 0% -> 0%
where the time goes in v7:
time: 159 us
  waiting for transfers between devices  94.1 us (59%)
  starting transfers between devices  17.1 us (11%)
  matrix products  14.9 us (9%)
  other arithmetic  14.6 us (9%)
  local copies, waits for them, and re-layouts  12.2 us (8%)
  between operations  5.6 us (4%)
    all_to_all x1, waiting for transfers between devices, local(): lax.all_to_all(packed.reshape(owners, capacity * side, side), ('sect', 's...  87.6 us
    dot_general x1, matrix products, local(): jnp.einsum('bij,bkj->bik', section, col_kernel, preferred_element_type=jn...  9.34 us
    all_to_all x1, starting transfers between devices, local(): lax.all_to_all(packed_weight.reshape(owners, capacity, CELL_DEV), ('sect'...  6.38 us
    all_to_all x1, starting transfers between devices, local(): lax.all_to_all(packed.reshape(owners, capacity * side, side), ('sect', 's...  5.1 us
    ppermute x1, waiting for transfers between devices, local(): lax.ppermute(outgoing, 'band', [(i, (i + shift) % band_count) for i in ra...  4.64 us
    dot_general x1, matrix products, local(): jnp.einsum('sc,sij->cij', received_weight, received, preferred_element_ty...  4.63 us
    gather x1, local copies, waits for them, and re-layouts, local(): packed = jnp.take(warped, source, axis=0, mode='clip')  4.33 us
  transfers between devices with their start and end apart: 5, of which 3 were waited for; matrix products, arithmetic and copies ran while one was open for 17% of the time, Pallas kernels for 0%

profile of v7, /device:TPU:1, one launch (start us, length us, event | category | flops | bytes accessed | tf_op | source)
XLA Modules:
  0.0 158.5 jit_solution(13224755929601837270)
XLA Ops:
  0.6 1.0 convert_reduce_fusion.1
  2.8 0.9 convolution_convert_fusion
  4.4 6.4 %all-to-all-start = ((bf16[8,4,4]{1,2,0:T(4,128)(2,1)}), bf16[8,4,4]{1,2,0:T(4,128)(2,1)S(1)}, u32[]{:S(2)}, u32[]{:S(2)}) async-start(bf16[8,4,4]{1,2,0:T(4,128)(2,1)} %copy.23), calls=%async_computation | async-start | bytes 16384 | tf_op jit(solution)/shard_map/all_to_all | solution.py:130
  12.6 0.8 multiply_reduce_fusion
  13.4 0.8 slice_reduce_fusion.49
  14.3 0.9 slice_reduce_fusion.24
  15.2 0.9 slice_reduce_fusion.23
  18.6 1.3 select_reduce_fusion
  19.9 9.3 %fusion.136 = bf16[16,256,256]{2,1,0:T(8,128)(2,1)} fusion(pred[256,256]{1,0:T(8,128)(4,1)S(1)} %get-tuple-element.77, pred[256,256]{1,0:T(8,128)(4,1)S(1)} %get-tuple-element.78, pred[256,256]{1,0:T(8,128)(4,1)S(1)} %get-tuple-element.79, pred[256,256]{1,0:T(8,128)(4,1)S(1)} %get-tuple-element.80, pred[256,256]{1,0:T(8,128)(4,1)S(1)} %get-tuple-element.81, ...), kind=kOutput, calls=%fused_computation.82 | convolution fusion | flops 1128267776 | bytes 5834304 | tf_op jit(solution)/shard_map/bij,bkj->bik/dot_general | solution.py:101
  29.9 4.3 %gather_fusion = bf16[32,256,256]{2,1,0:T(8,128)(2,1)} fusion(bf16[16,256,256]{2,1,0:T(8,128)(2,1)} %fusion.136, s32[1024]{0:T(1024)S(1)} %pad_clamp_fusion), kind=kCustom, calls=%fused_computation | custom fusion | bytes 8388736 | tf_op jit(solution)/shard_map/jit(_take)/gather | solution.py:113
  34.2 5.1 %all-to-all-start.1 = ((bf16[8,1024,256]{2,1,0:T(8,128)(2,1)}), bf16[8,1024,256]{2,1,0:T(8,128)(2,1)}, u32[]{:S(2)}, u32[]{:S(2)}) async-start(bf16[8,1024,256]{2,1,0:T(8,128)(2,1)} %bitcast.42), calls=%async_computation.1 | async-start | bytes 8388608 | tf_op jit(solution)/shard_map/all_to_all | solution.py:123
  45.0 87.6 %all-to-all-done.1 = bf16[8,1024,256]{2,1,0:T(8,128)(2,1)} async-done(((bf16[8,1024,256]{2,1,0:T(8,128)(2,1)}), bf16[8,1024,256]{2,1,0:T(8,128)(2,1)}, u32[]{:S(2)}, u32[]{:S(2)}) %all-to-all-start.1) | async-done | bytes 4194336 | tf_op jit(solution)/shard_map/all_to_all | solution.py:123
  132.6 4.6 %divide_convert_fusion = bf16[4,256,256]{2,0,1:T(4,128)(2,1)S(1)} fusion(bf16[32,4,1]{0,1,2:T(4,128)(2,1)S(1)} %reshape.187, bf16[32,256,256]{2,1,0:T(8,128)(2,1)} %bitcast.11, f32[4]{0:T(128)S(1)} %broadcast_maximum_fusion), kind=kOutput, calls=%fused_computation.135 | convolution fusion | flops 17301504 | bytes 4718864 | tf_op jit(solution)/shard_map/sc,sij->cij/dot_general | solution.py:140
  137.2 0.8 copy-done.1
  138.2 1.9 %collective-permute-start = (bf16[256,4]{1,0:T(8,128)(2,1)S(1)}, bf16[256,4]{1,0:T(8,128)(2,1)S(1)}, u32[]{:S(2)}, u32[]{:S(2)}) collective-permute-start(bf16[256,4]{1,0:T(8,128)(2,1)S(1)} %get-tuple-element.66), channel_id=1, source_target_pairs={{0,1},{1,4},{4,5},{5,8},{8,9},{9,12},{12,13},{2,3},{3,6},{6,7},{7,... | collective-permute-start | bytes 6152 | tf_op jit(solution)/shard_map/ppermute | solution.py:23
  140.1 2.4 %collective-permute-start.1 = (bf16[256,4]{1,0:T(8,128)(2,1)S(1)}, bf16[256,4]{1,0:T(8,128)(2,1)S(1)}, u32[]{:S(2)}, u32[]{:S(2)}) collective-permute-start(bf16[256,4]{1,0:T(8,128)(2,1)S(1)} %get-tuple-element.65), channel_id=1, source_target_pairs={{1,0},{4,1},{5,4},{8,5},{9,8},{12,9},{13,12},{3,2},{6,3},{7,6},{10... | collective-permute-start | bytes 6152 | tf_op jit(solution)/shard_map/ppermute | solution.py:24
  142.5 1.3 broadcast_select_fusion
  143.9 1.8 %collective-permute-done.1 = bf16[256,4]{1,0:T(8,128)(2,1)S(1)} collective-permute-done((bf16[256,4]{1,0:T(8,128)(2,1)S(1)}, bf16[256,4]{1,0:T(8,128)(2,1)S(1)}, u32[]{:S(2)}, u32[]{:S(2)}) %collective-permute-start.1) | collective-permute-done | bytes 2080 | tf_op jit(solution)/shard_map/ppermute | solution.py:24
  146.5 1.3 collective-permute-start.2
  147.7 2.2 %broadcast_in_dim_reshape.3 = bf16[1,256,1024]{2,1,0:T(8,128)(2,1)} reshape(bf16[256,4,256]{2,1,0:T(4,128)(2,1)} %bitcast.46) | data formatting | bytes 1048576 | tf_op jit(solution)/shard_map/broadcast_in_dim;reshape | solution.py:167
  149.9 4.6 %collective-permute-done.2 = bf16[137,1032]{1,0:T(8,128)(2,1)S(1)} collective-permute-done((bf16[137,1032]{1,0:T(8,128)(2,1)S(1)}, bf16[137,1032]{1,0:T(8,128)(2,1)S(1)}, u32[]{:S(2)}, u32[]{:S(2)}) %collective-permute-start.2) | collective-permute-done | bytes 282800 | tf_op jit(solution)/shard_map/ppermute | solution.py:161
  155.2 0.8 multiply_add_fusion
  156.0 1.2 fusion.233
  157.2 1.3 fusion.244
  (44 shorter events, 9.3 us)
Async XLA Ops:
  0.6 19.3 %copy-start = (bf16[1,16,256,256]{3,2,1,0:T(8,128)(2,1)S(1)}, bf16[1,16,256,256]{3,2,1,0:T(8,128)(2,1)}, u32[]{:S(2)}) copy-start(bf16[1,16,256,256]{3,2,1,0:T(8,128)(2,1)} %param.10) | copy-start | bytes 6291460
  2.3 0.5 copy-start.2
  4.4 29.8 %all-to-all-start = ((bf16[8,4,4]{1,2,0:T(4,128)(2,1)}), bf16[8,4,4]{1,2,0:T(4,128)(2,1)S(1)}, u32[]{:S(2)}, u32[]{:S(2)}) async-start(bf16[8,4,4]{1,2,0:T(4,128)(2,1)} %copy.23), calls=%async_computation | async-start | bytes 16384 | tf_op jit(solution)/shard_map/all_to_all | solution.py:130
  34.2 98.3 %all-to-all-start.1 = ((bf16[8,1024,256]{2,1,0:T(8,128)(2,1)}), bf16[8,1024,256]{2,1,0:T(8,128)(2,1)}, u32[]{:S(2)}, u32[]{:S(2)}) async-start(bf16[8,1024,256]{2,1,0:T(8,128)(2,1)} %bitcast.42), calls=%async_computation.1 | async-start | bytes 8388608 | tf_op jit(solution)/shard_map/all_to_all | solution.py:123
  137.2 0.8 copy-start.1
  138.2 5.7 %collective-permute-start = (bf16[256,4]{1,0:T(8,128)(2,1)S(1)}, bf16[256,4]{1,0:T(8,128)(2,1)S(1)}, u32[]{:S(2)}, u32[]{:S(2)}) collective-permute-start(bf16[256,4]{1,0:T(8,128)(2,1)S(1)} %get-tuple-element.66), channel_id=1, source_target_pairs={{0,1},{1,4},{4,5},{5,8},{8,9},{9,12},{12,13},{2,3},{3,6},{6,7},{7,... | collective-permute-start | bytes 6152 | tf_op jit(solution)/shard_map/ppermute | solution.py:23
  140.1 5.6 %collective-permute-start.1 = (bf16[256,4]{1,0:T(8,128)(2,1)S(1)}, bf16[256,4]{1,0:T(8,128)(2,1)S(1)}, u32[]{:S(2)}, u32[]{:S(2)}) collective-permute-start(bf16[256,4]{1,0:T(8,128)(2,1)S(1)} %get-tuple-element.65), channel_id=1, source_target_pairs={{1,0},{4,1},{5,4},{8,5},{9,8},{12,9},{13,12},{3,2},{6,3},{7,6},{10... | collective-permute-start | bytes 6152 | tf_op jit(solution)/shard_map/ppermute | solution.py:24
  146.5 8.1 %collective-permute-start.2 = (bf16[137,1032]{1,0:T(8,128)(2,1)S(1)}, bf16[137,1032]{1,0:T(8,128)(2,1)S(1)}, u32[]{:S(2)}, u32[]{:S(2)}) collective-permute-start(bf16[137,1032]{1,0:T(8,128)(2,1)S(1)} %fusion.254), channel_id=1, source_target_pairs={{0,2},{2,0},{1,3},{3,1},{4,6},{6,4},{5,7},{7,5},{8,10},{10,8},{9,1... | collective-permute-start | bytes 848312 | tf_op jit(solution)/shard_map/ppermute | solution.py:161

commit v8 on v7

--- a/solution.py
+++ b/solution.py
@@ -35,10 +35,10 @@
     spacing = jnp.arange(-band, band + 1, dtype=jnp.float32)
     tap = jnp.arange(-PSF_R, PSF_R + 1, dtype=jnp.float32)
     tap_weight = jnp.exp(-spread[..., None] * (tap * tap))
-    weight_total = jnp.sum(tap_weight, axis=-1)
     taps = lanczos_tap(spacing + (shift[..., None, None] + tap[:, None]))
+    taps = jnp.concatenate([taps, jnp.ones(taps.shape[:-1] + (1,), jnp.float32)], axis=-1)
     summed = jnp.sum(tap_weight[..., None] * taps, axis=-2)
-    return (summed / weight_total[..., None]).astype(jnp.bfloat16)
+    return (summed[..., :-1] / summed[..., -1:]).astype(jnp.bfloat16)
 
 
 def toeplitz(values, side):
@@ -138,13 +138,11 @@
     received = received.reshape(slot_count, side, side)
     received_weight = received_weight.reshape(slot_count, CELL_DEV)
     numerator = jnp.einsum(
-        "sc,sij->cij", received_weight, received, preferred_element_type=jnp.float32
+        "sc,sij->icj", received_weight, received, preferred_element_type=jnp.float32
     )
     denominator = jnp.sum(received_weight.astype(jnp.float32), axis=0)
-    cell_mean = (numerator / jnp.maximum(denominator, 1.0)[:, None, None]).astype(jnp.bfloat16)
-    coadd = (
-        cell_mean.reshape(CELL_DEV, side, side).transpose(1, 0, 2).reshape(side, CELL_DEV * side)
-    )
+    cell_mean = (numerator / jnp.maximum(denominator, 1.0)[None, :, None]).astype(jnp.bfloat16)
+    coadd = cell_mean.reshape(side, CELL_DEV * side)
     padded = extended(coadd, ((("sect", "sub"), 1),), DET_R)
     band_count = lax.axis_size("band")
     height = side // band_count

time: 159 us -> 158 us (level)
  no operation moved by 1% of the time
where the time goes in v8:
time: 158 us
  waiting for transfers between devices  94.1 us (60%)
  starting transfers between devices  17.1 us (11%)
  matrix products  15 us (9%)
  other arithmetic  13.4 us (8%)
  local copies, waits for them, and re-layouts  12.4 us (8%)
  between operations  5.61 us (4%)
    all_to_all x1, waiting for transfers between devices, local(): lax.all_to_all(packed.reshape(owners, capacity * side, side), ('sect', 's...  87.6 us
    dot_general x1, matrix products, local(): jnp.einsum('bij,bkj->bik', section, col_kernel, preferred_element_type=jn...  9.45 us
    all_to_all x1, starting transfers between devices, local(): lax.all_to_all(packed_weight.reshape(owners, capacity, CELL_DEV), ('sect'...  6.38 us
    all_to_all x1, starting transfers between devices, local(): lax.all_to_all(packed.reshape(owners, capacity * side, side), ('sect', 's...  5.1 us
    ppermute x1, waiting for transfers between devices, local(): lax.ppermute(outgoing, 'band', [(i, (i + shift) % band_count) for i in ra...  4.63 us
    dot_general x1, matrix products, local(): jnp.einsum('sc,sij->icj', received_weight, received, preferred_element_ty...  4.63 us
    gather x1, local copies, waits for them, and re-layouts, local(): packed = jnp.take(warped, source, axis=0, mode='clip')  4.33 us
  transfers between devices with their start and end apart: 5, of which 3 were waited for; matrix products, arithmetic and copies ran while one was open for 17% of the time, Pallas kernels for 0%

profile of v8, /device:TPU:1, one launch (start us, length us, event | category | flops | bytes accessed | tf_op | source)
XLA Modules:
  0.0 157.5 jit_solution(18172916688981508260)
XLA Ops:
  0.6 1.0 convert_reduce_fusion.1
  2.8 0.9 convolution_convert_fusion
  4.5 6.4 %all-to-all-start.1 = ((bf16[8,4,4]{1,2,0:T(4,128)(2,1)}), bf16[8,4,4]{1,2,0:T(4,128)(2,1)S(1)}, u32[]{:S(2)}, u32[]{:S(2)}) async-start(bf16[8,4,4]{1,2,0:T(4,128)(2,1)} %copy.22), calls=%async_computation.1 | async-start | bytes 16384 | tf_op jit(solution)/shard_map/all_to_all | solution.py:130
  11.6 0.7 broadcast_add_fusion
  12.3 0.7 fusion.258
  13.5 0.9 slice_reduce_fusion.50
  14.4 0.9 slice_reduce_fusion.25
  15.4 0.9 slice_reduce_fusion.24
  18.8 9.5 %fusion.136 = bf16[16,256,256]{2,1,0:T(8,128)(2,1)} fusion(pred[256,256]{1,0:T(8,128)(4,1)S(1)} %get-tuple-element.75, pred[256,256]{1,0:T(8,128)(4,1)S(1)} %get-tuple-element.76, pred[256,256]{1,0:T(8,128)(4,1)S(1)} %get-tuple-element.77, pred[256,256]{1,0:T(8,128)(4,1)S(1)} %get-tuple-element.78, pred[256,256]{1,0:T(8,128)(4,1)S(1)} %get-tuple-element.79, ...), kind=kOutput, calls=%fused_computation.82 | convolution fusion | flops 1128267776 | bytes 5834304 | tf_op jit(solution)/shard_map/bij,bkj->bik/dot_general | solution.py:101
  28.9 4.3 %gather_fusion = bf16[32,256,256]{2,1,0:T(8,128)(2,1)} fusion(bf16[16,256,256]{2,1,0:T(8,128)(2,1)} %fusion.136, s32[1024]{0:T(1024)S(1)} %pad_clamp_fusion), kind=kCustom, calls=%fused_computation | custom fusion | bytes 8388736 | tf_op jit(solution)/shard_map/jit(_take)/gather | solution.py:113
  33.2 5.1 %all-to-all-start = ((bf16[8,1024,256]{2,1,0:T(8,128)(2,1)}), bf16[8,1024,256]{2,1,0:T(8,128)(2,1)}, u32[]{:S(2)}, u32[]{:S(2)}) async-start(bf16[8,1024,256]{2,1,0:T(8,128)(2,1)} %bitcast.42), calls=%async_computation | async-start | bytes 8388608 | tf_op jit(solution)/shard_map/all_to_all | solution.py:123
  44.0 87.6 %all-to-all-done = bf16[8,1024,256]{2,1,0:T(8,128)(2,1)} async-done(((bf16[8,1024,256]{2,1,0:T(8,128)(2,1)}), bf16[8,1024,256]{2,1,0:T(8,128)(2,1)}, u32[]{:S(2)}, u32[]{:S(2)}) %all-to-all-start) | async-done | bytes 4194336 | tf_op jit(solution)/shard_map/all_to_all | solution.py:123
  131.6 4.6 %divide_convert_fusion = bf16[256,256,4]{1,2,0:T(4,128)(2,1)S(1)} fusion(bf16[32,4,1]{0,1,2:T(4,128)(2,1)S(1)} %reshape.186, bf16[32,256,256]{2,1,0:T(8,128)(2,1)} %bitcast.9, f32[4]{0:T(128)S(1)} %broadcast_maximum_fusion), kind=kOutput, calls=%fused_computation.135 | convolution fusion | flops 17301504 | bytes 4718864 | tf_op jit(solution)/shard_map/sc,sij->icj/dot_general | solution.py:140
  136.2 0.8 copy-done.1
  137.2 1.9 %collective-permute-start = (bf16[256,4]{1,0:T(8,128)(2,1)S(1)}, bf16[256,4]{1,0:T(8,128)(2,1)S(1)}, u32[]{:S(2)}, u32[]{:S(2)}) collective-permute-start(bf16[256,4]{1,0:T(8,128)(2,1)S(1)} %get-tuple-element.66), channel_id=1, source_target_pairs={{0,1},{1,4},{4,5},{5,8},{8,9},{9,12},{12,13},{2,3},{3,6},{6,7},{7,... | collective-permute-start | bytes 6152 | tf_op jit(solution)/shard_map/ppermute | solution.py:23
  139.1 2.4 %collective-permute-start.1 = (bf16[256,4]{1,0:T(8,128)(2,1)S(1)}, bf16[256,4]{1,0:T(8,128)(2,1)S(1)}, u32[]{:S(2)}, u32[]{:S(2)}) collective-permute-start(bf16[256,4]{1,0:T(8,128)(2,1)S(1)} %get-tuple-element.65), channel_id=1, source_target_pairs={{1,0},{4,1},{5,4},{8,5},{9,8},{12,9},{13,12},{3,2},{6,3},{7,6},{10... | collective-permute-start | bytes 6152 | tf_op jit(solution)/shard_map/ppermute | solution.py:24
  141.5 1.3 broadcast_select_fusion
  142.9 1.8 %collective-permute-done.1 = bf16[256,4]{1,0:T(8,128)(2,1)S(1)} collective-permute-done((bf16[256,4]{1,0:T(8,128)(2,1)S(1)}, bf16[256,4]{1,0:T(8,128)(2,1)S(1)}, u32[]{:S(2)}, u32[]{:S(2)}) %collective-permute-start.1) | collective-permute-done | bytes 2080 | tf_op jit(solution)/shard_map/ppermute | solution.py:24
  145.5 1.3 collective-permute-start.2
  146.8 2.2 %broadcast_in_dim_reshape.3 = bf16[1,256,1024]{2,1,0:T(8,128)(2,1)} reshape(bf16[256,4,256]{2,1,0:T(4,128)(2,1)} %bitcast.46) | data formatting | bytes 1048576 | tf_op jit(solution)/shard_map/broadcast_in_dim;reshape | solution.py:165
  148.9 4.6 %collective-permute-done.2 = bf16[137,1032]{1,0:T(8,128)(2,1)S(1)} collective-permute-done((bf16[137,1032]{1,0:T(8,128)(2,1)S(1)}, bf16[137,1032]{1,0:T(8,128)(2,1)S(1)}, u32[]{:S(2)}, u32[]{:S(2)}) %collective-permute-start.2) | collective-permute-done | bytes 282800 | tf_op jit(solution)/shard_map/ppermute | solution.py:159
  154.2 0.8 multiply_add_fusion
  155.0 1.2 fusion.233
  156.2 1.3 fusion.244
  (47 shorter events, 8.6 us)
Async XLA Ops:
  0.6 18.2 %copy-start = (bf16[1,16,256,256]{3,2,1,0:T(8,128)(2,1)S(1)}, bf16[1,16,256,256]{3,2,1,0:T(8,128)(2,1)}, u32[]{:S(2)}) copy-start(bf16[1,16,256,256]{3,2,1,0:T(8,128)(2,1)} %param.10) | copy-start | bytes 6291460
  2.3 0.5 copy-start.2
  4.5 28.8 %all-to-all-start.1 = ((bf16[8,4,4]{1,2,0:T(4,128)(2,1)}), bf16[8,4,4]{1,2,0:T(4,128)(2,1)S(1)}, u32[]{:S(2)}, u32[]{:S(2)}) async-start(bf16[8,4,4]{1,2,0:T(4,128)(2,1)} %copy.22), calls=%async_computation.1 | async-start | bytes 16384 | tf_op jit(solution)/shard_map/all_to_all | solution.py:130
  10.8 7.4 %copy-start.3 = (s32[16]{0:T(128)S(1)}, s32[16]{0:T(128)}, u32[]{:S(2)}) copy-start(s32[16]{0:T(128)} %copy-done.2) | copy-start | bytes 196
  33.2 98.3 %all-to-all-start = ((bf16[8,1024,256]{2,1,0:T(8,128)(2,1)}), bf16[8,1024,256]{2,1,0:T(8,128)(2,1)}, u32[]{:S(2)}, u32[]{:S(2)}) async-start(bf16[8,1024,256]{2,1,0:T(8,128)(2,1)} %bitcast.42), calls=%async_computation | async-start | bytes 8388608 | tf_op jit(solution)/shard_map/all_to_all | solution.py:123
  136.2 0.8 copy-start.1
  137.2 5.7 %collective-permute-start = (bf16[256,4]{1,0:T(8,128)(2,1)S(1)}, bf16[256,4]{1,0:T(8,128)(2,1)S(1)}, u32[]{:S(2)}, u32[]{:S(2)}) collective-permute-start(bf16[256,4]{1,0:T(8,128)(2,1)S(1)} %get-tuple-element.66), channel_id=1, source_target_pairs={{0,1},{1,4},{4,5},{5,8},{8,9},{9,12},{12,13},{2,3},{3,6},{6,7},{7,... | collective-permute-start | bytes 6152 | tf_op jit(solution)/shard_map/ppermute | solution.py:23
  139.1 5.6 %collective-permute-start.1 = (bf16[256,4]{1,0:T(8,128)(2,1)S(1)}, bf16[256,4]{1,0:T(8,128)(2,1)S(1)}, u32[]{:S(2)}, u32[]{:S(2)}) collective-permute-start(bf16[256,4]{1,0:T(8,128)(2,1)S(1)} %get-tuple-element.65), channel_id=1, source_target_pairs={{1,0},{4,1},{5,4},{8,5},{9,8},{12,9},{13,12},{3,2},{6,3},{7,6},{10... | collective-permute-start | bytes 6152 | tf_op jit(solution)/shard_map/ppermute | solution.py:24
  145.5 8.1 %collective-permute-start.2 = (bf16[137,1032]{1,0:T(8,128)(2,1)S(1)}, bf16[137,1032]{1,0:T(8,128)(2,1)S(1)}, u32[]{:S(2)}, u32[]{:S(2)}) collective-permute-start(bf16[137,1032]{1,0:T(8,128)(2,1)S(1)} %fusion.254), channel_id=1, source_target_pairs={{0,2},{2,0},{1,3},{3,1},{4,6},{6,4},{5,7},{7,5},{8,10},{10,8},{9,1... | collective-permute-start | bytes 848312 | tf_op jit(solution)/shard_map/ppermute | solution.py:159

commit v9 on v8

--- a/solution.py
+++ b/solution.py
@@ -3,6 +3,8 @@
 import jax
 import jax.numpy as jnp
 from jax import lax
+from jax.experimental import pallas as pl
+from jax.experimental.pallas import tpu as pltpu
 from jax.sharding import PartitionSpec as P
 
 CELL_DEV = 4
@@ -51,6 +53,62 @@
     return matrix
 
 
+def base_rows(values, side):
+    band = PSF_R + 4
+    gap = jnp.zeros((values.shape[0], side - 2 * band - 1), jnp.float32)
+    values = values.astype(jnp.float32)
+    rows = jnp.concatenate([values[:, 0, band::-1], gap, values[:, 0, : band : -1]], axis=-1)
+    cols = jnp.concatenate([values[:, 1, band:], gap, values[:, 1, :band]], axis=-1)
+    return rows[:, None, :], cols[:, None, :]
+
+
+def warp_kernel(source_ref, rows_ref, cols_ref, image_ref, out_ref):
+    side = image_ref.shape[-1]
+    row_base = jnp.broadcast_to(rows_ref[0], (side, side))
+    col_base = jnp.broadcast_to(cols_ref[0], (side, side))
+    lag = lax.broadcasted_iota(jnp.int32, (side, side), 0) - lax.broadcasted_iota(
+        jnp.int32, (side, side), 1
+    )
+    inside = jnp.abs(lag) <= PSF_R + 4
+    row_kernel = jnp.where(
+        inside, pltpu.roll(row_base, 0, 1, stride=1, stride_axis=0), 0.0
+    ).astype(jnp.bfloat16)
+    col_kernel_t = jnp.where(
+        inside, pltpu.roll(col_base, 0, 1, stride=1, stride_axis=0), 0.0
+    ).astype(jnp.bfloat16)
+    section = jnp.dot(row_kernel, image_ref[0], preferred_element_type=jnp.float32)
+    out_ref[0] = jnp.dot(
+        section.astype(jnp.bfloat16), col_kernel_t, preferred_element_type=jnp.float32
+    ).astype(jnp.bfloat16)
+
+
+def warp_slots(images, values, source, interpret=False):
+    count, side = images.shape[0], images.shape[-1]
+    slot_count = source.shape[0]
+    rows, cols = base_rows(values, side)
+    vector_spec = pl.BlockSpec((1, 1, side), lambda s, src: (src[s], 0, 0))
+    return pl.pallas_call(
+        warp_kernel,
+        grid_spec=pltpu.PrefetchScalarGridSpec(
+            num_scalar_prefetch=1,
+            grid=(slot_count,),
+            in_specs=[
+                vector_spec,
+                vector_spec,
+                pl.BlockSpec((1, side, side), lambda s, src: (src[s], 0, 0)),
+            ],
+            out_specs=pl.BlockSpec((1, side, side), lambda s, src: (s, 0, 0)),
+        ),
+        out_shape=jax.ShapeDtypeStruct((slot_count, side, side), jnp.bfloat16),
+        cost_estimate=pl.CostEstimate(
+            flops=4 * slot_count * side**3,
+            transcendentals=0,
+            bytes_accessed=4 * slot_count * side * side,
+        ),
+        interpret=interpret,
+    )(source, rows, cols, images)
+
+
 def gain_pieces(gain):
     high = lax.reduce_precision(gain, exponent_bits=8, mantissa_bits=7)
     rest = gain - high
@@ -93,14 +151,6 @@
     capacity = max(2, -(-2 * count // owners))
     slot_count = owners * capacity
     values = band_values(offsets[0], widths[0])
-    row_kernel = toeplitz(values[:, 0], side)
-    col_kernel = toeplitz(values[:, 1], side)
-    section = jnp.einsum(
-        "bij,bjk->bik", row_kernel, images[0], preferred_element_type=jnp.float32
-    ).astype(jnp.bfloat16)
-    warped = jnp.einsum(
-        "bij,bkj->bik", section, col_kernel, preferred_element_type=jnp.float32
-    ).astype(jnp.bfloat16)
     target = dest[0]
     same_owner = target[:, None] == target[None, :]
     block_order = jnp.arange(count, dtype=jnp.int32)
@@ -110,7 +160,7 @@
     matching = jnp.arange(slot_count, dtype=jnp.int32)[:, None] == slot_index[None, :]
     source = jnp.sum(jnp.where(matching, block_order[None, :], 0), axis=1)
     placing = matching.astype(jnp.bfloat16)
-    packed = jnp.take(warped, source, axis=0, mode="clip")
+    packed = warp_slots(images[0], values, source)
     cell_weight = jnp.where(
         cells[0][:, None] == jnp.arange(CELL_DEV, dtype=jnp.int32)[None, :],
         weights[0][:, None],

time: 158 us -> 162 us (1.025)
  Pallas kernels: 0 us -> 22.5 us
  matrix products: 15 us -> 5.55 us
  local copies, waits for them, and re-layouts: 12.4 us -> 4.6 us
  other arithmetic: 13.4 us -> 10.9 us
    pallas_call x0 -> x1, Pallas kernels: none -> 22.5 us  [warp_slots(): pl.pallas_call(warp_kernel, grid_spec=pltpu.PrefetchScalarGridSpec(num_sc...]
    dot_general x1 -> x0, matrix products: 9.45 us -> none  [local(): jnp.einsum('bij,bkj->bik', section, col_kernel, preferred_element_type=jn...]
    gather x1 -> x0, local copies, waits for them, and re-layouts: 4.33 us -> none  [local(): packed = jnp.take(warped, source, axis=0, mode='clip')]
    slice x3 -> x0, local copies, waits for them, and re-layouts: 2.7 us -> none  [toeplitz(): values[..., index, None, None]]
    eq x13 -> x0, other arithmetic: 1.9 us -> none  [toeplitz(): lag == index - band]
  transfers between devices with their start and end apart: 5 -> 5, of which waited for: 3 -> 3; matrix products, arithmetic and copies ran while one was open for 17% -> 5% of each run, Pallas kernels for 0% -> 14%
where the time goes in v9:
time: 162 us
  waiting for transfers between devices  95.3 us (59%)
  Pallas kernels  22.5 us (14%)
  starting transfers between devices  17.3 us (11%)
  other arithmetic  10.9 us (7%)
  matrix products  5.55 us (3%)
  between operations  5.49 us (3%)
  local copies, waits for them, and re-layouts  4.6 us (3%)
    all_to_all x1, waiting for transfers between devices, local(): lax.all_to_all(packed.reshape(owners, capacity * side, side), ('sect', 's...  87.6 us
    pallas_call x1, Pallas kernels, warp_slots(): pl.pallas_call(warp_kernel, grid_spec=pltpu.PrefetchScalarGridSpec(num_sc...  22.5 us
    all_to_all x1, starting transfers between devices, local(): lax.all_to_all(packed_weight.reshape(owners, capacity, CELL_DEV), ('sect'...  6.38 us
    ppermute x1, waiting for transfers between devices, local(): lax.ppermute(outgoing, 'band', [(i, (i + shift) % band_count) for i in ra...  5.85 us
    all_to_all x1, starting transfers between devices, local(): lax.all_to_all(packed.reshape(owners, capacity * side, side), ('sect', 's...  5.45 us
    dot_general x1, matrix products, local(): jnp.einsum('sc,sij->icj', received_weight, received, preferred_element_ty...  4.63 us
  transfers between devices with their start and end apart: 5, of which 3 were waited for; matrix products, arithmetic and copies ran while one was open for 5% of the time, Pallas kernels for 14%

profile of v9, /device:TPU:1, one launch (start us, length us, event | category | flops | bytes accessed | tf_op | source)
XLA Modules:
  0.0 161.5 jit_solution(6268041668404742502)
XLA Ops:
  0.6 0.9 convert_reduce_fusion.1
  1.5 0.7 fusion.77
  2.2 0.9 convolution_convert_fusion
  3.8 6.4 %all-to-all-start.1 = ((bf16[8,4,4]{1,2,0:T(4,128)(2,1)}), bf16[8,4,4]{1,2,0:T(4,128)(2,1)S(1)}, u32[]{:S(2)}, u32[]{:S(2)}) async-start(bf16[8,4,4]{1,2,0:T(4,128)(2,1)} %copy.23), calls=%async_computation.1 | async-start | bytes 16384 | tf_op jit(solution)/shard_map/all_to_all | solution.py:180
  10.2 0.7 negate_bitcast_fusion
  10.9 0.7 broadcast_add_fusion
  11.7 0.7 fusion.38
  13.0 0.6 select_reduce_fusion.source_ref
  14.6 0.6 copy.22.rows_ref
  15.2 22.5 %shard_map.86 = bf16[32,256,256]{2,1,0:T(8,128)(2,1)} custom-call(s32[32]{0:T(128)} %select_reduce_fusion.source_ref, f32[16,1,256]{2,1,0:T(1,128)} %copy.22.rows_ref, f32[16,1,256]{2,1,0:T(1,128)} %broadcast_in_dim.59.cols_ref, bf16[16,256,256]{2,1,0:T(8,128)(2,1)} %bitcast.46), custom_call_target="tpu_custom_call" | custom-call | flops 2147483648 | bytes 8388608 | tf_op jit(solution)/shard_map/pallas_call | solution.py:90
  37.7 5.4 %all-to-all-start = ((bf16[8,1024,256]{2,1,0:T(8,128)(2,1)}), bf16[8,1024,256]{2,1,0:T(8,128)(2,1)}, u32[]{:S(2)}, u32[]{:S(2)}) async-start(bf16[8,1024,256]{2,1,0:T(8,128)(2,1)} %bitcast.38), calls=%async_computation | async-start | bytes 8388608 | tf_op jit(solution)/shard_map/all_to_all | solution.py:173
  47.9 0.6 compare_reduce_fusion
  48.8 87.6 %all-to-all-done = bf16[8,1024,256]{2,1,0:T(8,128)(2,1)} async-done(((bf16[8,1024,256]{2,1,0:T(8,128)(2,1)}), bf16[8,1024,256]{2,1,0:T(8,128)(2,1)}, u32[]{:S(2)}, u32[]{:S(2)}) %all-to-all-start) | async-done | bytes 4194336 | tf_op jit(solution)/shard_map/all_to_all | solution.py:173
  136.4 4.6 %divide_convert_fusion = bf16[256,256,4]{1,2,0:T(4,128)(2,1)S(1)} fusion(bf16[32,4,1]{0,1,2:T(4,128)(2,1)S(1)} %reshape.127, bf16[32,256,256]{2,1,0:T(8,128)(2,1)} %bitcast.12, f32[4]{0:T(128)S(1)} %broadcast_maximum_fusion), kind=kOutput, calls=%fused_computation.3 | convolution fusion | flops 17301504 | bytes 4718864 | tf_op jit(solution)/shard_map/sc,sij->icj/dot_general | solution.py:190
  141.2 1.9 %collective-permute-start = (bf16[256,4]{1,0:T(8,128)(2,1)S(1)}, bf16[256,4]{1,0:T(8,128)(2,1)S(1)}, u32[]{:S(2)}, u32[]{:S(2)}) collective-permute-start(bf16[256,4]{1,0:T(8,128)(2,1)S(1)} %get-tuple-element.16), channel_id=1, source_target_pairs={{0,1},{1,4},{4,5},{5,8},{8,9},{9,12},{12,13},{2,3},{3,6},{6,7},{7,... | collective-permute-start | bytes 6152 | tf_op jit(solution)/shard_map/ppermute | solution.py:25
  143.1 2.4 %collective-permute-start.1 = (bf16[256,4]{1,0:T(8,128)(2,1)S(1)}, bf16[256,4]{1,0:T(8,128)(2,1)S(1)}, u32[]{:S(2)}, u32[]{:S(2)}) collective-permute-start(bf16[256,4]{1,0:T(8,128)(2,1)S(1)} %get-tuple-element.15), channel_id=1, source_target_pairs={{1,0},{4,1},{5,4},{8,5},{9,8},{12,9},{13,12},{3,2},{6,3},{7,6},{10... | collective-permute-start | bytes 6152 | tf_op jit(solution)/shard_map/ppermute | solution.py:26
  145.6 1.4 broadcast_select_fusion
  146.9 1.8 %collective-permute-done.1 = bf16[256,4]{1,0:T(8,128)(2,1)S(1)} collective-permute-done((bf16[256,4]{1,0:T(8,128)(2,1)S(1)}, bf16[256,4]{1,0:T(8,128)(2,1)S(1)}, u32[]{:S(2)}, u32[]{:S(2)}) %collective-permute-start.1) | collective-permute-done | bytes 2080 | tf_op jit(solution)/shard_map/ppermute | solution.py:26
  149.5 1.1 collective-permute-start.2
  150.6 1.2 broadcast_in_dim_reshape.3
  151.7 5.9 %collective-permute-done.2 = bf16[137,1032]{1,0:T(8,128)(2,1)S(1)} collective-permute-done((bf16[137,1032]{1,0:T(8,128)(2,1)S(1)}, bf16[137,1032]{1,0:T(8,128)(2,1)S(1)}, u32[]{:S(2)}, u32[]{:S(2)}) %collective-permute-start.2) | collective-permute-done | bytes 282800 | tf_op jit(solution)/shard_map/ppermute | solution.py:209
  158.2 0.8 multiply_add_fusion
  159.0 1.2 fusion.13
  160.2 1.3 fusion.24
  (29 shorter events, 4.0 us)
Async XLA Ops:
  3.8 33.9 %all-to-all-start.1 = ((bf16[8,4,4]{1,2,0:T(4,128)(2,1)}), bf16[8,4,4]{1,2,0:T(4,128)(2,1)S(1)}, u32[]{:S(2)}, u32[]{:S(2)}) async-start(bf16[8,4,4]{1,2,0:T(4,128)(2,1)} %copy.23), calls=%async_computation.1 | async-start | bytes 16384 | tf_op jit(solution)/shard_map/all_to_all | solution.py:180
  37.7 98.7 %all-to-all-start = ((bf16[8,1024,256]{2,1,0:T(8,128)(2,1)}), bf16[8,1024,256]{2,1,0:T(8,128)(2,1)}, u32[]{:S(2)}, u32[]{:S(2)}) async-start(bf16[8,1024,256]{2,1,0:T(8,128)(2,1)} %bitcast.38), calls=%async_computation | async-start | bytes 8388608 | tf_op jit(solution)/shard_map/all_to_all | solution.py:173
  141.2 5.7 %collective-permute-start = (bf16[256,4]{1,0:T(8,128)(2,1)S(1)}, bf16[256,4]{1,0:T(8,128)(2,1)S(1)}, u32[]{:S(2)}, u32[]{:S(2)}) collective-permute-start(bf16[256,4]{1,0:T(8,128)(2,1)S(1)} %get-tuple-element.16), channel_id=1, source_target_pairs={{0,1},{1,4},{4,5},{5,8},{8,9},{9,12},{12,13},{2,3},{3,6},{6,7},{7,... | collective-permute-start | bytes 6152 | tf_op jit(solution)/shard_map/ppermute | solution.py:25
  143.1 5.6 %collective-permute-start.1 = (bf16[256,4]{1,0:T(8,128)(2,1)S(1)}, bf16[256,4]{1,0:T(8,128)(2,1)S(1)}, u32[]{:S(2)}, u32[]{:S(2)}) collective-permute-start(bf16[256,4]{1,0:T(8,128)(2,1)S(1)} %get-tuple-element.15), channel_id=1, source_target_pairs={{1,0},{4,1},{5,4},{8,5},{9,8},{12,9},{13,12},{3,2},{6,3},{7,6},{10... | collective-permute-start | bytes 6152 | tf_op jit(solution)/shard_map/ppermute | solution.py:26
  149.5 8.1 %collective-permute-start.2 = (bf16[137,1032]{1,0:T(8,128)(2,1)S(1)}, bf16[137,1032]{1,0:T(8,128)(2,1)S(1)}, u32[]{:S(2)}, u32[]{:S(2)}) collective-permute-start(bf16[137,1032]{1,0:T(8,128)(2,1)S(1)} %fusion.34), channel_id=1, source_target_pairs={{0,2},{2,0},{1,3},{3,1},{4,6},{6,4},{5,7},{7,5},{8,10},{10,8},{9,1... | collective-permute-start | bytes 848312 | tf_op jit(solution)/shard_map/ppermute | solution.py:209

commit v10 on v9

--- a/solution.py
+++ b/solution.py
@@ -62,7 +62,7 @@
     return rows[:, None, :], cols[:, None, :]
 
 
-def warp_kernel(source_ref, rows_ref, cols_ref, image_ref, out_ref):
+def warp_kernel(slot_ref, rows_ref, cols_ref, image_ref, blank_ref, out_ref):
     side = image_ref.shape[-1]
     row_base = jnp.broadcast_to(rows_ref[0], (side, side))
     col_base = jnp.broadcast_to(cols_ref[0], (side, side))
@@ -82,31 +82,33 @@
     ).astype(jnp.bfloat16)
 
 
-def warp_slots(images, values, source, interpret=False):
+def warp_slots(images, values, slot_index, slot_count, interpret=False):
     count, side = images.shape[0], images.shape[-1]
-    slot_count = source.shape[0]
     rows, cols = base_rows(values, side)
-    vector_spec = pl.BlockSpec((1, 1, side), lambda s, src: (src[s], 0, 0))
+    blank = jnp.zeros((slot_count, side, side), jnp.bfloat16)
+    vector_spec = pl.BlockSpec((1, 1, side), lambda b, slots: (b, 0, 0))
     return pl.pallas_call(
         warp_kernel,
         grid_spec=pltpu.PrefetchScalarGridSpec(
             num_scalar_prefetch=1,
-            grid=(slot_count,),
+            grid=(count,),
             in_specs=[
                 vector_spec,
                 vector_spec,
-                pl.BlockSpec((1, side, side), lambda s, src: (src[s], 0, 0)),
+                pl.BlockSpec((1, side, side), lambda b, slots: (b, 0, 0)),
+                pl.BlockSpec(memory_space=pl.ANY),
             ],
-            out_specs=pl.BlockSpec((1, side, side), lambda s, src: (s, 0, 0)),
+            out_specs=pl.BlockSpec((1, side, side), lambda b, slots: (slots[b], 0, 0)),
         ),
         out_shape=jax.ShapeDtypeStruct((slot_count, side, side), jnp.bfloat16),
+        input_output_aliases={4: 0},
         cost_estimate=pl.CostEstimate(
-            flops=4 * slot_count * side**3,
+            flops=4 * count * side**3,
             transcendentals=0,
-            bytes_accessed=4 * slot_count * side * side,
+            bytes_accessed=2 * (2 * count + slot_count) * side * side,
         ),
         interpret=interpret,
-    )(source, rows, cols, images)
+    )(slot_index, rows, cols, images, blank)
 
 
 def gain_pieces(gain):
@@ -160,7 +162,9 @@
     matching = jnp.arange(slot_count, dtype=jnp.int32)[:, None] == slot_index[None, :]
     source = jnp.sum(jnp.where(matching, block_order[None, :], 0), axis=1)
     placing = matching.astype(jnp.bfloat16)
-    packed = warp_slots(images[0], values, source)
+    packed = warp_slots(
+        images[0], values, jnp.minimum(slot_index, slot_count - 1).astype(jnp.int32), slot_count
+    )
     cell_weight = jnp.where(
         cells[0][:, None] == jnp.arange(CELL_DEV, dtype=jnp.int32)[None, :],
         weights[0][:, None],

time: 162 us -> 155 us (0.957)
  Pallas kernels: 22.5 us -> 13 us
  local copies, waits for them, and re-layouts: 4.6 us -> 7.05 us
    pallas_call x1, Pallas kernels: 22.5 us -> 13 us  [warp_slots(): pl.pallas_call(warp_kernel, grid_spec=pltpu.PrefetchScalarGridSpec(num_sc...]
    broadcast_in_dim x0 -> x1, local copies, waits for them, and re-layouts: none -> 2.44 us  [warp_slots(): blank = jnp.zeros((slot_count, side, side), jnp.bfloat16)]
  transfers between devices with their start and end apart: 5 -> 5, of which waited for: 3 -> 3; matrix products, arithmetic and copies ran while one was open for 5% -> 7% of each run, Pallas kernels for 14% -> 8%
where the time goes in v10:
time: 155 us
  waiting for transfers between devices  95.1 us (61%)
  starting transfers between devices  17.1 us (11%)
  Pallas kernels  13 us (8%)
  other arithmetic  11.4 us (7%)
  local copies, waits for them, and re-layouts  7.05 us (5%)
  matrix products  5.55 us (4%)
  between operations  5.49 us (4%)
    all_to_all x1, waiting for transfers between devices, local(): lax.all_to_all(packed.reshape(owners, capacity * side, side), ('sect', 's...  87.6 us
    pallas_call x1, Pallas kernels, warp_slots(): pl.pallas_call(warp_kernel, grid_spec=pltpu.PrefetchScalarGridSpec(num_sc...  13 us
    all_to_all x1, starting transfers between devices, local(): lax.all_to_all(packed_weight.reshape(owners, capacity, CELL_DEV), ('sect'...  6.38 us
    ppermute x1, waiting for transfers between devices, local(): lax.ppermute(outgoing, 'band', [(i, (i + shift) % band_count) for i in ra...  5.67 us
    all_to_all x1, starting transfers between devices, local(): lax.all_to_all(packed.reshape(owners, capacity * side, side), ('sect', 's...  5.09 us
    dot_general x1, matrix products, local(): jnp.einsum('sc,sij->icj', received_weight, received, preferred_element_ty...  4.63 us
  transfers between devices with their start and end apart: 5, of which 3 were waited for; matrix products, arithmetic and copies ran while one was open for 7% of the time, Pallas kernels for 8%

profile of v10, /device:TPU:1, one launch (start us, length us, event | category | flops | bytes accessed | tf_op | source)
XLA Modules:
  0.0 154.6 jit_solution(14467643615879584321)
XLA Ops:
  0.6 0.9 convert_reduce_fusion.1
  1.5 0.7 fusion.77
  2.2 0.9 convolution_convert_fusion
  3.8 6.4 %all-to-all-start.1 = ((bf16[8,4,4]{1,2,0:T(4,128)(2,1)}), bf16[8,4,4]{1,2,0:T(4,128)(2,1)S(1)}, u32[]{:S(2)}, u32[]{:S(2)}) async-start(bf16[8,4,4]{1,2,0:T(4,128)(2,1)} %copy.24), calls=%async_computation.1 | async-start | bytes 16384 | tf_op jit(solution)/shard_map/all_to_all | solution.py:184
  10.2 0.7 negate_bitcast_fusion
  10.9 0.7 broadcast_add_fusion
  11.7 0.7 fusion.38
  13.0 1.2 add_minimum_fusion.slot_ref
  15.7 2.4 %broadcast_in_dim.48.blank_ref = bf16[32,256,256]{2,1,0:T(8,128)(2,1)} broadcast(bf16[]{:T(256)} %constant.102.clone.1), dimensions={} | broadcast | bytes 4194306 | tf_op jit(solution)/shard_map/broadcast_in_dim | solution.py:88
  18.2 13.0 %shard_map.86 = bf16[32,256,256]{2,1,0:T(8,128)(2,1)} custom-call(s32[16]{0:T(128)} %add_minimum_fusion.slot_ref, f32[16,1,256]{2,1,0:T(1,128)} %copy.23.rows_ref, f32[16,1,256]{2,1,0:T(1,128)} %broadcast_in_dim.47.cols_ref, bf16[16,256,256]{2,1,0:T(8,128)(2,1)} %bitcast.44, ...), custom_call_target="tpu_custom_call", output_to_operand_aliasing={{}: (4, {})} | custom-call | flops 1073741824 | bytes 8388608 | tf_op jit(solution)/shard_map/pallas_call | solution.py:90
  31.1 5.1 %all-to-all-start = ((bf16[8,1024,256]{2,1,0:T(8,128)(2,1)}), bf16[8,1024,256]{2,1,0:T(8,128)(2,1)}, u32[]{:S(2)}, u32[]{:S(2)}) async-start(bf16[8,1024,256]{2,1,0:T(8,128)(2,1)} %bitcast.39), calls=%async_computation | async-start | bytes 8388608 | tf_op jit(solution)/shard_map/all_to_all | solution.py:177
  41.0 0.6 compare_reduce_fusion
  41.9 87.6 %all-to-all-done = bf16[8,1024,256]{2,1,0:T(8,128)(2,1)} async-done(((bf16[8,1024,256]{2,1,0:T(8,128)(2,1)}), bf16[8,1024,256]{2,1,0:T(8,128)(2,1)}, u32[]{:S(2)}, u32[]{:S(2)}) %all-to-all-start) | async-done | bytes 4194336 | tf_op jit(solution)/shard_map/all_to_all | solution.py:177
  129.5 4.6 %divide_convert_fusion = bf16[256,256,4]{1,2,0:T(4,128)(2,1)S(1)} fusion(bf16[32,4,1]{0,1,2:T(4,128)(2,1)S(1)} %reshape.127, bf16[32,256,256]{2,1,0:T(8,128)(2,1)} %bitcast.10, f32[4]{0:T(128)S(1)} %broadcast_maximum_fusion), kind=kOutput, calls=%fused_computation.3 | convolution fusion | flops 17301504 | bytes 4718864 | tf_op jit(solution)/shard_map/sc,sij->icj/dot_general | solution.py:194
  134.3 1.9 %collective-permute-start = (bf16[256,4]{1,0:T(8,128)(2,1)S(1)}, bf16[256,4]{1,0:T(8,128)(2,1)S(1)}, u32[]{:S(2)}, u32[]{:S(2)}) collective-permute-start(bf16[256,4]{1,0:T(8,128)(2,1)S(1)} %get-tuple-element.16), channel_id=1, source_target_pairs={{0,1},{1,4},{4,5},{5,8},{8,9},{9,12},{12,13},{2,3},{3,6},{6,7},{7,... | collective-permute-start | bytes 6152 | tf_op jit(solution)/shard_map/ppermute | solution.py:25
  136.2 2.4 %collective-permute-start.1 = (bf16[256,4]{1,0:T(8,128)(2,1)S(1)}, bf16[256,4]{1,0:T(8,128)(2,1)S(1)}, u32[]{:S(2)}, u32[]{:S(2)}) collective-permute-start(bf16[256,4]{1,0:T(8,128)(2,1)S(1)} %get-tuple-element.15), channel_id=1, source_target_pairs={{1,0},{4,1},{5,4},{8,5},{9,8},{12,9},{13,12},{3,2},{6,3},{7,6},{10... | collective-permute-start | bytes 6152 | tf_op jit(solution)/shard_map/ppermute | solution.py:26
  138.6 1.4 broadcast_select_fusion
  140.0 1.8 %collective-permute-done.1 = bf16[256,4]{1,0:T(8,128)(2,1)S(1)} collective-permute-done((bf16[256,4]{1,0:T(8,128)(2,1)S(1)}, bf16[256,4]{1,0:T(8,128)(2,1)S(1)}, u32[]{:S(2)}, u32[]{:S(2)}) %collective-permute-start.1) | collective-permute-done | bytes 2080 | tf_op jit(solution)/shard_map/ppermute | solution.py:26
  142.6 1.3 collective-permute-start.2
  143.8 1.2 broadcast_in_dim_reshape.3
  145.0 5.7 %collective-permute-done.2 = bf16[137,1032]{1,0:T(8,128)(2,1)S(1)} collective-permute-done((bf16[137,1032]{1,0:T(8,128)(2,1)S(1)}, bf16[137,1032]{1,0:T(8,128)(2,1)S(1)}, u32[]{:S(2)}, u32[]{:S(2)}) %collective-permute-start.2) | collective-permute-done | bytes 282800 | tf_op jit(solution)/shard_map/ppermute | solution.py:213
  151.3 0.8 multiply_add_fusion
  152.1 1.2 fusion.13
  153.3 1.3 fusion.24
  (30 shorter events, 4.6 us)
Async XLA Ops:
  3.8 27.3 %all-to-all-start.1 = ((bf16[8,4,4]{1,2,0:T(4,128)(2,1)}), bf16[8,4,4]{1,2,0:T(4,128)(2,1)S(1)}, u32[]{:S(2)}, u32[]{:S(2)}) async-start(bf16[8,4,4]{1,2,0:T(4,128)(2,1)} %copy.24), calls=%async_computation.1 | async-start | bytes 16384 | tf_op jit(solution)/shard_map/all_to_all | solution.py:184
  31.1 98.3 %all-to-all-start = ((bf16[8,1024,256]{2,1,0:T(8,128)(2,1)}), bf16[8,1024,256]{2,1,0:T(8,128)(2,1)}, u32[]{:S(2)}, u32[]{:S(2)}) async-start(bf16[8,1024,256]{2,1,0:T(8,128)(2,1)} %bitcast.39), calls=%async_computation | async-start | bytes 8388608 | tf_op jit(solution)/shard_map/all_to_all | solution.py:177
  134.3 5.7 %collective-permute-start = (bf16[256,4]{1,0:T(8,128)(2,1)S(1)}, bf16[256,4]{1,0:T(8,128)(2,1)S(1)}, u32[]{:S(2)}, u32[]{:S(2)}) collective-permute-start(bf16[256,4]{1,0:T(8,128)(2,1)S(1)} %get-tuple-element.16), channel_id=1, source_target_pairs={{0,1},{1,4},{4,5},{5,8},{8,9},{9,12},{12,13},{2,3},{3,6},{6,7},{7,... | collective-permute-start | bytes 6152 | tf_op jit(solution)/shard_map/ppermute | solution.py:25
  136.2 5.6 %collective-permute-start.1 = (bf16[256,4]{1,0:T(8,128)(2,1)S(1)}, bf16[256,4]{1,0:T(8,128)(2,1)S(1)}, u32[]{:S(2)}, u32[]{:S(2)}) collective-permute-start(bf16[256,4]{1,0:T(8,128)(2,1)S(1)} %get-tuple-element.15), channel_id=1, source_target_pairs={{1,0},{4,1},{5,4},{8,5},{9,8},{12,9},{13,12},{3,2},{6,3},{7,6},{10... | collective-permute-start | bytes 6152 | tf_op jit(solution)/shard_map/ppermute | solution.py:26
  142.6 8.1 %collective-permute-start.2 = (bf16[137,1032]{1,0:T(8,128)(2,1)S(1)}, bf16[137,1032]{1,0:T(8,128)(2,1)S(1)}, u32[]{:S(2)}, u32[]{:S(2)}) collective-permute-start(bf16[137,1032]{1,0:T(8,128)(2,1)S(1)} %fusion.34), channel_id=1, source_target_pairs={{0,2},{2,0},{1,3},{3,1},{4,6},{6,4},{5,7},{7,5},{8,10},{10,8},{9,1... | collective-permute-start | bytes 848312 | tf_op jit(solution)/shard_map/ppermute | solution.py:213

commit v11 on v10

--- a/solution.py
+++ b/solution.py
@@ -62,20 +62,17 @@
     return rows[:, None, :], cols[:, None, :]
 
 
-def warp_kernel(slot_ref, rows_ref, cols_ref, image_ref, blank_ref, out_ref):
+def warp_kernel(slot_ref, rows_ref, cols_ref, inside_ref, image_ref, blank_ref, out_ref):
     side = image_ref.shape[-1]
     row_base = jnp.broadcast_to(rows_ref[0], (side, side))
     col_base = jnp.broadcast_to(cols_ref[0], (side, side))
-    lag = lax.broadcasted_iota(jnp.int32, (side, side), 0) - lax.broadcasted_iota(
-        jnp.int32, (side, side), 1
-    )
-    inside = jnp.abs(lag) <= PSF_R + 4
-    row_kernel = jnp.where(
-        inside, pltpu.roll(row_base, 0, 1, stride=1, stride_axis=0), 0.0
-    ).astype(jnp.bfloat16)
-    col_kernel_t = jnp.where(
-        inside, pltpu.roll(col_base, 0, 1, stride=1, stride_axis=0), 0.0
-    ).astype(jnp.bfloat16)
+    inside = inside_ref[...]
+    row_kernel = (pltpu.roll(row_base, 0, 1, stride=1, stride_axis=0) * inside).astype(
+        jnp.bfloat16
+    )
+    col_kernel_t = (pltpu.roll(col_base, 0, 1, stride=1, stride_axis=0) * inside).astype(
+        jnp.bfloat16
+    )
     section = jnp.dot(row_kernel, image_ref[0], preferred_element_type=jnp.float32)
     out_ref[0] = jnp.dot(
         section.astype(jnp.bfloat16), col_kernel_t, preferred_element_type=jnp.float32
@@ -86,6 +83,8 @@
     count, side = images.shape[0], images.shape[-1]
     rows, cols = base_rows(values, side)
     blank = jnp.zeros((slot_count, side, side), jnp.bfloat16)
+    position = jnp.arange(side, dtype=jnp.int32)
+    inside = (jnp.abs(position[:, None] - position[None, :]) <= PSF_R + 4).astype(jnp.float32)
     vector_spec = pl.BlockSpec((1, 1, side), lambda b, slots: (b, 0, 0))
     return pl.pallas_call(
         warp_kernel,
@@ -95,20 +94,21 @@
             in_specs=[
                 vector_spec,
                 vector_spec,
+                pl.BlockSpec((side, side), lambda b, slots: (0, 0)),
                 pl.BlockSpec((1, side, side), lambda b, slots: (b, 0, 0)),
                 pl.BlockSpec(memory_space=pl.ANY),
             ],
             out_specs=pl.BlockSpec((1, side, side), lambda b, slots: (slots[b], 0, 0)),
         ),
         out_shape=jax.ShapeDtypeStruct((slot_count, side, side), jnp.bfloat16),
-        input_output_aliases={4: 0},
+        input_output_aliases={5: 0},
         cost_estimate=pl.CostEstimate(
             flops=4 * count * side**3,
             transcendentals=0,
             bytes_accessed=2 * (2 * count + slot_count) * side * side,
         ),
         interpret=interpret,
-    )(slot_index, rows, cols, images, blank)
+    )(slot_index, rows, cols, inside, images, blank)
 
 
 def gain_pieces(gain):

time: 155 us -> 156 us (level)
  transfers between devices with their start and end apart: 5 -> 5, of which waited for: 3 -> 3; matrix products, arithmetic and copies ran while one was open for 7% -> 8% of each run, Pallas kernels for 8% -> 8%
where the time goes in v11:
time: 156 us; the launch traced here: 155 us
  waiting for transfers between devices  95.1 us (61%)
  starting transfers between devices  17.1 us (11%)
  Pallas kernels  13 us (8%)
  other arithmetic  12.2 us (8%)
  local copies, waits for them, and re-layouts  7.03 us (5%)
  matrix products  5.55 us (4%)
  between operations  5.49 us (4%)
    all_to_all x1, waiting for transfers between devices, local(): lax.all_to_all(packed.reshape(owners, capacity * side, side), ('sect', 's...  87.6 us
    pallas_call x1, Pallas kernels, warp_slots(): pl.pallas_call(warp_kernel, grid_spec=pltpu.PrefetchScalarGridSpec(num_sc...  13 us
    all_to_all x1, starting transfers between devices, local(): lax.all_to_all(packed_weight.reshape(owners, capacity, CELL_DEV), ('sect'...  6.38 us
    ppermute x1, waiting for transfers between devices, local(): lax.ppermute(outgoing, 'band', [(i, (i + shift) % band_count) for i in ra...  5.69 us
    all_to_all x1, starting transfers between devices, local(): lax.all_to_all(packed.reshape(owners, capacity * side, side), ('sect', 's...  5.12 us
    dot_general x1, matrix products, local(): jnp.einsum('sc,sij->icj', received_weight, received, preferred_element_ty...  4.63 us
  transfers between devices with their start and end apart: 5, of which 3 were waited for; matrix products, arithmetic and copies ran while one was open for 8% of the time, Pallas kernels for 8%

profile of v11, /device:TPU:1, one launch (start us, length us, event | category | flops | bytes accessed | tf_op | source)
XLA Modules:
  0.0 155.4 jit_solution(11100857725475147062)
XLA Ops:
  0.6 0.9 convert_reduce_fusion.1
  1.5 0.7 fusion.78
  2.2 0.9 convolution_convert_fusion
  3.8 6.4 %all-to-all-start.1 = ((bf16[8,4,4]{1,2,0:T(4,128)(2,1)}), bf16[8,4,4]{1,2,0:T(4,128)(2,1)S(1)}, u32[]{:S(2)}, u32[]{:S(2)}) async-start(bf16[8,4,4]{1,2,0:T(4,128)(2,1)} %copy.24), calls=%async_computation.1 | async-start | bytes 16384 | tf_op jit(solution)/shard_map/all_to_all | solution.py:184
  10.2 0.7 negate_bitcast_fusion
  10.9 0.7 broadcast_add_fusion
  11.7 0.7 fusion.38
  13.0 1.2 add_minimum_fusion.slot_ref
  14.2 0.7 fusion.67.inside_ref
  16.5 2.4 %broadcast_in_dim.50.blank_ref = bf16[32,256,256]{2,1,0:T(8,128)(2,1)} broadcast(bf16[]{:T(256)} %constant.104.clone.1), dimensions={} | broadcast | bytes 4194306 | tf_op jit(solution)/shard_map/broadcast_in_dim | solution.py:85
  18.9 13.0 %shard_map.86 = bf16[32,256,256]{2,1,0:T(8,128)(2,1)} custom-call(s32[16]{0:T(128)} %add_minimum_fusion.slot_ref, f32[16,1,256]{2,1,0:T(1,128)} %copy.23.rows_ref, f32[16,1,256]{2,1,0:T(1,128)} %broadcast_in_dim.49.cols_ref, f32[256,256]{1,0:T(8,128)} %fusion.67.inside_ref, bf16[16,256,256]{2,1,0:T(8,128)(2,1)} %bitcast.44, ...), custom_call_target="tpu_custom_call", output_to_operand_aliasing={{}: (5, {})} | custom-call | flops 1073741824 | bytes 8388608 | tf_op jit(solution)/shard_map/pallas_call | solution.py:89
  31.9 5.1 %all-to-all-start = ((bf16[8,1024,256]{2,1,0:T(8,128)(2,1)}), bf16[8,1024,256]{2,1,0:T(8,128)(2,1)}, u32[]{:S(2)}, u32[]{:S(2)}) async-start(bf16[8,1024,256]{2,1,0:T(8,128)(2,1)} %bitcast.39), calls=%async_computation | async-start | bytes 8388608 | tf_op jit(solution)/shard_map/all_to_all | solution.py:177
  42.7 87.6 %all-to-all-done = bf16[8,1024,256]{2,1,0:T(8,128)(2,1)} async-done(((bf16[8,1024,256]{2,1,0:T(8,128)(2,1)}), bf16[8,1024,256]{2,1,0:T(8,128)(2,1)}, u32[]{:S(2)}, u32[]{:S(2)}) %all-to-all-start) | async-done | bytes 4194336 | tf_op jit(solution)/shard_map/all_to_all | solution.py:177
  130.3 4.6 %divide_convert_fusion = bf16[256,256,4]{1,2,0:T(4,128)(2,1)S(1)} fusion(bf16[32,4,1]{0,1,2:T(4,128)(2,1)S(1)} %reshape.127, bf16[32,256,256]{2,1,0:T(8,128)(2,1)} %bitcast.10, f32[4]{0:T(128)S(1)} %broadcast_maximum_fusion), kind=kOutput, calls=%fused_computation.3 | convolution fusion | flops 17301504 | bytes 4718864 | tf_op jit(solution)/shard_map/sc,sij->icj/dot_general | solution.py:194
  135.1 1.9 %collective-permute-start = (bf16[256,4]{1,0:T(8,128)(2,1)S(1)}, bf16[256,4]{1,0:T(8,128)(2,1)S(1)}, u32[]{:S(2)}, u32[]{:S(2)}) collective-permute-start(bf16[256,4]{1,0:T(8,128)(2,1)S(1)} %get-tuple-element.16), channel_id=1, source_target_pairs={{0,1},{1,4},{4,5},{5,8},{8,9},{9,12},{12,13},{2,3},{3,6},{6,7},{7,... | collective-permute-start | bytes 6152 | tf_op jit(solution)/shard_map/ppermute | solution.py:25
  137.0 2.4 %collective-permute-start.1 = (bf16[256,4]{1,0:T(8,128)(2,1)S(1)}, bf16[256,4]{1,0:T(8,128)(2,1)S(1)}, u32[]{:S(2)}, u32[]{:S(2)}) collective-permute-start(bf16[256,4]{1,0:T(8,128)(2,1)S(1)} %get-tuple-element.15), channel_id=1, source_target_pairs={{1,0},{4,1},{5,4},{8,5},{9,8},{12,9},{13,12},{3,2},{6,3},{7,6},{10... | collective-permute-start | bytes 6152 | tf_op jit(solution)/shard_map/ppermute | solution.py:26
  139.4 1.4 broadcast_select_fusion
  140.8 1.8 %collective-permute-done.1 = bf16[256,4]{1,0:T(8,128)(2,1)S(1)} collective-permute-done((bf16[256,4]{1,0:T(8,128)(2,1)S(1)}, bf16[256,4]{1,0:T(8,128)(2,1)S(1)}, u32[]{:S(2)}, u32[]{:S(2)}) %collective-permute-start.1) | collective-permute-done | bytes 2080 | tf_op jit(solution)/shard_map/ppermute | solution.py:26
  143.4 1.3 collective-permute-start.2
  144.6 1.2 broadcast_in_dim_reshape.3
  145.8 5.7 %collective-permute-done.2 = bf16[137,1032]{1,0:T(8,128)(2,1)S(1)} collective-permute-done((bf16[137,1032]{1,0:T(8,128)(2,1)S(1)}, bf16[137,1032]{1,0:T(8,128)(2,1)S(1)}, u32[]{:S(2)}, u32[]{:S(2)}) %collective-permute-start.2) | collective-permute-done | bytes 282800 | tf_op jit(solution)/shard_map/ppermute | solution.py:213
  152.1 0.8 multiply_add_fusion
  152.9 1.2 fusion.13
  154.1 1.3 fusion.24
  (31 shorter events, 5.2 us)
Async XLA Ops:
  3.8 28.1 %all-to-all-start.1 = ((bf16[8,4,4]{1,2,0:T(4,128)(2,1)}), bf16[8,4,4]{1,2,0:T(4,128)(2,1)S(1)}, u32[]{:S(2)}, u32[]{:S(2)}) async-start(bf16[8,4,4]{1,2,0:T(4,128)(2,1)} %copy.24), calls=%async_computation.1 | async-start | bytes 16384 | tf_op jit(solution)/shard_map/all_to_all | solution.py:184
  31.9 98.4 %all-to-all-start = ((bf16[8,1024,256]{2,1,0:T(8,128)(2,1)}), bf16[8,1024,256]{2,1,0:T(8,128)(2,1)}, u32[]{:S(2)}, u32[]{:S(2)}) async-start(bf16[8,1024,256]{2,1,0:T(8,128)(2,1)} %bitcast.39), calls=%async_computation | async-start | bytes 8388608 | tf_op jit(solution)/shard_map/all_to_all | solution.py:177
  135.1 5.7 %collective-permute-start = (bf16[256,4]{1,0:T(8,128)(2,1)S(1)}, bf16[256,4]{1,0:T(8,128)(2,1)S(1)}, u32[]{:S(2)}, u32[]{:S(2)}) collective-permute-start(bf16[256,4]{1,0:T(8,128)(2,1)S(1)} %get-tuple-element.16), channel_id=1, source_target_pairs={{0,1},{1,4},{4,5},{5,8},{8,9},{9,12},{12,13},{2,3},{3,6},{6,7},{7,... | collective-permute-start | bytes 6152 | tf_op jit(solution)/shard_map/ppermute | solution.py:25
  137.0 5.6 %collective-permute-start.1 = (bf16[256,4]{1,0:T(8,128)(2,1)S(1)}, bf16[256,4]{1,0:T(8,128)(2,1)S(1)}, u32[]{:S(2)}, u32[]{:S(2)}) collective-permute-start(bf16[256,4]{1,0:T(8,128)(2,1)S(1)} %get-tuple-element.15), channel_id=1, source_target_pairs={{1,0},{4,1},{5,4},{8,5},{9,8},{12,9},{13,12},{3,2},{6,3},{7,6},{10... | collective-permute-start | bytes 6152 | tf_op jit(solution)/shard_map/ppermute | solution.py:26
  143.4 8.1 %collective-permute-start.2 = (bf16[137,1032]{1,0:T(8,128)(2,1)S(1)}, bf16[137,1032]{1,0:T(8,128)(2,1)S(1)}, u32[]{:S(2)}, u32[]{:S(2)}) collective-permute-start(bf16[137,1032]{1,0:T(8,128)(2,1)S(1)} %fusion.34), channel_id=1, source_target_pairs={{0,2},{2,0},{1,3},{3,1},{4,6},{6,4},{5,7},{7,5},{8,10},{10,8},{9,1... | collective-permute-start | bytes 848312 | tf_op jit(solution)/shard_map/ppermute | solution.py:213

commit v12 on v11

--- a/solution.py
+++ b/solution.py
@@ -62,43 +62,59 @@
     return rows[:, None, :], cols[:, None, :]
 
 
-def warp_kernel(slot_ref, rows_ref, cols_ref, inside_ref, image_ref, blank_ref, out_ref):
+def warp_kernel(slot_ref, rows_ref, cols_ref, inside_ref, image_ref, blank_ref, out_ref, done_ref, sems):
     side = image_ref.shape[-1]
-    row_base = jnp.broadcast_to(rows_ref[0], (side, side))
-    col_base = jnp.broadcast_to(cols_ref[0], (side, side))
+    group = image_ref.shape[0]
+    step = pl.program_id(0)
     inside = inside_ref[...]
-    row_kernel = (pltpu.roll(row_base, 0, 1, stride=1, stride_axis=0) * inside).astype(
-        jnp.bfloat16
-    )
-    col_kernel_t = (pltpu.roll(col_base, 0, 1, stride=1, stride_axis=0) * inside).astype(
-        jnp.bfloat16
-    )
-    section = jnp.dot(row_kernel, image_ref[0], preferred_element_type=jnp.float32)
-    out_ref[0] = jnp.dot(
-        section.astype(jnp.bfloat16), col_kernel_t, preferred_element_type=jnp.float32
-    ).astype(jnp.bfloat16)
+    copies = []
+    for member in range(group):
+        row_base = jnp.broadcast_to(rows_ref[member], (side, side))
+        col_base = jnp.broadcast_to(cols_ref[member], (side, side))
+        row_kernel = (pltpu.roll(row_base, 0, 1, stride=1, stride_axis=0) * inside).astype(
+            jnp.bfloat16
+        )
+        col_kernel_t = (pltpu.roll(col_base, 0, 1, stride=1, stride_axis=0) * inside).astype(
+            jnp.bfloat16
+        )
+        section = jnp.dot(row_kernel, image_ref[member], preferred_element_type=jnp.float32)
+        done_ref[member] = jnp.dot(
+            section.astype(jnp.bfloat16), col_kernel_t, preferred_element_type=jnp.float32
+        ).astype(jnp.bfloat16)
+        copy = pltpu.make_async_copy(
+            done_ref.at[member], out_ref.at[slot_ref[step * group + member]], sems.at[member]
+        )
+        copy.start()
+        copies.append(copy)
+    for copy in copies:
+        copy.wait()
 
 
 def warp_slots(images, values, slot_index, slot_count, interpret=False):
     count, side = images.shape[0], images.shape[-1]
+    group = 2 if count % 2 == 0 else 1
     rows, cols = base_rows(values, side)
     blank = jnp.zeros((slot_count, side, side), jnp.bfloat16)
     position = jnp.arange(side, dtype=jnp.int32)
     inside = (jnp.abs(position[:, None] - position[None, :]) <= PSF_R + 4).astype(jnp.float32)
-    vector_spec = pl.BlockSpec((1, 1, side), lambda b, slots: (b, 0, 0))
+    vector_spec = pl.BlockSpec((group, 1, side), lambda b, slots: (b, 0, 0))
     return pl.pallas_call(
         warp_kernel,
         grid_spec=pltpu.PrefetchScalarGridSpec(
             num_scalar_prefetch=1,
-            grid=(count,),
+            grid=(count // group,),
             in_specs=[
                 vector_spec,
                 vector_spec,
                 pl.BlockSpec((side, side), lambda b, slots: (0, 0)),
-                pl.BlockSpec((1, side, side), lambda b, slots: (b, 0, 0)),
+                pl.BlockSpec((group, side, side), lambda b, slots: (b, 0, 0)),
                 pl.BlockSpec(memory_space=pl.ANY),
             ],
-            out_specs=pl.BlockSpec((1, side, side), lambda b, slots: (slots[b], 0, 0)),
+            out_specs=pl.BlockSpec(memory_space=pl.ANY),
+            scratch_shapes=[
+                pltpu.VMEM((group, side, side), jnp.bfloat16),
+                pltpu.SemaphoreType.DMA((group,)),
+            ],
         ),
         out_shape=jax.ShapeDtypeStruct((slot_count, side, side), jnp.bfloat16),
         input_output_aliases={5: 0},

time: 156 us -> 153 us (0.981)
  Pallas kernels: 13 us -> 10.5 us
    pallas_call x1, Pallas kernels: 13 us -> 10.5 us  [warp_slots(): pl.pallas_call(warp_kernel, grid_spec=pltpu.PrefetchScalarGridSpec(num_sc...]
  transfers between devices with their start and end apart: 5 -> 5, of which waited for: 3 -> 3; matrix products, arithmetic and copies ran while one was open for 8% -> 8% of each run, Pallas kernels for 8% -> 7%
where the time goes in v12:
time: 153 us
  waiting for transfers between devices  95.1 us (62%)
  starting transfers between devices  17.1 us (11%)
  other arithmetic  12.2 us (8%)
  Pallas kernels  10.5 us (7%)
  local copies, waits for them, and re-layouts  7.03 us (5%)
  matrix products  5.55 us (4%)
  between operations  5.51 us (4%)
    all_to_all x1, waiting for transfers between devices, local(): lax.all_to_all(packed.reshape(owners, capacity * side, side), ('sect', 's...  87.6 us
    pallas_call x1, Pallas kernels, warp_slots(): pl.pallas_call(warp_kernel, grid_spec=pltpu.PrefetchScalarGridSpec(num_sc...  10.5 us
    all_to_all x1, starting transfers between devices, local(): lax.all_to_all(packed_weight.reshape(owners, capacity, CELL_DEV), ('sect'...  6.38 us
    ppermute x1, waiting for transfers between devices, local(): lax.ppermute(outgoing, 'band', [(i, (i + shift) % band_count) for i in ra...  5.69 us
    all_to_all x1, starting transfers between devices, local(): lax.all_to_all(packed.reshape(owners, capacity * side, side), ('sect', 's...  5.12 us
    dot_general x1, matrix products, local(): jnp.einsum('sc,sij->icj', received_weight, received, preferred_element_ty...  4.63 us
  transfers between devices with their start and end apart: 5, of which 3 were waited for; matrix products, arithmetic and copies ran while one was open for 8% of the time, Pallas kernels for 7%

profile of v12, /device:TPU:1, one launch (start us, length us, event | category | flops | bytes accessed | tf_op | source)
XLA Modules:
  0.0 153.0 jit_solution(10202720559742661376)
XLA Ops:
  0.6 0.9 convert_reduce_fusion.1
  1.5 0.7 fusion.78
  2.2 0.9 convolution_convert_fusion
  3.8 6.4 %all-to-all-start.1 = ((bf16[8,4,4]{1,2,0:T(4,128)(2,1)}), bf16[8,4,4]{1,2,0:T(4,128)(2,1)S(1)}, u32[]{:S(2)}, u32[]{:S(2)}) async-start(bf16[8,4,4]{1,2,0:T(4,128)(2,1)} %copy.24), calls=%async_computation.1 | async-start | bytes 16384 | tf_op jit(solution)/shard_map/all_to_all | solution.py:200
  10.2 0.7 negate_bitcast_fusion
  10.9 0.7 broadcast_add_fusion
  11.7 0.7 fusion.38
  13.0 1.2 add_minimum_fusion.slot_ref
  14.2 0.7 fusion.67.inside_ref
  16.5 2.4 %broadcast_in_dim.50.blank_ref = bf16[32,256,256]{2,1,0:T(8,128)(2,1)} broadcast(bf16[]{:T(256)} %constant.104.clone.1), dimensions={} | broadcast | bytes 4194306 | tf_op jit(solution)/shard_map/broadcast_in_dim | solution.py:97
  18.9 10.5 %shard_map.86 = bf16[32,256,256]{2,1,0:T(8,128)(2,1)} custom-call(s32[16]{0:T(128)} %add_minimum_fusion.slot_ref, f32[16,1,256]{2,1,0:T(1,128)} %copy.23.rows_ref, f32[16,1,256]{2,1,0:T(1,128)} %broadcast_in_dim.49.cols_ref, f32[256,256]{1,0:T(8,128)} %fusion.67.inside_ref, bf16[16,256,256]{2,1,0:T(8,128)(2,1)} %bitcast.44, ...), custom_call_target="tpu_custom_call", output_to_operand_aliasing={{}: (5, {})} | custom-call | flops 1073741824 | bytes 8388608 | tf_op jit(solution)/shard_map/pallas_call | solution.py:101
  29.5 5.1 %all-to-all-start = ((bf16[8,1024,256]{2,1,0:T(8,128)(2,1)}), bf16[8,1024,256]{2,1,0:T(8,128)(2,1)}, u32[]{:S(2)}, u32[]{:S(2)}) async-start(bf16[8,1024,256]{2,1,0:T(8,128)(2,1)} %bitcast.39), calls=%async_computation | async-start | bytes 8388608 | tf_op jit(solution)/shard_map/all_to_all | solution.py:193
  40.2 87.6 %all-to-all-done = bf16[8,1024,256]{2,1,0:T(8,128)(2,1)} async-done(((bf16[8,1024,256]{2,1,0:T(8,128)(2,1)}), bf16[8,1024,256]{2,1,0:T(8,128)(2,1)}, u32[]{:S(2)}, u32[]{:S(2)}) %all-to-all-start) | async-done | bytes 4194336 | tf_op jit(solution)/shard_map/all_to_all | solution.py:193
  127.8 4.6 %divide_convert_fusion = bf16[256,256,4]{1,2,0:T(4,128)(2,1)S(1)} fusion(bf16[32,4,1]{0,1,2:T(4,128)(2,1)S(1)} %reshape.127, bf16[32,256,256]{2,1,0:T(8,128)(2,1)} %bitcast.10, f32[4]{0:T(128)S(1)} %broadcast_maximum_fusion), kind=kOutput, calls=%fused_computation.3 | convolution fusion | flops 17301504 | bytes 4718864 | tf_op jit(solution)/shard_map/sc,sij->icj/dot_general | solution.py:210
  132.6 1.9 %collective-permute-start = (bf16[256,4]{1,0:T(8,128)(2,1)S(1)}, bf16[256,4]{1,0:T(8,128)(2,1)S(1)}, u32[]{:S(2)}, u32[]{:S(2)}) collective-permute-start(bf16[256,4]{1,0:T(8,128)(2,1)S(1)} %get-tuple-element.16), channel_id=1, source_target_pairs={{0,1},{1,4},{4,5},{5,8},{8,9},{9,12},{12,13},{2,3},{3,6},{6,7},{7,... | collective-permute-start | bytes 6152 | tf_op jit(solution)/shard_map/ppermute | solution.py:25
  134.6 2.4 %collective-permute-start.1 = (bf16[256,4]{1,0:T(8,128)(2,1)S(1)}, bf16[256,4]{1,0:T(8,128)(2,1)S(1)}, u32[]{:S(2)}, u32[]{:S(2)}) collective-permute-start(bf16[256,4]{1,0:T(8,128)(2,1)S(1)} %get-tuple-element.15), channel_id=1, source_target_pairs={{1,0},{4,1},{5,4},{8,5},{9,8},{12,9},{13,12},{3,2},{6,3},{7,6},{10... | collective-permute-start | bytes 6152 | tf_op jit(solution)/shard_map/ppermute | solution.py:26
  137.0 1.4 broadcast_select_fusion
  138.4 1.8 %collective-permute-done.1 = bf16[256,4]{1,0:T(8,128)(2,1)S(1)} collective-permute-done((bf16[256,4]{1,0:T(8,128)(2,1)S(1)}, bf16[256,4]{1,0:T(8,128)(2,1)S(1)}, u32[]{:S(2)}, u32[]{:S(2)}) %collective-permute-start.1) | collective-permute-done | bytes 2080 | tf_op jit(solution)/shard_map/ppermute | solution.py:26
  140.9 1.3 collective-permute-start.2
  142.2 1.2 broadcast_in_dim_reshape.3
  143.3 5.7 %collective-permute-done.2 = bf16[137,1032]{1,0:T(8,128)(2,1)S(1)} collective-permute-done((bf16[137,1032]{1,0:T(8,128)(2,1)S(1)}, bf16[137,1032]{1,0:T(8,128)(2,1)S(1)}, u32[]{:S(2)}, u32[]{:S(2)}) %collective-permute-start.2) | collective-permute-done | bytes 282800 | tf_op jit(solution)/shard_map/ppermute | solution.py:229
  149.6 0.8 multiply_add_fusion
  150.4 1.2 fusion.13
  151.7 1.3 fusion.24
  (31 shorter events, 5.2 us)
Async XLA Ops:
  3.8 25.6 %all-to-all-start.1 = ((bf16[8,4,4]{1,2,0:T(4,128)(2,1)}), bf16[8,4,4]{1,2,0:T(4,128)(2,1)S(1)}, u32[]{:S(2)}, u32[]{:S(2)}) async-start(bf16[8,4,4]{1,2,0:T(4,128)(2,1)} %copy.24), calls=%async_computation.1 | async-start | bytes 16384 | tf_op jit(solution)/shard_map/all_to_all | solution.py:200
  29.5 98.4 %all-to-all-start = ((bf16[8,1024,256]{2,1,0:T(8,128)(2,1)}), bf16[8,1024,256]{2,1,0:T(8,128)(2,1)}, u32[]{:S(2)}, u32[]{:S(2)}) async-start(bf16[8,1024,256]{2,1,0:T(8,128)(2,1)} %bitcast.39), calls=%async_computation | async-start | bytes 8388608 | tf_op jit(solution)/shard_map/all_to_all | solution.py:193
  132.6 5.7 %collective-permute-start = (bf16[256,4]{1,0:T(8,128)(2,1)S(1)}, bf16[256,4]{1,0:T(8,128)(2,1)S(1)}, u32[]{:S(2)}, u32[]{:S(2)}) collective-permute-start(bf16[256,4]{1,0:T(8,128)(2,1)S(1)} %get-tuple-element.16), channel_id=1, source_target_pairs={{0,1},{1,4},{4,5},{5,8},{8,9},{9,12},{12,13},{2,3},{3,6},{6,7},{7,... | collective-permute-start | bytes 6152 | tf_op jit(solution)/shard_map/ppermute | solution.py:25
  134.6 5.6 %collective-permute-start.1 = (bf16[256,4]{1,0:T(8,128)(2,1)S(1)}, bf16[256,4]{1,0:T(8,128)(2,1)S(1)}, u32[]{:S(2)}, u32[]{:S(2)}) collective-permute-start(bf16[256,4]{1,0:T(8,128)(2,1)S(1)} %get-tuple-element.15), channel_id=1, source_target_pairs={{1,0},{4,1},{5,4},{8,5},{9,8},{12,9},{13,12},{3,2},{6,3},{7,6},{10... | collective-permute-start | bytes 6152 | tf_op jit(solution)/shard_map/ppermute | solution.py:26
  140.9 8.1 %collective-permute-start.2 = (bf16[137,1032]{1,0:T(8,128)(2,1)S(1)}, bf16[137,1032]{1,0:T(8,128)(2,1)S(1)}, u32[]{:S(2)}, u32[]{:S(2)}) collective-permute-start(bf16[137,1032]{1,0:T(8,128)(2,1)S(1)} %fusion.34), channel_id=1, source_target_pairs={{0,2},{2,0},{1,3},{3,1},{4,6},{6,4},{5,7},{7,5},{8,10},{10,8},{9,1... | collective-permute-start | bytes 848312 | tf_op jit(solution)/shard_map/ppermute | solution.py:229

commit v13 on v12

--- a/solution.py
+++ b/solution.py
@@ -81,20 +81,26 @@
         done_ref[member] = jnp.dot(
             section.astype(jnp.bfloat16), col_kernel_t, preferred_element_type=jnp.float32
         ).astype(jnp.bfloat16)
-        copy = pltpu.make_async_copy(
-            done_ref.at[member], out_ref.at[slot_ref[step * group + member]], sems.at[member]
-        )
+        slot = slot_ref[step * group + member]
+        capacity = (out_ref.shape[1] - 16) // side
+        target = out_ref.at[slot // capacity, pl.ds((slot % capacity) * side, side), :]
+        copy = pltpu.make_async_copy(done_ref.at[member], target, sems.at[member])
         copy.start()
         copies.append(copy)
     for copy in copies:
         copy.wait()
 
 
-def warp_slots(images, values, slot_index, slot_count, interpret=False):
+def warp_slots(images, values, slot_index, slot_weight, interpret=False):
     count, side = images.shape[0], images.shape[-1]
+    owners, capacity, cell_count = slot_weight.shape
     group = 2 if count % 2 == 0 else 1
     rows, cols = base_rows(values, side)
-    blank = jnp.zeros((slot_count, side, side), jnp.bfloat16)
+    blank = (
+        jnp.zeros((owners, capacity * side + 16, side), jnp.bfloat16)
+        .at[:, capacity * side, : capacity * cell_count]
+        .set(slot_weight.reshape(owners, capacity * cell_count))
+    )
     position = jnp.arange(side, dtype=jnp.int32)
     inside = (jnp.abs(position[:, None] - position[None, :]) <= PSF_R + 4).astype(jnp.float32)
     vector_spec = pl.BlockSpec((group, 1, side), lambda b, slots: (b, 0, 0))
@@ -116,12 +122,12 @@
                 pltpu.SemaphoreType.DMA((group,)),
             ],
         ),
-        out_shape=jax.ShapeDtypeStruct((slot_count, side, side), jnp.bfloat16),
+        out_shape=jax.ShapeDtypeStruct(blank.shape, jnp.bfloat16),
         input_output_aliases={5: 0},
         cost_estimate=pl.CostEstimate(
             flops=4 * count * side**3,
             transcendentals=0,
-            bytes_accessed=2 * (2 * count + slot_count) * side * side,
+            bytes_accessed=2 * (2 * count * side * side + blank.size),
         ),
         interpret=interpret,
     )(slot_index, rows, cols, inside, images, blank)
@@ -178,9 +184,6 @@
     matching = jnp.arange(slot_count, dtype=jnp.int32)[:, None] == slot_index[None, :]
     source = jnp.sum(jnp.where(matching, block_order[None, :], 0), axis=1)
     placing = matching.astype(jnp.bfloat16)
-    packed = warp_slots(
-        images[0], values, jnp.minimum(slot_index, slot_count - 1).astype(jnp.int32), slot_count
-    )
     cell_weight = jnp.where(
         cells[0][:, None] == jnp.arange(CELL_DEV, dtype=jnp.int32)[None, :],
         weights[0][:, None],
@@ -189,24 +192,17 @@
     packed_weight = jnp.dot(placing, cell_weight, preferred_element_type=jnp.float32).astype(
         jnp.bfloat16
     )
-    received, received_weight = (
-        lax.all_to_all(
-            packed.reshape(owners, capacity * side, side),
-            ("sect", "sub"),
-            split_axis=0,
-            concat_axis=0,
-            tiled=True,
-        ),
-        lax.all_to_all(
-            packed_weight.reshape(owners, capacity, CELL_DEV),
-            ("sect", "sub"),
-            split_axis=0,
-            concat_axis=0,
-            tiled=True,
-        ),
-    )
-    received = received.reshape(slot_count, side, side)
-    received_weight = received_weight.reshape(slot_count, CELL_DEV)
+    packed = warp_slots(
+        images[0],
+        values,
+        jnp.minimum(slot_index, slot_count - 1).astype(jnp.int32),
+        packed_weight.reshape(owners, capacity, CELL_DEV),
+    )
+    received = lax.all_to_all(packed, ("sect", "sub"), split_axis=0, concat_axis=0, tiled=True)
+    received_weight = received[:, capacity * side, : capacity * CELL_DEV].reshape(
+        slot_count, CELL_DEV
+    )
+    received = received[:, : capacity * side].reshape(slot_count, side, side)
     numerator = jnp.einsum(
         "sc,sij->icj", received_weight, received, preferred_element_type=jnp.float32
     )

time: 153 us -> 150 us (0.980)
  starting transfers between devices: 17.1 us -> 12 us
  local copies, waits for them, and re-layouts: 7.03 us -> 9.57 us
  matrix products: 5.55 us -> 3.36 us
  waiting for transfers between devices: 95.1 us -> 96.7 us
    all_to_all x2 -> x1, starting transfers between devices: 11.5 us -> 6.4 us  [local(): lax.all_to_all(packed, ('sect', 'sub'), split_axis=0, concat_axis=0, tile...]
    slice x0 -> x2, local copies, waits for them, and re-layouts: none -> 3.2 us  [the longest x1 2.46 us: local(): received = received[:, :capacity * side].reshape(slot_count, side, side)]
    broadcast_in_dim x1 -> x0, local copies, waits for them, and re-layouts: 2.44 us -> none  [warp_slots(): blank = jnp.zeros((slot_count, side, side), jnp.bfloat16)]
    scatter x0 -> x1, local copies, waits for them, and re-layouts: none -> 2.29 us  [warp_slots(): blank = jnp.zeros((owners, capacity * side + 16, side), jnp.bfloat16).at[...]
    dot_general x1, matrix products: 4.63 us -> 2.44 us  [local(): jnp.einsum('sc,sij->icj', received_weight, received, preferred_element_ty...]
    all_to_all x2 -> x1, waiting for transfers between devices: 87.6 us -> 89.2 us  [local(): lax.all_to_all(packed, ('sect', 'sub'), split_axis=0, concat_axis=0, tile...]
  transfers between devices with their start and end apart: 5 -> 4, of which waited for: 3 -> 3; matrix products, arithmetic and copies ran while one was open for 8% -> 2% of each run, Pallas kernels for 7% -> 0%
where the time goes in v13:
time: 150 us
  waiting for transfers between devices  96.7 us (64%)
  other arithmetic  12 us (8%)
  starting transfers between devices  12 us (8%)
  Pallas kernels  10.5 us (7%)
  local copies, waits for them, and re-layouts  9.57 us (6%)
  between operations  5.51 us (4%)
  matrix products  3.36 us (2%)
    all_to_all x1, waiting for transfers between devices, local(): lax.all_to_all(packed, ('sect', 'sub'), split_axis=0, concat_axis=0, tile...  89.2 us
    pallas_call x1, Pallas kernels, warp_slots(): pl.pallas_call(warp_kernel, grid_spec=pltpu.PrefetchScalarGridSpec(num_sc...  10.5 us
    all_to_all x1, starting transfers between devices, local(): lax.all_to_all(packed, ('sect', 'sub'), split_axis=0, concat_axis=0, tile...  6.4 us
    ppermute x1, waiting for transfers between devices, local(): lax.ppermute(outgoing, 'band', [(i, (i + shift) % band_count) for i in ra...  5.67 us
  transfers between devices with their start and end apart: 4, of which 3 were waited for; matrix products, arithmetic and copies ran while one was open for 2% of the time, Pallas kernels for 0%

profile of v13, /device:TPU:1, one launch (start us, length us, event | category | flops | bytes accessed | tf_op | source)
XLA Modules:
  0.0 149.7 jit_solution(8654777935351573906)
XLA Ops:
  0.7 0.7 negate_bitcast_fusion
  1.4 0.7 broadcast_add_fusion
  2.1 0.7 fusion.38
  3.4 0.9 convert_reduce_fusion.1
  5.0 1.2 add_minimum_fusion.slot_ref
  6.2 0.7 fusion.67.inside_ref
  8.5 0.9 convolution_convert_fusion
  9.6 2.3 %scatter.6.blank_ref = bf16[8,1040,256]{2,1,0:T(8,128)(2,1)} pad(bf16[8,1,16]{2,1,0:T(2,128)(2,1)S(1)} %reshape.157, bf16[]{:T(256)} %constant.134.clone.1), padding=0_0x1024_15x0_240 | pad | bytes 4260098 | tf_op jit(solution)/shard_map/scatter | solution.py:102
  11.9 10.5 %shard_map.86 = bf16[8,1040,256]{2,1,0:T(8,128)(2,1)} custom-call(s32[16]{0:T(128)} %add_minimum_fusion.slot_ref, f32[16,1,256]{2,1,0:T(1,128)} %copy.26.rows_ref, f32[16,1,256]{2,1,0:T(1,128)} %broadcast_in_dim.47.cols_ref, f32[256,256]{1,0:T(8,128)} %fusion.67.inside_ref, bf16[16,256,256]{2,1,0:T(8,128)(2,1)} %bitcast.41, ...), custom_call_target="tpu_custom_call", output_to_operand_aliasing={{}: (5, {})} | custom-call | flops 1073741824 | bytes 8454144 | tf_op jit(solution)/shard_map/pallas_call | solution.py:107
  22.4 6.4 %all-to-all-start = ((bf16[8,1040,256]{2,1,0:T(8,128)(2,1)}), bf16[8,1040,256]{2,1,0:T(8,128)(2,1)}, u32[]{:S(2)}, u32[]{:S(2)}) async-start(bf16[8,1040,256]{2,1,0:T(8,128)(2,1)} %shard_map.86), calls=%async_computation | async-start | bytes 8519680 | tf_op jit(solution)/shard_map/all_to_all | solution.py:201
  34.2 89.2 %all-to-all-done = bf16[8,1040,256]{2,1,0:T(8,128)(2,1)} async-done(((bf16[8,1040,256]{2,1,0:T(8,128)(2,1)}), bf16[8,1040,256]{2,1,0:T(8,128)(2,1)}, u32[]{:S(2)}, u32[]{:S(2)}) %all-to-all-start) | async-done | bytes 4259872 | tf_op jit(solution)/shard_map/all_to_all | solution.py:201
  123.5 0.7 slice_reduce_fusion.1
  124.3 2.5 %slice.167 = bf16[8,1024,256]{2,1,0:T(8,128)(2,1)S(1)} slice(bf16[8,1040,256]{2,1,0:T(8,128)(2,1)} %all-to-all-done), slice={[0:8], [0:1024], [0:256]} | slice | bytes 8388608 | tf_op jit(solution)/shard_map/slice | solution.py:205
  126.8 2.4 %divide_convert_fusion = bf16[256,256,4]{1,2,0:T(4,128)(2,1)S(1)} fusion(bf16[32,256,256]{2,1,0:T(8,128)(2,1)S(1)} %bitcast.36, f32[4]{0:T(128)S(1)} %broadcast_maximum_fusion, bf16[32,4]{1,0:T(8,128)(2,1)S(1)} %reshape_squeeze.3), kind=kOutput, calls=%fused_computation.3 | convolution fusion | flops 17301504 | bytes 4718864 | tf_op jit(solution)/shard_map/sc,sij->icj/dot_general | solution.py:206
  129.4 1.9 %collective-permute-start = (bf16[256,4]{1,0:T(8,128)(2,1)S(1)}, bf16[256,4]{1,0:T(8,128)(2,1)S(1)}, u32[]{:S(2)}, u32[]{:S(2)}) collective-permute-start(bf16[256,4]{1,0:T(8,128)(2,1)S(1)} %get-tuple-element.28), channel_id=1, source_target_pairs={{0,1},{1,4},{4,5},{5,8},{8,9},{9,12},{12,13},{2,3},{3,6},{6,7},{7,... | collective-permute-start | bytes 6152 | tf_op jit(solution)/shard_map/ppermute | solution.py:25
  131.4 2.4 %collective-permute-start.1 = (bf16[256,4]{1,0:T(8,128)(2,1)S(1)}, bf16[256,4]{1,0:T(8,128)(2,1)S(1)}, u32[]{:S(2)}, u32[]{:S(2)}) collective-permute-start(bf16[256,4]{1,0:T(8,128)(2,1)S(1)} %get-tuple-element.27), channel_id=1, source_target_pairs={{1,0},{4,1},{5,4},{8,5},{9,8},{12,9},{13,12},{3,2},{6,3},{7,6},{10... | collective-permute-start | bytes 6152 | tf_op jit(solution)/shard_map/ppermute | solution.py:26
  133.8 1.4 broadcast_select_fusion
  135.1 1.8 %collective-permute-done.1 = bf16[256,4]{1,0:T(8,128)(2,1)S(1)} collective-permute-done((bf16[256,4]{1,0:T(8,128)(2,1)S(1)}, bf16[256,4]{1,0:T(8,128)(2,1)S(1)}, u32[]{:S(2)}, u32[]{:S(2)}) %collective-permute-start.1) | collective-permute-done | bytes 2080 | tf_op jit(solution)/shard_map/ppermute | solution.py:26
  137.7 1.3 collective-permute-start.2
  139.0 1.2 broadcast_in_dim_reshape.3
  140.1 5.7 %collective-permute-done.2 = bf16[137,1032]{1,0:T(8,128)(2,1)S(1)} collective-permute-done((bf16[137,1032]{1,0:T(8,128)(2,1)S(1)}, bf16[137,1032]{1,0:T(8,128)(2,1)S(1)}, u32[]{:S(2)}, u32[]{:S(2)}) %collective-permute-start.2) | collective-permute-done | bytes 282800 | tf_op jit(solution)/shard_map/ppermute | solution.py:225
  146.4 0.8 multiply_add_fusion
  147.2 1.2 fusion.13
  148.4 1.3 fusion.24
  (30 shorter events, 5.3 us)
Async XLA Ops:
  22.4 101.1 %all-to-all-start = ((bf16[8,1040,256]{2,1,0:T(8,128)(2,1)}), bf16[8,1040,256]{2,1,0:T(8,128)(2,1)}, u32[]{:S(2)}, u32[]{:S(2)}) async-start(bf16[8,1040,256]{2,1,0:T(8,128)(2,1)} %shard_map.86), calls=%async_computation | async-start | bytes 8519680 | tf_op jit(solution)/shard_map/all_to_all | solution.py:201
  129.4 5.7 %collective-permute-start = (bf16[256,4]{1,0:T(8,128)(2,1)S(1)}, bf16[256,4]{1,0:T(8,128)(2,1)S(1)}, u32[]{:S(2)}, u32[]{:S(2)}) collective-permute-start(bf16[256,4]{1,0:T(8,128)(2,1)S(1)} %get-tuple-element.28), channel_id=1, source_target_pairs={{0,1},{1,4},{4,5},{5,8},{8,9},{9,12},{12,13},{2,3},{3,6},{6,7},{7,... | collective-permute-start | bytes 6152 | tf_op jit(solution)/shard_map/ppermute | solution.py:25
  131.4 5.6 %collective-permute-start.1 = (bf16[256,4]{1,0:T(8,128)(2,1)S(1)}, bf16[256,4]{1,0:T(8,128)(2,1)S(1)}, u32[]{:S(2)}, u32[]{:S(2)}) collective-permute-start(bf16[256,4]{1,0:T(8,128)(2,1)S(1)} %get-tuple-element.27), channel_id=1, source_target_pairs={{1,0},{4,1},{5,4},{8,5},{9,8},{12,9},{13,12},{3,2},{6,3},{7,6},{10... | collective-permute-start | bytes 6152 | tf_op jit(solution)/shard_map/ppermute | solution.py:26
  137.7 8.1 %collective-permute-start.2 = (bf16[137,1032]{1,0:T(8,128)(2,1)S(1)}, bf16[137,1032]{1,0:T(8,128)(2,1)S(1)}, u32[]{:S(2)}, u32[]{:S(2)}) collective-permute-start(bf16[137,1032]{1,0:T(8,128)(2,1)S(1)} %fusion.34), channel_id=1, source_target_pairs={{0,2},{2,0},{1,3},{3,1},{4,6},{6,4},{5,7},{7,5},{8,10},{10,8},{9,1... | collective-permute-start | bytes 848312 | tf_op jit(solution)/shard_map/ppermute | solution.py:225

commit v14 on v13

--- a/solution.py
+++ b/solution.py
@@ -94,7 +94,7 @@
 def warp_slots(images, values, slot_index, slot_weight, interpret=False):
     count, side = images.shape[0], images.shape[-1]
     owners, capacity, cell_count = slot_weight.shape
-    group = 2 if count % 2 == 0 else 1
+    group = 4 if count % 4 == 0 else 1
     rows, cols = base_rows(values, side)
     blank = (
         jnp.zeros((owners, capacity * side + 16, side), jnp.bfloat16)

time: 150 us -> 146 us (0.973)
  Pallas kernels: 10.5 us -> 6.84 us
    pallas_call x1, Pallas kernels: 10.5 us -> 6.84 us  [warp_slots(): pl.pallas_call(warp_kernel, grid_spec=pltpu.PrefetchScalarGridSpec(num_sc...]
where the time goes in v14:
time: 146 us
  waiting for transfers between devices  96.7 us (66%)
  other arithmetic  12 us (8%)
  starting transfers between devices  11.9 us (8%)
  local copies, waits for them, and re-layouts  9.57 us (7%)
  Pallas kernels  6.84 us (5%)
  between operations  5.51 us (4%)
  matrix products  3.36 us (2%)
    all_to_all x1, waiting for transfers between devices, local(): lax.all_to_all(packed, ('sect', 'sub'), split_axis=0, concat_axis=0, tile...  89.2 us
    pallas_call x1, Pallas kernels, warp_slots(): pl.pallas_call(warp_kernel, grid_spec=pltpu.PrefetchScalarGridSpec(num_sc...  6.84 us
    all_to_all x1, starting transfers between devices, local(): lax.all_to_all(packed, ('sect', 'sub'), split_axis=0, concat_axis=0, tile...  6.36 us
    ppermute x1, waiting for transfers between devices, local(): lax.ppermute(outgoing, 'band', [(i, (i + shift) % band_count) for i in ra...  5.69 us
  transfers between devices with their start and end apart: 4, of which 3 were waited for; matrix products, arithmetic and copies ran while one was open for 2% of the time, Pallas kernels for 0%

profile of v14, /device:TPU:1, one launch (start us, length us, event | category | flops | bytes accessed | tf_op | source)
XLA Modules:
  0.0 146.0 jit_solution(17123397822936119210)
XLA Ops:
  0.7 0.7 negate_bitcast_fusion
  1.4 0.7 broadcast_add_fusion
  2.1 0.7 fusion.38
  3.4 0.9 convert_reduce_fusion.1
  5.0 1.2 add_minimum_fusion.slot_ref
  6.2 0.7 fusion.67.inside_ref
  8.5 0.9 convolution_convert_fusion
  9.6 2.3 %scatter.6.blank_ref = bf16[8,1040,256]{2,1,0:T(8,128)(2,1)} pad(bf16[8,1,16]{2,1,0:T(2,128)(2,1)S(1)} %reshape.157, bf16[]{:T(256)} %constant.134.clone.1), padding=0_0x1024_15x0_240 | pad | bytes 4260098 | tf_op jit(solution)/shard_map/scatter | solution.py:102
  11.9 6.8 %shard_map.86 = bf16[8,1040,256]{2,1,0:T(8,128)(2,1)} custom-call(s32[16]{0:T(128)} %add_minimum_fusion.slot_ref, f32[16,1,256]{2,1,0:T(1,128)} %copy.26.rows_ref, f32[16,1,256]{2,1,0:T(1,128)} %broadcast_in_dim.47.cols_ref, f32[256,256]{1,0:T(8,128)} %fusion.67.inside_ref, bf16[16,256,256]{2,1,0:T(8,128)(2,1)} %bitcast.41, ...), custom_call_target="tpu_custom_call", output_to_operand_aliasing={{}: (5, {})} | custom-call | flops 1073741824 | bytes 8454144 | tf_op jit(solution)/shard_map/pallas_call | solution.py:107
  18.7 6.4 %all-to-all-start = ((bf16[8,1040,256]{2,1,0:T(8,128)(2,1)}), bf16[8,1040,256]{2,1,0:T(8,128)(2,1)}, u32[]{:S(2)}, u32[]{:S(2)}) async-start(bf16[8,1040,256]{2,1,0:T(8,128)(2,1)} %shard_map.86), calls=%async_computation | async-start | bytes 8519680 | tf_op jit(solution)/shard_map/all_to_all | solution.py:201
  30.5 89.2 %all-to-all-done = bf16[8,1040,256]{2,1,0:T(8,128)(2,1)} async-done(((bf16[8,1040,256]{2,1,0:T(8,128)(2,1)}), bf16[8,1040,256]{2,1,0:T(8,128)(2,1)}, u32[]{:S(2)}, u32[]{:S(2)}) %all-to-all-start) | async-done | bytes 4259872 | tf_op jit(solution)/shard_map/all_to_all | solution.py:201
  119.7 0.7 slice_reduce_fusion.1
  120.6 2.5 %slice.167 = bf16[8,1024,256]{2,1,0:T(8,128)(2,1)S(1)} slice(bf16[8,1040,256]{2,1,0:T(8,128)(2,1)} %all-to-all-done), slice={[0:8], [0:1024], [0:256]} | slice | bytes 8388608 | tf_op jit(solution)/shard_map/slice | solution.py:205
  123.0 2.4 %divide_convert_fusion = bf16[256,256,4]{1,2,0:T(4,128)(2,1)S(1)} fusion(bf16[32,256,256]{2,1,0:T(8,128)(2,1)S(1)} %bitcast.36, f32[4]{0:T(128)S(1)} %broadcast_maximum_fusion, bf16[32,4]{1,0:T(8,128)(2,1)S(1)} %reshape_squeeze.3), kind=kOutput, calls=%fused_computation.3 | convolution fusion | flops 17301504 | bytes 4718864 | tf_op jit(solution)/shard_map/sc,sij->icj/dot_general | solution.py:206
  125.7 1.9 %collective-permute-start = (bf16[256,4]{1,0:T(8,128)(2,1)S(1)}, bf16[256,4]{1,0:T(8,128)(2,1)S(1)}, u32[]{:S(2)}, u32[]{:S(2)}) collective-permute-start(bf16[256,4]{1,0:T(8,128)(2,1)S(1)} %get-tuple-element.28), channel_id=1, source_target_pairs={{0,1},{1,4},{4,5},{5,8},{8,9},{9,12},{12,13},{2,3},{3,6},{6,7},{7,... | collective-permute-start | bytes 6152 | tf_op jit(solution)/shard_map/ppermute | solution.py:25
  127.6 2.4 %collective-permute-start.1 = (bf16[256,4]{1,0:T(8,128)(2,1)S(1)}, bf16[256,4]{1,0:T(8,128)(2,1)S(1)}, u32[]{:S(2)}, u32[]{:S(2)}) collective-permute-start(bf16[256,4]{1,0:T(8,128)(2,1)S(1)} %get-tuple-element.27), channel_id=1, source_target_pairs={{1,0},{4,1},{5,4},{8,5},{9,8},{12,9},{13,12},{3,2},{6,3},{7,6},{10... | collective-permute-start | bytes 6152 | tf_op jit(solution)/shard_map/ppermute | solution.py:26
  130.0 1.4 broadcast_select_fusion
  131.4 1.8 %collective-permute-done.1 = bf16[256,4]{1,0:T(8,128)(2,1)S(1)} collective-permute-done((bf16[256,4]{1,0:T(8,128)(2,1)S(1)}, bf16[256,4]{1,0:T(8,128)(2,1)S(1)}, u32[]{:S(2)}, u32[]{:S(2)}) %collective-permute-start.1) | collective-permute-done | bytes 2080 | tf_op jit(solution)/shard_map/ppermute | solution.py:26
  133.9 1.3 collective-permute-start.2
  135.2 1.2 broadcast_in_dim_reshape.3
  136.4 5.7 %collective-permute-done.2 = bf16[137,1032]{1,0:T(8,128)(2,1)S(1)} collective-permute-done((bf16[137,1032]{1,0:T(8,128)(2,1)S(1)}, bf16[137,1032]{1,0:T(8,128)(2,1)S(1)}, u32[]{:S(2)}, u32[]{:S(2)}) %collective-permute-start.2) | collective-permute-done | bytes 282800 | tf_op jit(solution)/shard_map/ppermute | solution.py:225
  142.7 0.8 multiply_add_fusion
  143.5 1.2 fusion.13
  144.7 1.3 fusion.24
  (30 shorter events, 5.3 us)
Async XLA Ops:
  18.7 101.0 %all-to-all-start = ((bf16[8,1040,256]{2,1,0:T(8,128)(2,1)}), bf16[8,1040,256]{2,1,0:T(8,128)(2,1)}, u32[]{:S(2)}, u32[]{:S(2)}) async-start(bf16[8,1040,256]{2,1,0:T(8,128)(2,1)} %shard_map.86), calls=%async_computation | async-start | bytes 8519680 | tf_op jit(solution)/shard_map/all_to_all | solution.py:201
  125.7 5.7 %collective-permute-start = (bf16[256,4]{1,0:T(8,128)(2,1)S(1)}, bf16[256,4]{1,0:T(8,128)(2,1)S(1)}, u32[]{:S(2)}, u32[]{:S(2)}) collective-permute-start(bf16[256,4]{1,0:T(8,128)(2,1)S(1)} %get-tuple-element.28), channel_id=1, source_target_pairs={{0,1},{1,4},{4,5},{5,8},{8,9},{9,12},{12,13},{2,3},{3,6},{6,7},{7,... | collective-permute-start | bytes 6152 | tf_op jit(solution)/shard_map/ppermute | solution.py:25
  127.6 5.6 %collective-permute-start.1 = (bf16[256,4]{1,0:T(8,128)(2,1)S(1)}, bf16[256,4]{1,0:T(8,128)(2,1)S(1)}, u32[]{:S(2)}, u32[]{:S(2)}) collective-permute-start(bf16[256,4]{1,0:T(8,128)(2,1)S(1)} %get-tuple-element.27), channel_id=1, source_target_pairs={{1,0},{4,1},{5,4},{8,5},{9,8},{12,9},{13,12},{3,2},{6,3},{7,6},{10... | collective-permute-start | bytes 6152 | tf_op jit(solution)/shard_map/ppermute | solution.py:26
  133.9 8.1 %collective-permute-start.2 = (bf16[137,1032]{1,0:T(8,128)(2,1)S(1)}, bf16[137,1032]{1,0:T(8,128)(2,1)S(1)}, u32[]{:S(2)}, u32[]{:S(2)}) collective-permute-start(bf16[137,1032]{1,0:T(8,128)(2,1)S(1)} %fusion.34), channel_id=1, source_target_pairs={{0,2},{2,0},{1,3},{3,1},{4,6},{6,4},{5,7},{7,5},{8,10},{10,8},{9,1... | collective-permute-start | bytes 848312 | tf_op jit(solution)/shard_map/ppermute | solution.py:225

commit v15 on v14

--- a/solution.py
+++ b/solution.py
@@ -94,7 +94,7 @@
 def warp_slots(images, values, slot_index, slot_weight, interpret=False):
     count, side = images.shape[0], images.shape[-1]
     owners, capacity, cell_count = slot_weight.shape
-    group = 4 if count % 4 == 0 else 1
+    group = next(size for size in (8, 4, 2, 1) if count % size == 0)
     rows, cols = base_rows(values, side)
     blank = (
         jnp.zeros((owners, capacity * side + 16, side), jnp.bfloat16)

time: 146 us -> 145 us (level)
  Pallas kernels: 6.84 us -> 5.09 us
    pallas_call x1, Pallas kernels: 6.84 us -> 5.09 us  [warp_slots(): pl.pallas_call(warp_kernel, grid_spec=pltpu.PrefetchScalarGridSpec(num_sc...]
where the time goes in v15:
time: 145 us; the launch traced here: 144 us
  waiting for transfers between devices  96.7 us (67%)
  other arithmetic  12 us (8%)
  starting transfers between devices  12 us (8%)
  local copies, waits for them, and re-layouts  9.57 us (7%)
  between operations  5.51 us (4%)
  Pallas kernels  5.09 us (4%)
  matrix products  3.36 us (2%)
    all_to_all x1, waiting for transfers between devices, local(): lax.all_to_all(packed, ('sect', 'sub'), split_axis=0, concat_axis=0, tile...  89.2 us
    all_to_all x1, starting transfers between devices, local(): lax.all_to_all(packed, ('sect', 'sub'), split_axis=0, concat_axis=0, tile...  6.39 us
    ppermute x1, waiting for transfers between devices, local(): lax.ppermute(outgoing, 'band', [(i, (i + shift) % band_count) for i in ra...  5.67 us
    pallas_call x1, Pallas kernels, warp_slots(): pl.pallas_call(warp_kernel, grid_spec=pltpu.PrefetchScalarGridSpec(num_sc...  5.09 us
  transfers between devices with their start and end apart: 4, of which 3 were waited for; matrix products, arithmetic and copies ran while one was open for 2% of the time, Pallas kernels for 0%

profile of v15, /device:TPU:1, one launch (start us, length us, event | category | flops | bytes accessed | tf_op | source)
XLA Modules:
  0.0 144.3 jit_solution(10638264528803229226)
XLA Ops:
  0.7 0.7 negate_bitcast_fusion
  1.4 0.7 broadcast_add_fusion
  2.1 0.7 fusion.38
  3.4 0.9 convert_reduce_fusion.1
  5.0 1.2 add_minimum_fusion.slot_ref
  6.2 0.7 fusion.67.inside_ref
  8.5 0.9 convolution_convert_fusion
  9.6 2.3 %scatter.6.blank_ref = bf16[8,1040,256]{2,1,0:T(8,128)(2,1)} pad(bf16[8,1,16]{2,1,0:T(2,128)(2,1)S(1)} %reshape.157, bf16[]{:T(256)} %constant.134.clone.1), padding=0_0x1024_15x0_240 | pad | bytes 4260098 | tf_op jit(solution)/shard_map/scatter | solution.py:102
  11.9 5.1 %shard_map.86 = bf16[8,1040,256]{2,1,0:T(8,128)(2,1)} custom-call(s32[16]{0:T(128)} %add_minimum_fusion.slot_ref, f32[16,1,256]{2,1,0:T(1,128)} %copy.26.rows_ref, f32[16,1,256]{2,1,0:T(1,128)} %broadcast_in_dim.47.cols_ref, f32[256,256]{1,0:T(8,128)} %fusion.67.inside_ref, bf16[16,256,256]{2,1,0:T(8,128)(2,1)} %bitcast.41, ...), custom_call_target="tpu_custom_call", output_to_operand_aliasing={{}: (5, {})} | custom-call | flops 1073741824 | bytes 8454144 | tf_op jit(solution)/shard_map/pallas_call | solution.py:107
  17.0 6.4 %all-to-all-start = ((bf16[8,1040,256]{2,1,0:T(8,128)(2,1)}), bf16[8,1040,256]{2,1,0:T(8,128)(2,1)}, u32[]{:S(2)}, u32[]{:S(2)}) async-start(bf16[8,1040,256]{2,1,0:T(8,128)(2,1)} %shard_map.86), calls=%async_computation | async-start | bytes 8519680 | tf_op jit(solution)/shard_map/all_to_all | solution.py:201
  28.8 89.2 %all-to-all-done = bf16[8,1040,256]{2,1,0:T(8,128)(2,1)} async-done(((bf16[8,1040,256]{2,1,0:T(8,128)(2,1)}), bf16[8,1040,256]{2,1,0:T(8,128)(2,1)}, u32[]{:S(2)}, u32[]{:S(2)}) %all-to-all-start) | async-done | bytes 4259872 | tf_op jit(solution)/shard_map/all_to_all | solution.py:201
  118.0 0.7 slice_reduce_fusion.1
  118.9 2.5 %slice.167 = bf16[8,1024,256]{2,1,0:T(8,128)(2,1)S(1)} slice(bf16[8,1040,256]{2,1,0:T(8,128)(2,1)} %all-to-all-done), slice={[0:8], [0:1024], [0:256]} | slice | bytes 8388608 | tf_op jit(solution)/shard_map/slice | solution.py:205
  121.3 2.4 %divide_convert_fusion = bf16[256,256,4]{1,2,0:T(4,128)(2,1)S(1)} fusion(bf16[32,256,256]{2,1,0:T(8,128)(2,1)S(1)} %bitcast.36, f32[4]{0:T(128)S(1)} %broadcast_maximum_fusion, bf16[32,4]{1,0:T(8,128)(2,1)S(1)} %reshape_squeeze.3), kind=kOutput, calls=%fused_computation.3 | convolution fusion | flops 17301504 | bytes 4718864 | tf_op jit(solution)/shard_map/sc,sij->icj/dot_general | solution.py:206
  124.0 1.9 %collective-permute-start = (bf16[256,4]{1,0:T(8,128)(2,1)S(1)}, bf16[256,4]{1,0:T(8,128)(2,1)S(1)}, u32[]{:S(2)}, u32[]{:S(2)}) collective-permute-start(bf16[256,4]{1,0:T(8,128)(2,1)S(1)} %get-tuple-element.28), channel_id=1, source_target_pairs={{0,1},{1,4},{4,5},{5,8},{8,9},{9,12},{12,13},{2,3},{3,6},{6,7},{7,... | collective-permute-start | bytes 6152 | tf_op jit(solution)/shard_map/ppermute | solution.py:25
  125.9 2.4 %collective-permute-start.1 = (bf16[256,4]{1,0:T(8,128)(2,1)S(1)}, bf16[256,4]{1,0:T(8,128)(2,1)S(1)}, u32[]{:S(2)}, u32[]{:S(2)}) collective-permute-start(bf16[256,4]{1,0:T(8,128)(2,1)S(1)} %get-tuple-element.27), channel_id=1, source_target_pairs={{1,0},{4,1},{5,4},{8,5},{9,8},{12,9},{13,12},{3,2},{6,3},{7,6},{10... | collective-permute-start | bytes 6152 | tf_op jit(solution)/shard_map/ppermute | solution.py:26
  128.3 1.4 broadcast_select_fusion
  129.7 1.8 %collective-permute-done.1 = bf16[256,4]{1,0:T(8,128)(2,1)S(1)} collective-permute-done((bf16[256,4]{1,0:T(8,128)(2,1)S(1)}, bf16[256,4]{1,0:T(8,128)(2,1)S(1)}, u32[]{:S(2)}, u32[]{:S(2)}) %collective-permute-start.1) | collective-permute-done | bytes 2080 | tf_op jit(solution)/shard_map/ppermute | solution.py:26
  132.2 1.3 collective-permute-start.2
  133.5 1.2 broadcast_in_dim_reshape.3
  134.7 5.7 %collective-permute-done.2 = bf16[137,1032]{1,0:T(8,128)(2,1)S(1)} collective-permute-done((bf16[137,1032]{1,0:T(8,128)(2,1)S(1)}, bf16[137,1032]{1,0:T(8,128)(2,1)S(1)}, u32[]{:S(2)}, u32[]{:S(2)}) %collective-permute-start.2) | collective-permute-done | bytes 282800 | tf_op jit(solution)/shard_map/ppermute | solution.py:225
  141.0 0.8 multiply_add_fusion
  141.8 1.2 fusion.13
  143.0 1.3 fusion.24
  (30 shorter events, 5.3 us)
Async XLA Ops:
  17.0 101.0 %all-to-all-start = ((bf16[8,1040,256]{2,1,0:T(8,128)(2,1)}), bf16[8,1040,256]{2,1,0:T(8,128)(2,1)}, u32[]{:S(2)}, u32[]{:S(2)}) async-start(bf16[8,1040,256]{2,1,0:T(8,128)(2,1)} %shard_map.86), calls=%async_computation | async-start | bytes 8519680 | tf_op jit(solution)/shard_map/all_to_all | solution.py:201
  124.0 5.7 %collective-permute-start = (bf16[256,4]{1,0:T(8,128)(2,1)S(1)}, bf16[256,4]{1,0:T(8,128)(2,1)S(1)}, u32[]{:S(2)}, u32[]{:S(2)}) collective-permute-start(bf16[256,4]{1,0:T(8,128)(2,1)S(1)} %get-tuple-element.28), channel_id=1, source_target_pairs={{0,1},{1,4},{4,5},{5,8},{8,9},{9,12},{12,13},{2,3},{3,6},{6,7},{7,... | collective-permute-start | bytes 6152 | tf_op jit(solution)/shard_map/ppermute | solution.py:25
  125.9 5.6 %collective-permute-start.1 = (bf16[256,4]{1,0:T(8,128)(2,1)S(1)}, bf16[256,4]{1,0:T(8,128)(2,1)S(1)}, u32[]{:S(2)}, u32[]{:S(2)}) collective-permute-start(bf16[256,4]{1,0:T(8,128)(2,1)S(1)} %get-tuple-element.27), channel_id=1, source_target_pairs={{1,0},{4,1},{5,4},{8,5},{9,8},{12,9},{13,12},{3,2},{6,3},{7,6},{10... | collective-permute-start | bytes 6152 | tf_op jit(solution)/shard_map/ppermute | solution.py:26
  132.2 8.1 %collective-permute-start.2 = (bf16[137,1032]{1,0:T(8,128)(2,1)S(1)}, bf16[137,1032]{1,0:T(8,128)(2,1)S(1)}, u32[]{:S(2)}, u32[]{:S(2)}) collective-permute-start(bf16[137,1032]{1,0:T(8,128)(2,1)S(1)} %fusion.34), channel_id=1, source_target_pairs={{0,2},{2,0},{1,3},{3,1},{4,6},{6,4},{5,7},{7,5},{8,10},{10,8},{9,1... | collective-permute-start | bytes 848312 | tf_op jit(solution)/shard_map/ppermute | solution.py:225

commit v16 on v15

--- a/solution.py
+++ b/solution.py
@@ -59,18 +59,22 @@
     values = values.astype(jnp.float32)
     rows = jnp.concatenate([values[:, 0, band::-1], gap, values[:, 0, : band : -1]], axis=-1)
     cols = jnp.concatenate([values[:, 1, band:], gap, values[:, 1, :band]], axis=-1)
-    return rows[:, None, :], cols[:, None, :]
-
-
-def warp_kernel(slot_ref, rows_ref, cols_ref, inside_ref, image_ref, blank_ref, out_ref, done_ref, sems):
+    return jnp.stack([rows, cols], axis=1)
+
+
+def warp_kernel(slot_ref, bases_ref, image_ref, blank_ref, out_ref, done_ref, sems):
     side = image_ref.shape[-1]
     group = image_ref.shape[0]
     step = pl.program_id(0)
-    inside = inside_ref[...]
+    lag = lax.broadcasted_iota(jnp.int32, (side, side), 0) - lax.broadcasted_iota(
+        jnp.int32, (side, side), 1
+    )
+    inside = (jnp.abs(lag) <= PSF_R + 4).astype(jnp.float32)
     copies = []
     for member in range(group):
-        row_base = jnp.broadcast_to(rows_ref[member], (side, side))
-        col_base = jnp.broadcast_to(cols_ref[member], (side, side))
+        bases = bases_ref[member]
+        row_base = jnp.broadcast_to(bases[0:1], (side, side))
+        col_base = jnp.broadcast_to(bases[1:2], (side, side))
         row_kernel = (pltpu.roll(row_base, 0, 1, stride=1, stride_axis=0) * inside).astype(
             jnp.bfloat16
         )
@@ -95,24 +99,19 @@
     count, side = images.shape[0], images.shape[-1]
     owners, capacity, cell_count = slot_weight.shape
     group = next(size for size in (8, 4, 2, 1) if count % size == 0)
-    rows, cols = base_rows(values, side)
+    bases = base_rows(values, side)
     blank = (
         jnp.zeros((owners, capacity * side + 16, side), jnp.bfloat16)
         .at[:, capacity * side, : capacity * cell_count]
         .set(slot_weight.reshape(owners, capacity * cell_count))
     )
-    position = jnp.arange(side, dtype=jnp.int32)
-    inside = (jnp.abs(position[:, None] - position[None, :]) <= PSF_R + 4).astype(jnp.float32)
-    vector_spec = pl.BlockSpec((group, 1, side), lambda b, slots: (b, 0, 0))
     return pl.pallas_call(
         warp_kernel,
         grid_spec=pltpu.PrefetchScalarGridSpec(
             num_scalar_prefetch=1,
             grid=(count // group,),
             in_specs=[
-                vector_spec,
-                vector_spec,
-                pl.BlockSpec((side, side), lambda b, slots: (0, 0)),
+                pl.BlockSpec((group, 2, side), lambda b, slots: (b, 0, 0)),
                 pl.BlockSpec((group, side, side), lambda b, slots: (b, 0, 0)),
                 pl.BlockSpec(memory_space=pl.ANY),
             ],
@@ -123,14 +122,14 @@
             ],
         ),
         out_shape=jax.ShapeDtypeStruct(blank.shape, jnp.bfloat16),
-        input_output_aliases={5: 0},
+        input_output_aliases={3: 0},
         cost_estimate=pl.CostEstimate(
             flops=4 * count * side**3,
             transcendentals=0,
             bytes_accessed=2 * (2 * count * side * side + blank.size),
         ),
         interpret=interpret,
-    )(slot_index, rows, cols, inside, images, blank)
+    )(slot_index, bases, images, blank)
 
 
 def gain_pieces(gain):

time: 145 us -> 143 us (0.986)
  no operation moved by 1% of the time
where the time goes in v16:
time: 143 us
  waiting for transfers between devices  96.7 us (68%)
  other arithmetic  12 us (8%)
  starting transfers between devices  12 us (8%)
  local copies, waits for them, and re-layouts  8.36 us (6%)
  between operations  5.53 us (4%)
  Pallas kernels  5.01 us (4%)
  matrix products  3.37 us (2%)
    all_to_all x1, waiting for transfers between devices, local(): lax.all_to_all(packed, ('sect', 'sub'), split_axis=0, concat_axis=0, tile...  89.2 us
    all_to_all x1, starting transfers between devices, local(): lax.all_to_all(packed, ('sect', 'sub'), split_axis=0, concat_axis=0, tile...  6.39 us
    ppermute x1, waiting for transfers between devices, local(): lax.ppermute(outgoing, 'band', [(i, (i + shift) % band_count) for i in ra...  5.68 us
    pallas_call x1, Pallas kernels, warp_slots(): pl.pallas_call(warp_kernel, grid_spec=pltpu.PrefetchScalarGridSpec(num_sc...  5.01 us
  transfers between devices with their start and end apart: 4, of which 3 were waited for; matrix products, arithmetic and copies ran while one was open for 2% of the time, Pallas kernels for 0%

profile of v16, /device:TPU:1, one launch (start us, length us, event | category | flops | bytes accessed | tf_op | source)
XLA Modules:
  0.0 142.9 jit_solution(10370539556581715094)
XLA Ops:
  0.7 0.7 negate_bitcast_fusion
  1.4 0.7 broadcast_add_fusion
  2.1 0.7 fusion.38
  3.4 0.9 convert_reduce_fusion.1
  4.4 0.7 fusion.78
  5.0 1.2 add_minimum_fusion.slot_ref
  6.5 0.9 convolution_convert_fusion
  8.3 2.3 %scatter.6.blank_ref = bf16[8,1040,256]{2,1,0:T(8,128)(2,1)} pad(bf16[8,1,16]{2,1,0:T(2,128)(2,1)S(1)} %reshape.157, bf16[]{:T(256)} %constant.132.clone.1), padding=0_0x1024_15x0_240 | pad | bytes 4260098 | tf_op jit(solution)/shard_map/scatter | solution.py:106
  10.6 5.0 %shard_map.86 = bf16[8,1040,256]{2,1,0:T(8,128)(2,1)} custom-call(s32[16]{0:T(128)} %add_minimum_fusion.slot_ref, f32[16,2,256]{2,1,0:T(2,128)} %pad_maximum_fusion.bases_ref, bf16[16,256,256]{2,1,0:T(8,128)(2,1)} %bitcast.41, bf16[8,1040,256]{2,1,0:T(8,128)(2,1)} %scatter.6.blank_ref), custom_call_target="tpu_custom_call", output_to_operand_aliasing={{}: (3, {})} | custom-call | flops 1073741824 | bytes 8454144 | tf_op jit(solution)/shard_map/pallas_call | solution.py:108
  15.6 6.4 %all-to-all-start = ((bf16[8,1040,256]{2,1,0:T(8,128)(2,1)}), bf16[8,1040,256]{2,1,0:T(8,128)(2,1)}, u32[]{:S(2)}, u32[]{:S(2)}) async-start(bf16[8,1040,256]{2,1,0:T(8,128)(2,1)} %shard_map.86), calls=%async_computation | async-start | bytes 8519680 | tf_op jit(solution)/shard_map/all_to_all | solution.py:200
  27.4 89.2 %all-to-all-done = bf16[8,1040,256]{2,1,0:T(8,128)(2,1)} async-done(((bf16[8,1040,256]{2,1,0:T(8,128)(2,1)}), bf16[8,1040,256]{2,1,0:T(8,128)(2,1)}, u32[]{:S(2)}, u32[]{:S(2)}) %all-to-all-start) | async-done | bytes 4259872 | tf_op jit(solution)/shard_map/all_to_all | solution.py:200
  116.7 0.7 slice_reduce_fusion.1
  117.5 2.5 %slice.167 = bf16[8,1024,256]{2,1,0:T(8,128)(2,1)S(1)} slice(bf16[8,1040,256]{2,1,0:T(8,128)(2,1)} %all-to-all-done), slice={[0:8], [0:1024], [0:256]} | slice | bytes 8388608 | tf_op jit(solution)/shard_map/slice | solution.py:204
  120.0 2.4 %divide_convert_fusion = bf16[256,256,4]{1,2,0:T(4,128)(2,1)S(1)} fusion(bf16[32,256,256]{2,1,0:T(8,128)(2,1)S(1)} %bitcast.36, f32[4]{0:T(128)S(1)} %broadcast_maximum_fusion, bf16[32,4]{1,0:T(8,128)(2,1)S(1)} %reshape_squeeze.3), kind=kOutput, calls=%fused_computation.3 | convolution fusion | flops 17301504 | bytes 4718864 | tf_op jit(solution)/shard_map/sc,sij->icj/dot_general | solution.py:205
  122.6 1.9 %collective-permute-start = (bf16[256,4]{1,0:T(8,128)(2,1)S(1)}, bf16[256,4]{1,0:T(8,128)(2,1)S(1)}, u32[]{:S(2)}, u32[]{:S(2)}) collective-permute-start(bf16[256,4]{1,0:T(8,128)(2,1)S(1)} %get-tuple-element.28), channel_id=1, source_target_pairs={{0,1},{1,4},{4,5},{5,8},{8,9},{9,12},{12,13},{2,3},{3,6},{6,7},{7,... | collective-permute-start | bytes 6152 | tf_op jit(solution)/shard_map/ppermute | solution.py:25
  124.5 2.4 %collective-permute-start.1 = (bf16[256,4]{1,0:T(8,128)(2,1)S(1)}, bf16[256,4]{1,0:T(8,128)(2,1)S(1)}, u32[]{:S(2)}, u32[]{:S(2)}) collective-permute-start(bf16[256,4]{1,0:T(8,128)(2,1)S(1)} %get-tuple-element.27), channel_id=1, source_target_pairs={{1,0},{4,1},{5,4},{8,5},{9,8},{12,9},{13,12},{3,2},{6,3},{7,6},{10... | collective-permute-start | bytes 6152 | tf_op jit(solution)/shard_map/ppermute | solution.py:26
  127.0 1.4 broadcast_select_fusion
  128.3 1.8 %collective-permute-done.1 = bf16[256,4]{1,0:T(8,128)(2,1)S(1)} collective-permute-done((bf16[256,4]{1,0:T(8,128)(2,1)S(1)}, bf16[256,4]{1,0:T(8,128)(2,1)S(1)}, u32[]{:S(2)}, u32[]{:S(2)}) %collective-permute-start.1) | collective-permute-done | bytes 2080 | tf_op jit(solution)/shard_map/ppermute | solution.py:26
  130.9 1.3 collective-permute-start.2
  132.2 1.2 broadcast_in_dim_reshape.3
  133.3 5.7 %collective-permute-done.2 = bf16[137,1032]{1,0:T(8,128)(2,1)S(1)} collective-permute-done((bf16[137,1032]{1,0:T(8,128)(2,1)S(1)}, bf16[137,1032]{1,0:T(8,128)(2,1)S(1)}, u32[]{:S(2)}, u32[]{:S(2)}) %collective-permute-start.2) | collective-permute-done | bytes 282800 | tf_op jit(solution)/shard_map/ppermute | solution.py:224
  139.6 0.8 multiply_add_fusion
  140.4 1.2 fusion.13
  141.6 1.3 fusion.24
  (30 shorter events, 4.1 us)
Async XLA Ops:
  15.6 101.0 %all-to-all-start = ((bf16[8,1040,256]{2,1,0:T(8,128)(2,1)}), bf16[8,1040,256]{2,1,0:T(8,128)(2,1)}, u32[]{:S(2)}, u32[]{:S(2)}) async-start(bf16[8,1040,256]{2,1,0:T(8,128)(2,1)} %shard_map.86), calls=%async_computation | async-start | bytes 8519680 | tf_op jit(solution)/shard_map/all_to_all | solution.py:200
  122.6 5.7 %collective-permute-start = (bf16[256,4]{1,0:T(8,128)(2,1)S(1)}, bf16[256,4]{1,0:T(8,128)(2,1)S(1)}, u32[]{:S(2)}, u32[]{:S(2)}) collective-permute-start(bf16[256,4]{1,0:T(8,128)(2,1)S(1)} %get-tuple-element.28), channel_id=1, source_target_pairs={{0,1},{1,4},{4,5},{5,8},{8,9},{9,12},{12,13},{2,3},{3,6},{6,7},{7,... | collective-permute-start | bytes 6152 | tf_op jit(solution)/shard_map/ppermute | solution.py:25
  124.5 5.6 %collective-permute-start.1 = (bf16[256,4]{1,0:T(8,128)(2,1)S(1)}, bf16[256,4]{1,0:T(8,128)(2,1)S(1)}, u32[]{:S(2)}, u32[]{:S(2)}) collective-permute-start(bf16[256,4]{1,0:T(8,128)(2,1)S(1)} %get-tuple-element.27), channel_id=1, source_target_pairs={{1,0},{4,1},{5,4},{8,5},{9,8},{12,9},{13,12},{3,2},{6,3},{7,6},{10... | collective-permute-start | bytes 6152 | tf_op jit(solution)/shard_map/ppermute | solution.py:26
  130.9 8.1 %collective-permute-start.2 = (bf16[137,1032]{1,0:T(8,128)(2,1)S(1)}, bf16[137,1032]{1,0:T(8,128)(2,1)S(1)}, u32[]{:S(2)}, u32[]{:S(2)}) collective-permute-start(bf16[137,1032]{1,0:T(8,128)(2,1)S(1)} %fusion.34), channel_id=1, source_target_pairs={{0,2},{2,0},{1,3},{3,1},{4,6},{6,4},{5,7},{7,5},{8,10},{10,8},{9,1... | collective-permute-start | bytes 848312 | tf_op jit(solution)/shard_map/ppermute | solution.py:224

commit v17 on v16

--- a/solution.py
+++ b/solution.py
@@ -98,7 +98,7 @@
 def warp_slots(images, values, slot_index, slot_weight, interpret=False):
     count, side = images.shape[0], images.shape[-1]
     owners, capacity, cell_count = slot_weight.shape
-    group = next(size for size in (8, 4, 2, 1) if count % size == 0)
+    group = next(size for size in (16, 8, 4, 2, 1) if count % size == 0)
     bases = base_rows(values, side)
     blank = (
         jnp.zeros((owners, capacity * side + 16, side), jnp.bfloat16)

time: 143 us -> 143 us (level)
  no operation moved by 1% of the time
where the time goes in v17:
time: 143 us; the launch traced here: 142 us
  waiting for transfers between devices  96.7 us (68%)
  other arithmetic  12 us (8%)
  starting transfers between devices  12 us (8%)
  local copies, waits for them, and re-layouts  8.36 us (6%)
  between operations  5.53 us (4%)
  Pallas kernels  4.47 us (3%)
  matrix products  3.37 us (2%)
    all_to_all x1, waiting for transfers between devices, local(): lax.all_to_all(packed, ('sect', 'sub'), split_axis=0, concat_axis=0, tile...  89.2 us
    all_to_all x1, starting transfers between devices, local(): lax.all_to_all(packed, ('sect', 'sub'), split_axis=0, concat_axis=0, tile...  6.4 us
    ppermute x1, waiting for transfers between devices, local(): lax.ppermute(outgoing, 'band', [(i, (i + shift) % band_count) for i in ra...  5.68 us
    pallas_call x1, Pallas kernels, warp_slots(): pl.pallas_call(warp_kernel, grid_spec=pltpu.PrefetchScalarGridSpec(num_sc...  4.47 us
  transfers between devices with their start and end apart: 4, of which 3 were waited for; matrix products, arithmetic and copies ran while one was open for 2% of the time, Pallas kernels for 0%

profile of v17, /device:TPU:1, one launch (start us, length us, event | category | flops | bytes accessed | tf_op | source)
XLA Modules:
  0.0 142.4 jit_solution(16646635651377238029)
XLA Ops:
  0.7 0.7 negate_bitcast_fusion
  1.4 0.7 broadcast_add_fusion
  2.1 0.7 fusion.38
  3.4 0.9 convert_reduce_fusion.1
  4.4 0.7 fusion.78
  5.0 1.2 add_minimum_fusion.slot_ref
  6.5 0.9 convolution_convert_fusion
  8.3 2.3 %scatter.6.blank_ref = bf16[8,1040,256]{2,1,0:T(8,128)(2,1)} pad(bf16[8,1,16]{2,1,0:T(2,128)(2,1)S(1)} %reshape.157, bf16[]{:T(256)} %constant.132.clone.1), padding=0_0x1024_15x0_240 | pad | bytes 4260098 | tf_op jit(solution)/shard_map/scatter | solution.py:106
  10.6 4.5 %shard_map.86 = bf16[8,1040,256]{2,1,0:T(8,128)(2,1)} custom-call(s32[16]{0:T(128)} %add_minimum_fusion.slot_ref, f32[16,2,256]{2,1,0:T(2,128)} %pad_maximum_fusion.bases_ref, bf16[16,256,256]{2,1,0:T(8,128)(2,1)} %bitcast.41, bf16[8,1040,256]{2,1,0:T(8,128)(2,1)} %scatter.6.blank_ref), custom_call_target="tpu_custom_call", output_to_operand_aliasing={{}: (3, {})} | custom-call | flops 1073741824 | bytes 8454144 | tf_op jit(solution)/shard_map/pallas_call | solution.py:108
  15.1 6.4 %all-to-all-start = ((bf16[8,1040,256]{2,1,0:T(8,128)(2,1)}), bf16[8,1040,256]{2,1,0:T(8,128)(2,1)}, u32[]{:S(2)}, u32[]{:S(2)}) async-start(bf16[8,1040,256]{2,1,0:T(8,128)(2,1)} %shard_map.86), calls=%async_computation | async-start | bytes 8519680 | tf_op jit(solution)/shard_map/all_to_all | solution.py:200
  26.9 89.2 %all-to-all-done = bf16[8,1040,256]{2,1,0:T(8,128)(2,1)} async-done(((bf16[8,1040,256]{2,1,0:T(8,128)(2,1)}), bf16[8,1040,256]{2,1,0:T(8,128)(2,1)}, u32[]{:S(2)}, u32[]{:S(2)}) %all-to-all-start) | async-done | bytes 4259872 | tf_op jit(solution)/shard_map/all_to_all | solution.py:200
  116.1 0.7 slice_reduce_fusion.1
  117.0 2.5 %slice.167 = bf16[8,1024,256]{2,1,0:T(8,128)(2,1)S(1)} slice(bf16[8,1040,256]{2,1,0:T(8,128)(2,1)} %all-to-all-done), slice={[0:8], [0:1024], [0:256]} | slice | bytes 8388608 | tf_op jit(solution)/shard_map/slice | solution.py:204
  119.4 2.4 %divide_convert_fusion = bf16[256,256,4]{1,2,0:T(4,128)(2,1)S(1)} fusion(bf16[32,256,256]{2,1,0:T(8,128)(2,1)S(1)} %bitcast.36, f32[4]{0:T(128)S(1)} %broadcast_maximum_fusion, bf16[32,4]{1,0:T(8,128)(2,1)S(1)} %reshape_squeeze.3), kind=kOutput, calls=%fused_computation.3 | convolution fusion | flops 17301504 | bytes 4718864 | tf_op jit(solution)/shard_map/sc,sij->icj/dot_general | solution.py:205
  122.1 1.9 %collective-permute-start = (bf16[256,4]{1,0:T(8,128)(2,1)S(1)}, bf16[256,4]{1,0:T(8,128)(2,1)S(1)}, u32[]{:S(2)}, u32[]{:S(2)}) collective-permute-start(bf16[256,4]{1,0:T(8,128)(2,1)S(1)} %get-tuple-element.28), channel_id=1, source_target_pairs={{0,1},{1,4},{4,5},{5,8},{8,9},{9,12},{12,13},{2,3},{3,6},{6,7},{7,... | collective-permute-start | bytes 6152 | tf_op jit(solution)/shard_map/ppermute | solution.py:25
  124.0 2.4 %collective-permute-start.1 = (bf16[256,4]{1,0:T(8,128)(2,1)S(1)}, bf16[256,4]{1,0:T(8,128)(2,1)S(1)}, u32[]{:S(2)}, u32[]{:S(2)}) collective-permute-start(bf16[256,4]{1,0:T(8,128)(2,1)S(1)} %get-tuple-element.27), channel_id=1, source_target_pairs={{1,0},{4,1},{5,4},{8,5},{9,8},{12,9},{13,12},{3,2},{6,3},{7,6},{10... | collective-permute-start | bytes 6152 | tf_op jit(solution)/shard_map/ppermute | solution.py:26
  126.4 1.4 broadcast_select_fusion
  127.8 1.8 %collective-permute-done.1 = bf16[256,4]{1,0:T(8,128)(2,1)S(1)} collective-permute-done((bf16[256,4]{1,0:T(8,128)(2,1)S(1)}, bf16[256,4]{1,0:T(8,128)(2,1)S(1)}, u32[]{:S(2)}, u32[]{:S(2)}) %collective-permute-start.1) | collective-permute-done | bytes 2080 | tf_op jit(solution)/shard_map/ppermute | solution.py:26
  130.4 1.3 collective-permute-start.2
  131.6 1.2 broadcast_in_dim_reshape.3
  132.8 5.7 %collective-permute-done.2 = bf16[137,1032]{1,0:T(8,128)(2,1)S(1)} collective-permute-done((bf16[137,1032]{1,0:T(8,128)(2,1)S(1)}, bf16[137,1032]{1,0:T(8,128)(2,1)S(1)}, u32[]{:S(2)}, u32[]{:S(2)}) %collective-permute-start.2) | collective-permute-done | bytes 282800 | tf_op jit(solution)/shard_map/ppermute | solution.py:224
  139.1 0.8 multiply_add_fusion
  139.9 1.2 fusion.13
  141.1 1.3 fusion.24
  (30 shorter events, 4.1 us)
Async XLA Ops:
  15.1 101.1 %all-to-all-start = ((bf16[8,1040,256]{2,1,0:T(8,128)(2,1)}), bf16[8,1040,256]{2,1,0:T(8,128)(2,1)}, u32[]{:S(2)}, u32[]{:S(2)}) async-start(bf16[8,1040,256]{2,1,0:T(8,128)(2,1)} %shard_map.86), calls=%async_computation | async-start | bytes 8519680 | tf_op jit(solution)/shard_map/all_to_all | solution.py:200
  122.1 5.7 %collective-permute-start = (bf16[256,4]{1,0:T(8,128)(2,1)S(1)}, bf16[256,4]{1,0:T(8,128)(2,1)S(1)}, u32[]{:S(2)}, u32[]{:S(2)}) collective-permute-start(bf16[256,4]{1,0:T(8,128)(2,1)S(1)} %get-tuple-element.28), channel_id=1, source_target_pairs={{0,1},{1,4},{4,5},{5,8},{8,9},{9,12},{12,13},{2,3},{3,6},{6,7},{7,... | collective-permute-start | bytes 6152 | tf_op jit(solution)/shard_map/ppermute | solution.py:25
  124.0 5.6 %collective-permute-start.1 = (bf16[256,4]{1,0:T(8,128)(2,1)S(1)}, bf16[256,4]{1,0:T(8,128)(2,1)S(1)}, u32[]{:S(2)}, u32[]{:S(2)}) collective-permute-start(bf16[256,4]{1,0:T(8,128)(2,1)S(1)} %get-tuple-element.27), channel_id=1, source_target_pairs={{1,0},{4,1},{5,4},{8,5},{9,8},{12,9},{13,12},{3,2},{6,3},{7,6},{10... | collective-permute-start | bytes 6152 | tf_op jit(solution)/shard_map/ppermute | solution.py:26
  130.4 8.1 %collective-permute-start.2 = (bf16[137,1032]{1,0:T(8,128)(2,1)S(1)}, bf16[137,1032]{1,0:T(8,128)(2,1)S(1)}, u32[]{:S(2)}, u32[]{:S(2)}) collective-permute-start(bf16[137,1032]{1,0:T(8,128)(2,1)S(1)} %fusion.34), channel_id=1, source_target_pairs={{0,2},{2,0},{1,3},{3,1},{4,6},{6,4},{5,7},{7,5},{8,10},{10,8},{9,1... | collective-permute-start | bytes 848312 | tf_op jit(solution)/shard_map/ppermute | solution.py:224

commit v18 on v17

--- a/solution.py
+++ b/solution.py
@@ -199,13 +199,18 @@
     )
     received = lax.all_to_all(packed, ("sect", "sub"), split_axis=0, concat_axis=0, tiled=True)
     received_weight = received[:, capacity * side, : capacity * CELL_DEV].reshape(
-        slot_count, CELL_DEV
-    )
-    received = received[:, : capacity * side].reshape(slot_count, side, side)
-    numerator = jnp.einsum(
-        "sc,sij->icj", received_weight, received, preferred_element_type=jnp.float32
-    )
-    denominator = jnp.sum(received_weight.astype(jnp.float32), axis=0)
+        owners, capacity, CELL_DEV
+    )
+    numerator = sum(
+        jnp.einsum(
+            "oc,oij->icj",
+            received_weight[:, rank],
+            received[:, rank * side : (rank + 1) * side],
+            preferred_element_type=jnp.float32,
+        )
+        for rank in range(capacity)
+    )
+    denominator = jnp.sum(received_weight.astype(jnp.float32), axis=(0, 1))
     cell_mean = (numerator / jnp.maximum(denominator, 1.0)[None, :, None]).astype(jnp.bfloat16)
     coadd = cell_mean.reshape(side, CELL_DEV * side)
     padded = extended(coadd, ((("sect", "sub"), 1),), DET_R)

time: 143 us -> 146 us (1.021)
    ppermute x1, waiting for transfers between devices: 1.8 us -> 0.01 us  [extended(): after = lax.ppermute(initial, axis, down)]
    ppermute x1, waiting for transfers between devices: 5.68 us -> 7.35 us  [local(): lax.ppermute(outgoing, 'band', [(i, (i + shift) % band_count) for i in ra...]
    dot_general x1 -> x4, matrix products: 2.44 us -> 3.15 us  [local(): jnp.einsum('oc,oij->icj', received_weight[:, rank], received[:, rank * si...]
  transfers between devices with their start and end apart: 4 -> 4, of which waited for: 3 -> 2; matrix products, arithmetic and copies ran while one was open for 2% -> 2% of each run, Pallas kernels for 0% -> 0%
where the time goes in v18:
time: 146 us; the launch traced here: 145 us
  waiting for transfers between devices  96.6 us (66%)
  starting transfers between devices  13.2 us (9%)
  other arithmetic  12.7 us (9%)
  local copies, waits for them, and re-layouts  8.59 us (6%)
  between operations  5.54 us (4%)
  Pallas kernels  4.47 us (3%)
  matrix products  4.08 us (3%)
    all_to_all x1, waiting for transfers between devices, local(): lax.all_to_all(packed, ('sect', 'sub'), split_axis=0, concat_axis=0, tile...  89.2 us
    ppermute x1, waiting for transfers between devices, local(): lax.ppermute(outgoing, 'band', [(i, (i + shift) % band_count) for i in ra...  7.35 us
    all_to_all x1, starting transfers between devices, local(): lax.all_to_all(packed, ('sect', 'sub'), split_axis=0, concat_axis=0, tile...  6.39 us
    pallas_call x1, Pallas kernels, warp_slots(): pl.pallas_call(warp_kernel, grid_spec=pltpu.PrefetchScalarGridSpec(num_sc...  4.47 us
    dot_general x4, matrix products, local(): jnp.einsum('oc,oij->icj', received_weight[:, rank], received[:, rank * si...  3.15 us
  transfers between devices with their start and end apart: 4, of which 2 were waited for; matrix products, arithmetic and copies ran while one was open for 2% of the time, Pallas kernels for 0%

profile of v18, /device:TPU:1, one launch (start us, length us, event | category | flops | bytes accessed | tf_op | source)
XLA Modules:
  0.0 145.2 jit_solution(14166125942849313295)
XLA Ops:
  0.6 0.9 convert_reduce_fusion
  2.2 1.2 add_minimum_fusion.slot_ref
  4.2 0.8 broadcast_add_fusion
  4.9 0.7 fusion.41
  6.2 0.9 convolution_convert_fusion
  8.3 2.3 %scatter.6.blank_ref = bf16[8,1040,256]{2,1,0:T(8,128)(2,1)} pad(bf16[8,1,16]{2,1,0:T(2,128)(2,1)S(1)} %reshape.157, bf16[]{:T(256)} %constant.132.clone.1), padding=0_0x1024_15x0_240 | pad | bytes 4260098 | tf_op jit(solution)/shard_map/scatter | solution.py:106
  10.6 4.5 %shard_map.86 = bf16[8,1040,256]{2,1,0:T(8,128)(2,1)} custom-call(s32[16]{0:T(128)} %add_minimum_fusion.slot_ref, f32[16,2,256]{2,1,0:T(2,128)} %pad_maximum_fusion.bases_ref, bf16[16,256,256]{2,1,0:T(8,128)(2,1)} %bitcast.53, bf16[8,1040,256]{2,1,0:T(8,128)(2,1)} %scatter.6.blank_ref), custom_call_target="tpu_custom_call", output_to_operand_aliasing={{}: (3, {})} | custom-call | flops 1073741824 | bytes 8454144 | tf_op jit(solution)/shard_map/pallas_call | solution.py:108
  15.1 6.4 %all-to-all-start = ((bf16[8,1040,256]{2,1,0:T(8,128)(2,1)}), bf16[8,1040,256]{2,1,0:T(8,128)(2,1)}, u32[]{:S(2)}, u32[]{:S(2)}) async-start(bf16[8,1040,256]{2,1,0:T(8,128)(2,1)} %shard_map.86), calls=%async_computation | async-start | bytes 8519680 | tf_op jit(solution)/shard_map/all_to_all | solution.py:200
  26.9 89.2 %all-to-all-done = bf16[8,1040,256]{2,1,0:T(8,128)(2,1)} async-done(((bf16[8,1040,256]{2,1,0:T(8,128)(2,1)}), bf16[8,1040,256]{2,1,0:T(8,128)(2,1)}, u32[]{:S(2)}, u32[]{:S(2)}) %all-to-all-start) | async-done | bytes 4259872 | tf_op jit(solution)/shard_map/all_to_all | solution.py:200
  116.1 0.7 convert_reduce_fusion.1
  117.8 2.6 %fusion.83 = (bf16[8,256,256]{2,1,0:T(8,128)(2,1)S(1)}, bf16[8,256,256]{2,1,0:T(8,128)(2,1)S(1)}, bf16[8,256,256]{2,1,0:T(8,128)(2,1)S(1)}, bf16[8,256,256]{2,1,0:T(8,128)(2,1)S(1)}) fusion(bf16[8,1040,256]{2,1,0:T(8,128)(2,1)} %all-to-all-done), kind=kLoop, calls=%fused_computation.150 | loop fusion | bytes 8388608 | tf_op jit(solution)/shard_map/slice | solution.py:208
  120.4 0.7 fusion.5
  121.1 0.8 convolution_add_fusion.2
  121.9 0.8 convolution_add_fusion.1
  122.8 0.8 fusion.1
  123.7 2.8 %collective-permute-start.1 = (bf16[256,4]{1,0:T(8,128)(2,1)S(1)}, bf16[256,4]{1,0:T(8,128)(2,1)S(1)}, u32[]{:S(2)}, u32[]{:S(2)}) collective-permute-start(bf16[256,4]{1,0:T(8,128)(2,1)S(1)} %get-tuple-element.31), channel_id=1, source_target_pairs={{1,0},{4,1},{5,4},{8,5},{9,8},{12,9},{13,12},{3,2},{6,3},{7,6},{10... | collective-permute-start | bytes 6152 | tf_op jit(solution)/shard_map/ppermute | solution.py:26
  126.5 2.8 %collective-permute-start = (bf16[256,4]{1,0:T(8,128)(2,1)S(1)}, bf16[256,4]{1,0:T(8,128)(2,1)S(1)}, u32[]{:S(2)}, u32[]{:S(2)}) collective-permute-start(bf16[256,4]{1,0:T(8,128)(2,1)S(1)} %get-tuple-element.32), channel_id=1, source_target_pairs={{0,1},{1,4},{4,5},{5,8},{8,9},{9,12},{12,13},{2,3},{3,6},{6,7},{7,... | collective-permute-start | bytes 6152 | tf_op jit(solution)/shard_map/ppermute | solution.py:25
  129.3 1.4 broadcast_select_fusion
  131.5 1.3 collective-permute-start.2
  132.8 1.2 broadcast_in_dim_reshape.3
  133.9 7.4 %collective-permute-done.2 = bf16[137,1032]{1,0:T(8,128)(2,1)S(1)} collective-permute-done((bf16[137,1032]{1,0:T(8,128)(2,1)S(1)}, bf16[137,1032]{1,0:T(8,128)(2,1)S(1)}, u32[]{:S(2)}, u32[]{:S(2)}) %collective-permute-start.2) | collective-permute-done | bytes 282800 | tf_op jit(solution)/shard_map/ppermute | solution.py:229
  141.9 0.8 multiply_add_fusion
  142.7 1.2 fusion.16
  143.9 1.3 fusion.27
  (35 shorter events, 6.2 us)
Async XLA Ops:
  15.1 101.0 %all-to-all-start = ((bf16[8,1040,256]{2,1,0:T(8,128)(2,1)}), bf16[8,1040,256]{2,1,0:T(8,128)(2,1)}, u32[]{:S(2)}, u32[]{:S(2)}) async-start(bf16[8,1040,256]{2,1,0:T(8,128)(2,1)} %shard_map.86), calls=%async_computation | async-start | bytes 8519680 | tf_op jit(solution)/shard_map/all_to_all | solution.py:200
  123.7 7.0 %collective-permute-start.1 = (bf16[256,4]{1,0:T(8,128)(2,1)S(1)}, bf16[256,4]{1,0:T(8,128)(2,1)S(1)}, u32[]{:S(2)}, u32[]{:S(2)}) collective-permute-start(bf16[256,4]{1,0:T(8,128)(2,1)S(1)} %get-tuple-element.31), channel_id=1, source_target_pairs={{1,0},{4,1},{5,4},{8,5},{9,8},{12,9},{13,12},{3,2},{6,3},{7,6},{10... | collective-permute-start | bytes 6152 | tf_op jit(solution)/shard_map/ppermute | solution.py:26
  126.5 4.2 %collective-permute-start = (bf16[256,4]{1,0:T(8,128)(2,1)S(1)}, bf16[256,4]{1,0:T(8,128)(2,1)S(1)}, u32[]{:S(2)}, u32[]{:S(2)}) collective-permute-start(bf16[256,4]{1,0:T(8,128)(2,1)S(1)} %get-tuple-element.32), channel_id=1, source_target_pairs={{0,1},{1,4},{4,5},{5,8},{8,9},{9,12},{12,13},{2,3},{3,6},{6,7},{7,... | collective-permute-start | bytes 6152 | tf_op jit(solution)/shard_map/ppermute | solution.py:25
  131.5 9.8 %collective-permute-start.2 = (bf16[137,1032]{1,0:T(8,128)(2,1)S(1)}, bf16[137,1032]{1,0:T(8,128)(2,1)S(1)}, u32[]{:S(2)}, u32[]{:S(2)}) collective-permute-start(bf16[137,1032]{1,0:T(8,128)(2,1)S(1)} %fusion.37), channel_id=1, source_target_pairs={{0,2},{2,0},{1,3},{3,1},{4,6},{6,4},{5,7},{7,5},{8,10},{10,8},{9,1... | collective-permute-start | bytes 848312 | tf_op jit(solution)/shard_map/ppermute | solution.py:229

commit v19 on v17

--- a/solution.py
+++ b/solution.py
@@ -182,15 +182,14 @@
     slot_index = target * capacity + rank_within
     matching = jnp.arange(slot_count, dtype=jnp.int32)[:, None] == slot_index[None, :]
     source = jnp.sum(jnp.where(matching, block_order[None, :], 0), axis=1)
-    placing = matching.astype(jnp.bfloat16)
     cell_weight = jnp.where(
         cells[0][:, None] == jnp.arange(CELL_DEV, dtype=jnp.int32)[None, :],
         weights[0][:, None],
         jnp.zeros((), jnp.bfloat16),
     )
-    packed_weight = jnp.dot(placing, cell_weight, preferred_element_type=jnp.float32).astype(
-        jnp.bfloat16
-    )
+    packed_weight = jnp.sum(
+        jnp.where(matching[:, :, None], cell_weight[None].astype(jnp.float32), 0.0), axis=1
+    ).astype(jnp.bfloat16)
     packed = warp_slots(
         images[0],
         values,

time: 143 us -> 143 us (level)
  no operation moved by 1% of the time
where the time goes in v19:
time: 143 us; the launch traced here: 142 us
  waiting for transfers between devices  96.7 us (68%)
  other arithmetic  12.8 us (9%)
  starting transfers between devices  12 us (8%)
  local copies, waits for them, and re-layouts  8.36 us (6%)
  between operations  5.53 us (4%)
  Pallas kernels  4.49 us (3%)
  matrix products  2.44 us (2%)
    all_to_all x1, waiting for transfers between devices, local(): lax.all_to_all(packed, ('sect', 'sub'), split_axis=0, concat_axis=0, tile...  89.2 us
    all_to_all x1, starting transfers between devices, local(): lax.all_to_all(packed, ('sect', 'sub'), split_axis=0, concat_axis=0, tile...  6.37 us
    ppermute x1, waiting for transfers between devices, local(): lax.ppermute(outgoing, 'band', [(i, (i + shift) % band_count) for i in ra...  5.64 us
    pallas_call x1, Pallas kernels, warp_slots(): pl.pallas_call(warp_kernel, grid_spec=pltpu.PrefetchScalarGridSpec(num_sc...  4.49 us
  transfers between devices with their start and end apart: 4, of which 3 were waited for; matrix products, arithmetic and copies ran while one was open for 2% of the time, Pallas kernels for 0%

profile of v19, /device:TPU:1, one launch (start us, length us, event | category | flops | bytes accessed | tf_op | source)
XLA Modules:
  0.0 142.3 jit_solution(2760998908531297100)
XLA Ops:
  0.7 0.7 negate_bitcast_fusion
  1.4 0.7 broadcast_add_fusion
  2.1 0.7 fusion.38
  3.4 0.9 convert_reduce_fusion.1
  4.4 0.7 fusion.74
  5.0 1.2 add_minimum_fusion.slot_ref
  6.6 0.7 fusion.72
  8.2 2.3 %scatter.6.blank_ref = bf16[8,1040,256]{2,1,0:T(8,128)(2,1)} pad(bf16[8,1,16]{2,1,0:T(2,128)(2,1)S(1)} %convert_element_type.73, bf16[]{:T(256)} %constant.132.clone.1), padding=0_0x1024_15x0_240 | pad | bytes 4260098 | tf_op jit(solution)/shard_map/scatter | solution.py:106
  10.5 4.5 %shard_map.86 = bf16[8,1040,256]{2,1,0:T(8,128)(2,1)} custom-call(s32[16]{0:T(128)} %add_minimum_fusion.slot_ref, f32[16,2,256]{2,1,0:T(2,128)} %pad_maximum_fusion.bases_ref, bf16[16,256,256]{2,1,0:T(8,128)(2,1)} %bitcast.41, bf16[8,1040,256]{2,1,0:T(8,128)(2,1)} %scatter.6.blank_ref), custom_call_target="tpu_custom_call", output_to_operand_aliasing={{}: (3, {})} | custom-call | flops 1073741824 | bytes 8454144 | tf_op jit(solution)/shard_map/pallas_call | solution.py:108
  15.0 6.4 %all-to-all-start = ((bf16[8,1040,256]{2,1,0:T(8,128)(2,1)}), bf16[8,1040,256]{2,1,0:T(8,128)(2,1)}, u32[]{:S(2)}, u32[]{:S(2)}) async-start(bf16[8,1040,256]{2,1,0:T(8,128)(2,1)} %shard_map.86), calls=%async_computation | async-start | bytes 8519680 | tf_op jit(solution)/shard_map/all_to_all | solution.py:199
  26.8 89.2 %all-to-all-done = bf16[8,1040,256]{2,1,0:T(8,128)(2,1)} async-done(((bf16[8,1040,256]{2,1,0:T(8,128)(2,1)}), bf16[8,1040,256]{2,1,0:T(8,128)(2,1)}, u32[]{:S(2)}, u32[]{:S(2)}) %all-to-all-start) | async-done | bytes 4259872 | tf_op jit(solution)/shard_map/all_to_all | solution.py:199
  116.0 0.7 slice_reduce_fusion.1
  116.9 2.5 %slice.167 = bf16[8,1024,256]{2,1,0:T(8,128)(2,1)S(1)} slice(bf16[8,1040,256]{2,1,0:T(8,128)(2,1)} %all-to-all-done), slice={[0:8], [0:1024], [0:256]} | slice | bytes 8388608 | tf_op jit(solution)/shard_map/slice | solution.py:203
  119.4 2.4 %divide_convert_fusion = bf16[256,256,4]{1,2,0:T(4,128)(2,1)S(1)} fusion(bf16[32,256,256]{2,1,0:T(8,128)(2,1)S(1)} %bitcast.36, f32[4]{0:T(128)S(1)} %broadcast_maximum_fusion, bf16[32,4]{1,0:T(8,128)(2,1)S(1)} %reshape_squeeze.3), kind=kOutput, calls=%fused_computation.2 | convolution fusion | flops 17301504 | bytes 4718864 | tf_op jit(solution)/shard_map/sc,sij->icj/dot_general | solution.py:204
  122.0 1.9 %collective-permute-start = (bf16[256,4]{1,0:T(8,128)(2,1)S(1)}, bf16[256,4]{1,0:T(8,128)(2,1)S(1)}, u32[]{:S(2)}, u32[]{:S(2)}) collective-permute-start(bf16[256,4]{1,0:T(8,128)(2,1)S(1)} %get-tuple-element.28), channel_id=1, source_target_pairs={{0,1},{1,4},{4,5},{5,8},{8,9},{9,12},{12,13},{2,3},{3,6},{6,7},{7,... | collective-permute-start | bytes 6152 | tf_op jit(solution)/shard_map/ppermute | solution.py:25
  123.9 2.4 %collective-permute-start.1 = (bf16[256,4]{1,0:T(8,128)(2,1)S(1)}, bf16[256,4]{1,0:T(8,128)(2,1)S(1)}, u32[]{:S(2)}, u32[]{:S(2)}) collective-permute-start(bf16[256,4]{1,0:T(8,128)(2,1)S(1)} %get-tuple-element.27), channel_id=1, source_target_pairs={{1,0},{4,1},{5,4},{8,5},{9,8},{12,9},{13,12},{3,2},{6,3},{7,6},{10... | collective-permute-start | bytes 6152 | tf_op jit(solution)/shard_map/ppermute | solution.py:26
  126.3 1.4 broadcast_select_fusion
  127.7 1.8 %collective-permute-done.1 = bf16[256,4]{1,0:T(8,128)(2,1)S(1)} collective-permute-done((bf16[256,4]{1,0:T(8,128)(2,1)S(1)}, bf16[256,4]{1,0:T(8,128)(2,1)S(1)}, u32[]{:S(2)}, u32[]{:S(2)}) %collective-permute-start.1) | collective-permute-done | bytes 2080 | tf_op jit(solution)/shard_map/ppermute | solution.py:26
  130.3 1.3 collective-permute-start.2
  131.6 1.2 broadcast_in_dim_reshape.3
  132.7 5.6 %collective-permute-done.2 = bf16[137,1032]{1,0:T(8,128)(2,1)S(1)} collective-permute-done((bf16[137,1032]{1,0:T(8,128)(2,1)S(1)}, bf16[137,1032]{1,0:T(8,128)(2,1)S(1)}, u32[]{:S(2)}, u32[]{:S(2)}) %collective-permute-start.2) | collective-permute-done | bytes 282800 | tf_op jit(solution)/shard_map/ppermute | solution.py:223
  139.0 0.8 multiply_add_fusion
  139.8 1.2 fusion.13
  141.0 1.3 fusion.24
  (32 shorter events, 4.2 us)
Async XLA Ops:
  15.0 101.0 %all-to-all-start = ((bf16[8,1040,256]{2,1,0:T(8,128)(2,1)}), bf16[8,1040,256]{2,1,0:T(8,128)(2,1)}, u32[]{:S(2)}, u32[]{:S(2)}) async-start(bf16[8,1040,256]{2,1,0:T(8,128)(2,1)} %shard_map.86), calls=%async_computation | async-start | bytes 8519680 | tf_op jit(solution)/shard_map/all_to_all | solution.py:199
  122.0 5.7 %collective-permute-start = (bf16[256,4]{1,0:T(8,128)(2,1)S(1)}, bf16[256,4]{1,0:T(8,128)(2,1)S(1)}, u32[]{:S(2)}, u32[]{:S(2)}) collective-permute-start(bf16[256,4]{1,0:T(8,128)(2,1)S(1)} %get-tuple-element.28), channel_id=1, source_target_pairs={{0,1},{1,4},{4,5},{5,8},{8,9},{9,12},{12,13},{2,3},{3,6},{6,7},{7,... | collective-permute-start | bytes 6152 | tf_op jit(solution)/shard_map/ppermute | solution.py:25
  123.9 5.6 %collective-permute-start.1 = (bf16[256,4]{1,0:T(8,128)(2,1)S(1)}, bf16[256,4]{1,0:T(8,128)(2,1)S(1)}, u32[]{:S(2)}, u32[]{:S(2)}) collective-permute-start(bf16[256,4]{1,0:T(8,128)(2,1)S(1)} %get-tuple-element.27), channel_id=1, source_target_pairs={{1,0},{4,1},{5,4},{8,5},{9,8},{12,9},{13,12},{3,2},{6,3},{7,6},{10... | collective-permute-start | bytes 6152 | tf_op jit(solution)/shard_map/ppermute | solution.py:26
  130.3 8.1 %collective-permute-start.2 = (bf16[137,1032]{1,0:T(8,128)(2,1)S(1)}, bf16[137,1032]{1,0:T(8,128)(2,1)S(1)}, u32[]{:S(2)}, u32[]{:S(2)}) collective-permute-start(bf16[137,1032]{1,0:T(8,128)(2,1)S(1)} %fusion.34), channel_id=1, source_target_pairs={{0,2},{2,0},{1,3},{3,1},{4,6},{6,4},{5,7},{7,5},{8,10},{10,8},{9,1... | collective-permute-start | bytes 848312 | tf_op jit(solution)/shard_map/ppermute | solution.py:223

commit v20 on v19

--- a/solution.py
+++ b/solution.py
@@ -207,7 +207,27 @@
     denominator = jnp.sum(received_weight.astype(jnp.float32), axis=0)
     cell_mean = (numerator / jnp.maximum(denominator, 1.0)[None, :, None]).astype(jnp.bfloat16)
     coadd = cell_mean.reshape(side, CELL_DEV * side)
-    padded = extended(coadd, ((("sect", "sub"), 1),), DET_R)
+    scale = jnp.maximum(denominator, 1.0)
+    first = jnp.einsum(
+        "s,sij->ij",
+        received_weight[:, 0],
+        received[:, :, :DET_R],
+        preferred_element_type=jnp.float32,
+    )
+    last = jnp.einsum(
+        "s,sij->ij",
+        received_weight[:, CELL_DEV - 1],
+        received[:, :, side - DET_R :],
+        preferred_element_type=jnp.float32,
+    )
+    first = (first / scale[0]).astype(jnp.bfloat16)
+    last = (last / scale[CELL_DEV - 1]).astype(jnp.bfloat16)
+    size = lax.axis_size(("sect", "sub"))
+    up = [(i, (i + 1) % size) for i in range(size - 1)]
+    down = [(j, i) for i, j in up]
+    before = lax.ppermute(last, ("sect", "sub"), up)
+    after = lax.ppermute(first, ("sect", "sub"), down)
+    padded = jnp.concatenate([before, coadd, after], axis=1)
     band_count = lax.axis_size("band")
     height = side // band_count
     framed = jnp.pad(padded, ((DET_R, DET_R), (0, 0)))

time: 143 us -> 147 us (1.028)
  other arithmetic: 12.8 us -> 15.8 us
  waiting for transfers between devices: 96.7 us -> 95.2 us
    ppermute x2, waiting for transfers between devices: 1.8 us -> 0.01 us  [the longest x1 0.01 us: local(): after = lax.ppermute(first, ('sect', 'sub'), down)]
    dot_general x0 -> x1, other arithmetic: none -> 1.71 us  [local(): jnp.einsum('s,sij->ij', received_weight[:, 0], received[:, :, :DET_R], pr...]
    ppermute x1, waiting for transfers between devices: 5.64 us -> 7.32 us  [local(): lax.ppermute(outgoing, 'band', [(i, (i + shift) % band_count) for i in ra...]
  transfers between devices with their start and end apart: 4 -> 4, of which waited for: 3 -> 2; matrix products, arithmetic and copies ran while one was open for 2% -> 4% of each run, Pallas kernels for 0% -> 0%
where the time goes in v20:
time: 147 us; the launch traced here: 146 us
  waiting for transfers between devices  95.2 us (65%)
  other arithmetic  15.8 us (11%)
  starting transfers between devices  13.3 us (9%)
  local copies, waits for them, and re-layouts  9.04 us (6%)
  between operations  5.59 us (4%)
  Pallas kernels  4.47 us (3%)
  matrix products  2.44 us (2%)
    all_to_all x1, waiting for transfers between devices, local(): lax.all_to_all(packed, ('sect', 'sub'), split_axis=0, concat_axis=0, tile...  87.9 us
    ppermute x1, waiting for transfers between devices, local(): lax.ppermute(outgoing, 'band', [(i, (i + shift) % band_count) for i in ra...  7.32 us
    all_to_all x1, starting transfers between devices, local(): lax.all_to_all(packed, ('sect', 'sub'), split_axis=0, concat_axis=0, tile...  6.39 us
    pallas_call x1, Pallas kernels, warp_slots(): pl.pallas_call(warp_kernel, grid_spec=pltpu.PrefetchScalarGridSpec(num_sc...  4.47 us
  transfers between devices with their start and end apart: 4, of which 2 were waited for; matrix products, arithmetic and copies ran while one was open for 4% of the time, Pallas kernels for 0%

profile of v20, /device:TPU:1, one launch (start us, length us, event | category | flops | bytes accessed | tf_op | source)
XLA Modules:
  0.0 145.8 jit_solution(3604101606330941446)
XLA Ops:
  0.7 0.7 negate_bitcast_fusion
  1.4 0.7 broadcast_add_fusion
  2.1 0.7 fusion.38
  3.4 0.9 convert_reduce_fusion.1
  5.0 1.2 add_minimum_fusion.slot_ref
  6.6 0.7 fusion.72
  8.2 2.3 %scatter.6.blank_ref = bf16[8,1040,256]{2,1,0:T(8,128)(2,1)} pad(bf16[8,1,16]{2,1,0:T(2,128)(2,1)S(1)} %convert_element_type.81, bf16[]{:T(256)} %constant.132.clone.1), padding=0_0x1024_15x0_240 | pad | bytes 4260098 | tf_op jit(solution)/shard_map/scatter | solution.py:106
  10.5 4.5 %shard_map.86 = bf16[8,1040,256]{2,1,0:T(8,128)(2,1)} custom-call(s32[16]{0:T(128)} %add_minimum_fusion.slot_ref, f32[16,2,256]{2,1,0:T(2,128)} %pad_maximum_fusion.bases_ref, bf16[16,256,256]{2,1,0:T(8,128)(2,1)} %bitcast.43, bf16[8,1040,256]{2,1,0:T(8,128)(2,1)} %scatter.6.blank_ref), custom_call_target="tpu_custom_call", output_to_operand_aliasing={{}: (3, {})} | custom-call | flops 1073741824 | bytes 8454144 | tf_op jit(solution)/shard_map/pallas_call | solution.py:108
  15.0 6.4 %all-to-all-start = ((bf16[8,1040,256]{2,1,0:T(8,128)(2,1)}), bf16[8,1040,256]{2,1,0:T(8,128)(2,1)}, u32[]{:S(2)}, u32[]{:S(2)}) async-start(bf16[8,1040,256]{2,1,0:T(8,128)(2,1)} %shard_map.86), calls=%async_computation | async-start | bytes 8519680 | tf_op jit(solution)/shard_map/all_to_all | solution.py:199
  26.8 1.4 broadcast_select_fusion
  28.2 87.9 %all-to-all-done = bf16[8,1040,256]{2,1,0:T(8,128)(2,1)} async-done(((bf16[8,1040,256]{2,1,0:T(8,128)(2,1)}), bf16[8,1040,256]{2,1,0:T(8,128)(2,1)}, u32[]{:S(2)}, u32[]{:S(2)}) %all-to-all-start) | async-done | bytes 4259872 | tf_op jit(solution)/shard_map/all_to_all | solution.py:199
  116.0 0.7 slice_reduce_fusion.3
  117.7 2.5 %slice.183 = bf16[8,1024,256]{2,1,0:T(8,128)(2,1)S(1)} slice(bf16[8,1040,256]{2,1,0:T(8,128)(2,1)} %all-to-all-done), slice={[0:8], [0:1024], [0:256]} | slice | bytes 8388608 | tf_op jit(solution)/shard_map/slice | solution.py:203
  120.1 1.7 %multiply_reduce_fusion = (f32[256,4]{1,0:T(8,128)S(1)}, f32[256,4]{1,0:T(8,128)S(1)}) fusion(bf16[32,256,256]{2,1,0:T(8,128)(2,1)S(1)} %bitcast.38, f32[32]{0:T(128)S(1)} %convert.17, f32[32]{0:T(128)S(1)} %convert.15), kind=kLoop, calls=%fused_computation | loop fusion | flops 194560 | bytes 139520 | tf_op jit(solution)/shard_map/s,sij->ij/dot_general | solution.py:211
  122.5 2.8 %collective-permute-start.1 = (bf16[256,4]{1,0:T(8,128)(2,1)S(1)}, bf16[256,4]{1,0:T(8,128)(2,1)S(1)}, u32[]{:S(2)}, u32[]{:S(2)}) collective-permute-start(bf16[256,4]{1,0:T(8,128)(2,1)S(1)} %divide_convert_fusion.1), channel_id=1, source_target_pairs={{1,0},{4,1},{5,4},{8,5},{9,8},{12,9},{13,12},{3,2},{6,3},{7,6},{10... | collective-permute-start | bytes 6152 | tf_op jit(solution)/shard_map/ppermute | solution.py:229
  125.3 0.7 divide_convert_fusion.2
  126.0 2.8 %collective-permute-start = (bf16[256,4]{1,0:T(8,128)(2,1)S(1)}, bf16[256,4]{1,0:T(8,128)(2,1)S(1)}, u32[]{:S(2)}, u32[]{:S(2)}) collective-permute-start(bf16[256,4]{1,0:T(8,128)(2,1)S(1)} %divide_convert_fusion.2), channel_id=1, source_target_pairs={{0,1},{1,4},{4,5},{5,8},{8,9},{9,12},{12,13},{2,3},{3,6},{6,7},{7,... | collective-permute-start | bytes 6152 | tf_op jit(solution)/shard_map/ppermute | solution.py:228
  128.8 2.4 %divide_convert_fusion = bf16[256,256,4]{1,2,0:T(4,128)(2,1)S(1)} fusion(bf16[32,256,256]{2,1,0:T(8,128)(2,1)S(1)} %bitcast.39, f32[4]{0:T(128)S(1)} %broadcast_maximum_fusion, bf16[32,4]{1,0:T(8,128)(2,1)S(1)} %reshape_squeeze.3), kind=kOutput, calls=%fused_computation.4 | convolution fusion | flops 17301504 | bytes 4718864 | tf_op jit(solution)/shard_map/sc,sij->icj/dot_general | solution.py:204
  132.1 1.3 collective-permute-start.2
  133.4 1.2 broadcast_in_dim_reshape.3
  134.6 7.3 %collective-permute-done.2 = bf16[137,1032]{1,0:T(8,128)(2,1)S(1)} collective-permute-done((bf16[137,1032]{1,0:T(8,128)(2,1)S(1)}, bf16[137,1032]{1,0:T(8,128)(2,1)S(1)}, u32[]{:S(2)}, u32[]{:S(2)}) %collective-permute-start.2) | collective-permute-done | bytes 282800 | tf_op jit(solution)/shard_map/ppermute | solution.py:243
  142.5 0.8 multiply_add_fusion
  143.3 1.2 fusion.13
  144.5 1.3 fusion.24
  (38 shorter events, 6.3 us)
Async XLA Ops:
  15.0 101.0 %all-to-all-start = ((bf16[8,1040,256]{2,1,0:T(8,128)(2,1)}), bf16[8,1040,256]{2,1,0:T(8,128)(2,1)}, u32[]{:S(2)}, u32[]{:S(2)}) async-start(bf16[8,1040,256]{2,1,0:T(8,128)(2,1)} %shard_map.86), calls=%async_computation | async-start | bytes 8519680 | tf_op jit(solution)/shard_map/all_to_all | solution.py:199
  122.5 8.8 %collective-permute-start.1 = (bf16[256,4]{1,0:T(8,128)(2,1)S(1)}, bf16[256,4]{1,0:T(8,128)(2,1)S(1)}, u32[]{:S(2)}, u32[]{:S(2)}) collective-permute-start(bf16[256,4]{1,0:T(8,128)(2,1)S(1)} %divide_convert_fusion.1), channel_id=1, source_target_pairs={{1,0},{4,1},{5,4},{8,5},{9,8},{12,9},{13,12},{3,2},{6,3},{7,6},{10... | collective-permute-start | bytes 6152 | tf_op jit(solution)/shard_map/ppermute | solution.py:229
  126.0 5.3 %collective-permute-start = (bf16[256,4]{1,0:T(8,128)(2,1)S(1)}, bf16[256,4]{1,0:T(8,128)(2,1)S(1)}, u32[]{:S(2)}, u32[]{:S(2)}) collective-permute-start(bf16[256,4]{1,0:T(8,128)(2,1)S(1)} %divide_convert_fusion.2), channel_id=1, source_target_pairs={{0,1},{1,4},{4,5},{5,8},{8,9},{9,12},{12,13},{2,3},{3,6},{6,7},{7,... | collective-permute-start | bytes 6152 | tf_op jit(solution)/shard_map/ppermute | solution.py:228
  132.1 9.8 %collective-permute-start.2 = (bf16[137,1032]{1,0:T(8,128)(2,1)S(1)}, bf16[137,1032]{1,0:T(8,128)(2,1)S(1)}, u32[]{:S(2)}, u32[]{:S(2)}) collective-permute-start(bf16[137,1032]{1,0:T(8,128)(2,1)S(1)} %fusion.34), channel_id=1, source_target_pairs={{0,2},{2,0},{1,3},{3,1},{4,6},{6,4},{5,7},{7,5},{8,10},{10,8},{9,1... | collective-permute-start | bytes 848312 | tf_op jit(solution)/shard_map/ppermute | solution.py:243

commit v21 on v19

--- a/solution.py
+++ b/solution.py
@@ -215,7 +215,8 @@
     span = height + 2 * DET_R
     me = lax.axis_index("band")
     own = lax.dynamic_slice_in_dim(framed, me * height, span, axis=0)
-    combined = band_gain[0] * own.astype(jnp.float32)
+    width = CELL_DEV * side
+    detection = smooth_rows_valid(smooth_columns(band_gain[0] * own.astype(jnp.float32), width), height)
     for shift in range(1, band_count):
         outgoing = jnp.concatenate(
             [lax.dynamic_slice_in_dim(framed, ((me + shift) % band_count) * height, span, axis=0), gain_row]
@@ -224,8 +225,9 @@
             outgoing, "band", [(i, (i + shift) % band_count) for i in range(band_count)]
         )
         gain = jnp.sum(incoming[span, :3].astype(jnp.float32))
-        combined = combined + gain * incoming[:span].astype(jnp.float32)
-    detection = smooth_rows_valid(smooth_columns(combined, CELL_DEV * side), height)
+        detection = detection + smooth_rows_valid(
+            smooth_columns(gain * incoming[:span].astype(jnp.float32), width), height
+        )
     return (coadd[None], detection)
 
 

time: 143 us -> 144 us (level)
  other arithmetic: 12.8 us -> 14.5 us
  transfers between devices with their start and end apart: 4 -> 4, of which waited for: 3 -> 3; matrix products, arithmetic and copies ran while one was open for 2% -> 3% of each run, Pallas kernels for 0% -> 0%
where the time goes in v21:
time: 144 us; the launch traced here: 143 us
  waiting for transfers between devices  96.1 us (67%)
  other arithmetic  14.5 us (10%)
  starting transfers between devices  12 us (8%)
  local copies, waits for them, and re-layouts  8.36 us (6%)
  between operations  5.54 us (4%)
  Pallas kernels  4.48 us (3%)
  matrix products  2.44 us (2%)
    all_to_all x1, waiting for transfers between devices, local(): lax.all_to_all(packed, ('sect', 'sub'), split_axis=0, concat_axis=0, tile...  89.2 us
    all_to_all x1, starting transfers between devices, local(): lax.all_to_all(packed, ('sect', 'sub'), split_axis=0, concat_axis=0, tile...  6.41 us
    ppermute x1, waiting for transfers between devices, local(): lax.ppermute(outgoing, 'band', [(i, (i + shift) % band_count) for i in ra...  6.23 us
    pallas_call x1, Pallas kernels, warp_slots(): pl.pallas_call(warp_kernel, grid_spec=pltpu.PrefetchScalarGridSpec(num_sc...  4.48 us
  transfers between devices with their start and end apart: 4, of which 3 were waited for; matrix products, arithmetic and copies ran while one was open for 3% of the time, Pallas kernels for 0%

profile of v21, /device:TPU:1, one launch (start us, length us, event | category | flops | bytes accessed | tf_op | source)
XLA Modules:
  0.0 143.4 jit_solution(237864443090504739)
XLA Ops:
  0.7 0.7 negate_bitcast_fusion
  1.4 0.7 broadcast_add_fusion
  2.1 0.7 fusion.55
  3.4 0.9 convert_reduce_fusion.1
  4.4 0.7 fusion.91
  5.0 1.2 add_minimum_fusion.slot_ref
  6.6 0.7 fusion.89
  8.2 2.3 %scatter.6.blank_ref = bf16[8,1040,256]{2,1,0:T(8,128)(2,1)} pad(bf16[8,1,16]{2,1,0:T(2,128)(2,1)S(1)} %convert_element_type.73, bf16[]{:T(256)} %constant.132.clone.1), padding=0_0x1024_15x0_240 | pad | bytes 4260098 | tf_op jit(solution)/shard_map/scatter | solution.py:106
  10.5 4.5 %shard_map.86 = bf16[8,1040,256]{2,1,0:T(8,128)(2,1)} custom-call(s32[16]{0:T(128)} %add_minimum_fusion.slot_ref, f32[16,2,256]{2,1,0:T(2,128)} %pad_maximum_fusion.bases_ref, bf16[16,256,256]{2,1,0:T(8,128)(2,1)} %bitcast.41, bf16[8,1040,256]{2,1,0:T(8,128)(2,1)} %scatter.6.blank_ref), custom_call_target="tpu_custom_call", output_to_operand_aliasing={{}: (3, {})} | custom-call | flops 1073741824 | bytes 8454144 | tf_op jit(solution)/shard_map/pallas_call | solution.py:108
  15.0 6.4 %all-to-all-start = ((bf16[8,1040,256]{2,1,0:T(8,128)(2,1)}), bf16[8,1040,256]{2,1,0:T(8,128)(2,1)}, u32[]{:S(2)}, u32[]{:S(2)}) async-start(bf16[8,1040,256]{2,1,0:T(8,128)(2,1)} %shard_map.86), calls=%async_computation | async-start | bytes 8519680 | tf_op jit(solution)/shard_map/all_to_all | solution.py:199
  26.8 89.2 %all-to-all-done = bf16[8,1040,256]{2,1,0:T(8,128)(2,1)} async-done(((bf16[8,1040,256]{2,1,0:T(8,128)(2,1)}), bf16[8,1040,256]{2,1,0:T(8,128)(2,1)}, u32[]{:S(2)}, u32[]{:S(2)}) %all-to-all-start) | async-done | bytes 4259872 | tf_op jit(solution)/shard_map/all_to_all | solution.py:199
  116.1 0.7 slice_reduce_fusion.1
  116.9 2.5 %slice.239 = bf16[8,1024,256]{2,1,0:T(8,128)(2,1)S(1)} slice(bf16[8,1040,256]{2,1,0:T(8,128)(2,1)} %all-to-all-done), slice={[0:8], [0:1024], [0:256]} | slice | bytes 8388608 | tf_op jit(solution)/shard_map/slice | solution.py:203
  119.4 2.4 %divide_convert_fusion = bf16[256,256,4]{1,2,0:T(4,128)(2,1)S(1)} fusion(bf16[32,256,256]{2,1,0:T(8,128)(2,1)S(1)} %bitcast.36, f32[4]{0:T(128)S(1)} %broadcast_maximum_fusion, bf16[32,4]{1,0:T(8,128)(2,1)S(1)} %reshape_squeeze.3), kind=kOutput, calls=%fused_computation.2 | convolution fusion | flops 17301504 | bytes 4718864 | tf_op jit(solution)/shard_map/sc,sij->icj/dot_general | solution.py:204
  122.0 1.9 %collective-permute-start = (bf16[256,4]{1,0:T(8,128)(2,1)S(1)}, bf16[256,4]{1,0:T(8,128)(2,1)S(1)}, u32[]{:S(2)}, u32[]{:S(2)}) collective-permute-start(bf16[256,4]{1,0:T(8,128)(2,1)S(1)} %get-tuple-element.28), channel_id=1, source_target_pairs={{0,1},{1,4},{4,5},{5,8},{8,9},{9,12},{12,13},{2,3},{3,6},{6,7},{7,... | collective-permute-start | bytes 6152 | tf_op jit(solution)/shard_map/ppermute | solution.py:25
  124.0 2.4 %collective-permute-start.1 = (bf16[256,4]{1,0:T(8,128)(2,1)S(1)}, bf16[256,4]{1,0:T(8,128)(2,1)S(1)}, u32[]{:S(2)}, u32[]{:S(2)}) collective-permute-start(bf16[256,4]{1,0:T(8,128)(2,1)S(1)} %get-tuple-element.27), channel_id=1, source_target_pairs={{1,0},{4,1},{5,4},{8,5},{9,8},{12,9},{13,12},{3,2},{6,3},{7,6},{10... | collective-permute-start | bytes 6152 | tf_op jit(solution)/shard_map/ppermute | solution.py:26
  126.4 1.4 broadcast_select_fusion
  127.7 1.2 broadcast_in_dim_reshape.3
  130.3 1.3 collective-permute-start.2
  131.7 1.2 fusion.21
  132.9 6.2 %collective-permute-done.2 = bf16[137,1032]{1,0:T(8,128)(2,1)S(1)} collective-permute-done((bf16[137,1032]{1,0:T(8,128)(2,1)S(1)}, bf16[137,1032]{1,0:T(8,128)(2,1)S(1)}, u32[]{:S(2)}, u32[]{:S(2)}) %collective-permute-start.2) | collective-permute-done | bytes 282800 | tf_op jit(solution)/shard_map/ppermute | solution.py:224
  139.7 0.7 convert_multiply_fusion
  140.4 1.2 fusion.13
  141.6 1.8 %fusion.33 = f32[128,1024]{1,0:T(8,128)} fusion(f32[136,1024]{1,0:T(8,128)S(1)} %fusion.13, f32[136,1024]{1,0:T(8,128)S(1)} %fusion.21), kind=kLoop, calls=%fused_computation.62 | loop fusion | flops 4587520 | bytes 9961472 | tf_op jit(solution)/shard_map/add | solution.py:228
  (34 shorter events, 5.0 us)
Async XLA Ops:
  15.0 101.1 %all-to-all-start = ((bf16[8,1040,256]{2,1,0:T(8,128)(2,1)}), bf16[8,1040,256]{2,1,0:T(8,128)(2,1)}, u32[]{:S(2)}, u32[]{:S(2)}) async-start(bf16[8,1040,256]{2,1,0:T(8,128)(2,1)} %shard_map.86), calls=%async_computation | async-start | bytes 8519680 | tf_op jit(solution)/shard_map/all_to_all | solution.py:199
  122.0 6.9 %collective-permute-start = (bf16[256,4]{1,0:T(8,128)(2,1)S(1)}, bf16[256,4]{1,0:T(8,128)(2,1)S(1)}, u32[]{:S(2)}, u32[]{:S(2)}) collective-permute-start(bf16[256,4]{1,0:T(8,128)(2,1)S(1)} %get-tuple-element.28), channel_id=1, source_target_pairs={{0,1},{1,4},{4,5},{5,8},{8,9},{9,12},{12,13},{2,3},{3,6},{6,7},{7,... | collective-permute-start | bytes 6152 | tf_op jit(solution)/shard_map/ppermute | solution.py:25
  124.0 5.6 %collective-permute-start.1 = (bf16[256,4]{1,0:T(8,128)(2,1)S(1)}, bf16[256,4]{1,0:T(8,128)(2,1)S(1)}, u32[]{:S(2)}, u32[]{:S(2)}) collective-permute-start(bf16[256,4]{1,0:T(8,128)(2,1)S(1)} %get-tuple-element.27), channel_id=1, source_target_pairs={{1,0},{4,1},{5,4},{8,5},{9,8},{12,9},{13,12},{3,2},{6,3},{7,6},{10... | collective-permute-start | bytes 6152 | tf_op jit(solution)/shard_map/ppermute | solution.py:26
  130.3 8.8 %collective-permute-start.2 = (bf16[137,1032]{1,0:T(8,128)(2,1)S(1)}, bf16[137,1032]{1,0:T(8,128)(2,1)S(1)}, u32[]{:S(2)}, u32[]{:S(2)}) collective-permute-start(bf16[137,1032]{1,0:T(8,128)(2,1)S(1)} %fusion.51), channel_id=1, source_target_pairs={{0,2},{2,0},{1,3},{3,1},{4,6},{6,4},{5,7},{7,5},{8,10},{10,8},{9,1... | collective-permute-start | bytes 848312 | tf_op jit(solution)/shard_map/ppermute | solution.py:224

commit v22 on v19

--- a/solution.py
+++ b/solution.py
@@ -62,10 +62,28 @@
     return jnp.stack([rows, cols], axis=1)
 
 
-def warp_kernel(slot_ref, bases_ref, image_ref, blank_ref, out_ref, done_ref, sems):
+def warp_kernel(
+    slot_ref, source_ref, bases_ref, image_ref, weight_ref, out_ref, done_ref, zero_ref, sems, fill_sems
+):
     side = image_ref.shape[-1]
     group = image_ref.shape[0]
-    step = pl.program_id(0)
+    capacity = (out_ref.shape[1] - 16) // side
+    slot_total = source_ref.shape[0]
+    zero_ref[...] = jnp.zeros((side, side), jnp.bfloat16)
+
+    def target(slot):
+        return out_ref.at[slot // capacity, pl.ds((slot % capacity) * side, side), :]
+
+    for slot in range(slot_total):
+
+        @pl.when(source_ref[slot] >= group)
+        def _():
+            pltpu.make_async_copy(zero_ref, target(slot), fill_sems.at[slot]).start()
+
+    weight_copy = pltpu.make_async_copy(
+        weight_ref, out_ref.at[:, pl.ds(capacity * side, 16), :], fill_sems.at[slot_total]
+    )
+    weight_copy.start()
     lag = lax.broadcasted_iota(jnp.int32, (side, side), 0) - lax.broadcasted_iota(
         jnp.int32, (side, side), 1
     )
@@ -85,51 +103,55 @@
         done_ref[member] = jnp.dot(
             section.astype(jnp.bfloat16), col_kernel_t, preferred_element_type=jnp.float32
         ).astype(jnp.bfloat16)
-        slot = slot_ref[step * group + member]
-        capacity = (out_ref.shape[1] - 16) // side
-        target = out_ref.at[slot // capacity, pl.ds((slot % capacity) * side, side), :]
-        copy = pltpu.make_async_copy(done_ref.at[member], target, sems.at[member])
+        copy = pltpu.make_async_copy(done_ref.at[member], target(slot_ref[member]), sems.at[member])
         copy.start()
         copies.append(copy)
     for copy in copies:
         copy.wait()
-
-
-def warp_slots(images, values, slot_index, slot_weight, interpret=False):
+    weight_copy.wait()
+    for slot in range(slot_total):
+
+        @pl.when(source_ref[slot] >= group)
+        def _():
+            pltpu.make_async_copy(zero_ref, target(slot), fill_sems.at[slot]).wait()
+
+
+def warp_slots(images, values, slot_index, slot_source, slot_weight, interpret=False):
     count, side = images.shape[0], images.shape[-1]
     owners, capacity, cell_count = slot_weight.shape
-    group = next(size for size in (16, 8, 4, 2, 1) if count % size == 0)
+    slot_total = owners * capacity
     bases = base_rows(values, side)
-    blank = (
-        jnp.zeros((owners, capacity * side + 16, side), jnp.bfloat16)
-        .at[:, capacity * side, : capacity * cell_count]
+    weight_rows = (
+        jnp.zeros((owners, 16, side), jnp.bfloat16)
+        .at[:, 0, : capacity * cell_count]
         .set(slot_weight.reshape(owners, capacity * cell_count))
     )
     return pl.pallas_call(
         warp_kernel,
         grid_spec=pltpu.PrefetchScalarGridSpec(
-            num_scalar_prefetch=1,
-            grid=(count // group,),
+            num_scalar_prefetch=2,
+            grid=(1,),
             in_specs=[
-                pl.BlockSpec((group, 2, side), lambda b, slots: (b, 0, 0)),
-                pl.BlockSpec((group, side, side), lambda b, slots: (b, 0, 0)),
-                pl.BlockSpec(memory_space=pl.ANY),
+                pl.BlockSpec((count, 2, side), lambda b, slots, sources: (0, 0, 0)),
+                pl.BlockSpec((count, side, side), lambda b, slots, sources: (0, 0, 0)),
+                pl.BlockSpec((owners, 16, side), lambda b, slots, sources: (0, 0, 0)),
             ],
             out_specs=pl.BlockSpec(memory_space=pl.ANY),
             scratch_shapes=[
-                pltpu.VMEM((group, side, side), jnp.bfloat16),
-                pltpu.SemaphoreType.DMA((group,)),
+                pltpu.VMEM((count, side, side), jnp.bfloat16),
+                pltpu.VMEM((side, side), jnp.bfloat16),
+                pltpu.SemaphoreType.DMA((count,)),
+                pltpu.SemaphoreType.DMA((slot_total + 1,)),
             ],
         ),
-        out_shape=jax.ShapeDtypeStruct(blank.shape, jnp.bfloat16),
-        input_output_aliases={3: 0},
+        out_shape=jax.ShapeDtypeStruct((owners, capacity * side + 16, side), jnp.bfloat16),
         cost_estimate=pl.CostEstimate(
             flops=4 * count * side**3,
             transcendentals=0,
-            bytes_accessed=2 * (2 * count * side * side + blank.size),
+            bytes_accessed=2 * (count + slot_total) * side * side,
         ),
         interpret=interpret,
-    )(slot_index, bases, images, blank)
+    )(slot_index, slot_source, bases, images, weight_rows)
 
 
 def gain_pieces(gain):
@@ -194,6 +216,7 @@
         images[0],
         values,
         jnp.minimum(slot_index, slot_count - 1).astype(jnp.int32),
+        jnp.where(jnp.any(matching, axis=1), source, count).astype(jnp.int32),
         packed_weight.reshape(owners, capacity, CELL_DEV),
     )
     received = lax.all_to_all(packed, ("sect", "sub"), split_axis=0, concat_axis=0, tiled=True)

time: 143 us -> 142 us (level)
  local copies, waits for them, and re-layouts: 8.36 us -> 6.72 us
    scatter x1, local copies, waits for them, and re-layouts: 2.28 us -> 0.64 us  [warp_slots(): weight_rows = jnp.zeros((owners, 16, side), jnp.bfloat16).at[:, 0, :capac...]
where the time goes in v22:
time: 142 us
  waiting for transfers between devices  96.7 us (68%)
  other arithmetic  13.5 us (10%)
  starting transfers between devices  12 us (8%)
  local copies, waits for them, and re-layouts  6.72 us (5%)
  between operations  5.53 us (4%)
  Pallas kernels  5.1 us (4%)
  matrix products  2.44 us (2%)
    all_to_all x1, waiting for transfers between devices, local(): lax.all_to_all(packed, ('sect', 'sub'), split_axis=0, concat_axis=0, tile...  89.2 us
    all_to_all x1, starting transfers between devices, local(): lax.all_to_all(packed, ('sect', 'sub'), split_axis=0, concat_axis=0, tile...  6.41 us
    ppermute x1, waiting for transfers between devices, local(): lax.ppermute(outgoing, 'band', [(i, (i + shift) % band_count) for i in ra...  5.7 us
    pallas_call x1, Pallas kernels, warp_slots(): pl.pallas_call(warp_kernel, grid_spec=pltpu.PrefetchScalarGridSpec(num_sc...  5.1 us
  transfers between devices with their start and end apart: 4, of which 3 were waited for; matrix products, arithmetic and copies ran while one was open for 2% of the time, Pallas kernels for 0%

profile of v22, /device:TPU:1, one launch (start us, length us, event | category | flops | bytes accessed | tf_op | source)
XLA Modules:
  0.0 142.0 jit_solution(1580068419254542512)
XLA Ops:
  0.7 0.7 negate_bitcast_fusion
  1.4 0.7 broadcast_add_fusion
  2.1 0.7 fusion.38
  3.4 0.9 convert_reduce_fusion.1
  4.4 0.7 fusion.75
  5.2 1.2 add_minimum_fusion.slot_ref
  6.7 0.7 fusion.73
  7.7 0.7 pad_maximum_fusion.bases_ref
  9.6 5.1 %shard_map.86 = bf16[8,1040,256]{2,1,0:T(8,128)(2,1)} custom-call(s32[16]{0:T(128)} %add_minimum_fusion.slot_ref, s32[32]{0:T(128)} %broadcast_select_fusion.1.source_ref, f32[16,2,256]{2,1,0:T(2,128)} %pad_maximum_fusion.bases_ref, bf16[16,256,256]{2,1,0:T(8,128)(2,1)} %bitcast.39, bf16[8,16,256]{2,1,0:T(8,128)(2,1)} %scatter.6.weight_ref), custom_call_target="tpu_custom_call" | custom-call | flops 1073741824 | bytes 6291456 | tf_op jit(solution)/shard_map/pallas_call | solution.py:129
  14.7 6.4 %all-to-all-start = ((bf16[8,1040,256]{2,1,0:T(8,128)(2,1)}), bf16[8,1040,256]{2,1,0:T(8,128)(2,1)}, u32[]{:S(2)}, u32[]{:S(2)}) async-start(bf16[8,1040,256]{2,1,0:T(8,128)(2,1)} %shard_map.86), calls=%async_computation | async-start | bytes 8519680 | tf_op jit(solution)/shard_map/all_to_all | solution.py:222
  26.5 89.2 %all-to-all-done = bf16[8,1040,256]{2,1,0:T(8,128)(2,1)} async-done(((bf16[8,1040,256]{2,1,0:T(8,128)(2,1)}), bf16[8,1040,256]{2,1,0:T(8,128)(2,1)}, u32[]{:S(2)}, u32[]{:S(2)}) %all-to-all-start) | async-done | bytes 4259872 | tf_op jit(solution)/shard_map/all_to_all | solution.py:222
  115.7 0.7 slice_reduce_fusion.1
  116.6 2.5 %slice.165 = bf16[8,1024,256]{2,1,0:T(8,128)(2,1)S(1)} slice(bf16[8,1040,256]{2,1,0:T(8,128)(2,1)} %all-to-all-done), slice={[0:8], [0:1024], [0:256]} | slice | bytes 8388608 | tf_op jit(solution)/shard_map/slice | solution.py:226
  119.0 2.4 %divide_convert_fusion = bf16[256,256,4]{1,2,0:T(4,128)(2,1)S(1)} fusion(bf16[32,256,256]{2,1,0:T(8,128)(2,1)S(1)} %bitcast.36, f32[4]{0:T(128)S(1)} %broadcast_maximum_fusion, bf16[32,4]{1,0:T(8,128)(2,1)S(1)} %reshape_squeeze.3), kind=kOutput, calls=%fused_computation.2 | convolution fusion | flops 17301504 | bytes 4718864 | tf_op jit(solution)/shard_map/sc,sij->icj/dot_general | solution.py:227
  121.7 1.9 %collective-permute-start = (bf16[256,4]{1,0:T(8,128)(2,1)S(1)}, bf16[256,4]{1,0:T(8,128)(2,1)S(1)}, u32[]{:S(2)}, u32[]{:S(2)}) collective-permute-start(bf16[256,4]{1,0:T(8,128)(2,1)S(1)} %get-tuple-element.28), channel_id=1, source_target_pairs={{0,1},{1,4},{4,5},{5,8},{8,9},{9,12},{12,13},{2,3},{3,6},{6,7},{7,... | collective-permute-start | bytes 6152 | tf_op jit(solution)/shard_map/ppermute | solution.py:25
  123.6 2.4 %collective-permute-start.1 = (bf16[256,4]{1,0:T(8,128)(2,1)S(1)}, bf16[256,4]{1,0:T(8,128)(2,1)S(1)}, u32[]{:S(2)}, u32[]{:S(2)}) collective-permute-start(bf16[256,4]{1,0:T(8,128)(2,1)S(1)} %get-tuple-element.27), channel_id=1, source_target_pairs={{1,0},{4,1},{5,4},{8,5},{9,8},{12,9},{13,12},{3,2},{6,3},{7,6},{10... | collective-permute-start | bytes 6152 | tf_op jit(solution)/shard_map/ppermute | solution.py:26
  126.0 1.4 broadcast_select_fusion
  127.4 1.8 %collective-permute-done.1 = bf16[256,4]{1,0:T(8,128)(2,1)S(1)} collective-permute-done((bf16[256,4]{1,0:T(8,128)(2,1)S(1)}, bf16[256,4]{1,0:T(8,128)(2,1)S(1)}, u32[]{:S(2)}, u32[]{:S(2)}) %collective-permute-start.1) | collective-permute-done | bytes 2080 | tf_op jit(solution)/shard_map/ppermute | solution.py:26
  129.9 1.2 collective-permute-start.2
  131.2 1.2 broadcast_in_dim_reshape.3
  132.4 5.7 %collective-permute-done.2 = bf16[137,1032]{1,0:T(8,128)(2,1)S(1)} collective-permute-done((bf16[137,1032]{1,0:T(8,128)(2,1)S(1)}, bf16[137,1032]{1,0:T(8,128)(2,1)S(1)}, u32[]{:S(2)}, u32[]{:S(2)}) %collective-permute-start.2) | collective-permute-done | bytes 282800 | tf_op jit(solution)/shard_map/ppermute | solution.py:246
  138.7 0.8 multiply_add_fusion
  139.5 1.2 fusion.13
  140.7 1.3 fusion.24
  (34 shorter events, 4.9 us)
Async XLA Ops:
  14.7 101.1 %all-to-all-start = ((bf16[8,1040,256]{2,1,0:T(8,128)(2,1)}), bf16[8,1040,256]{2,1,0:T(8,128)(2,1)}, u32[]{:S(2)}, u32[]{:S(2)}) async-start(bf16[8,1040,256]{2,1,0:T(8,128)(2,1)} %shard_map.86), calls=%async_computation | async-start | bytes 8519680 | tf_op jit(solution)/shard_map/all_to_all | solution.py:222
  121.7 5.7 %collective-permute-start = (bf16[256,4]{1,0:T(8,128)(2,1)S(1)}, bf16[256,4]{1,0:T(8,128)(2,1)S(1)}, u32[]{:S(2)}, u32[]{:S(2)}) collective-permute-start(bf16[256,4]{1,0:T(8,128)(2,1)S(1)} %get-tuple-element.28), channel_id=1, source_target_pairs={{0,1},{1,4},{4,5},{5,8},{8,9},{9,12},{12,13},{2,3},{3,6},{6,7},{7,... | collective-permute-start | bytes 6152 | tf_op jit(solution)/shard_map/ppermute | solution.py:25
  123.6 5.6 %collective-permute-start.1 = (bf16[256,4]{1,0:T(8,128)(2,1)S(1)}, bf16[256,4]{1,0:T(8,128)(2,1)S(1)}, u32[]{:S(2)}, u32[]{:S(2)}) collective-permute-start(bf16[256,4]{1,0:T(8,128)(2,1)S(1)} %get-tuple-element.27), channel_id=1, source_target_pairs={{1,0},{4,1},{5,4},{8,5},{9,8},{12,9},{13,12},{3,2},{6,3},{7,6},{10... | collective-permute-start | bytes 6152 | tf_op jit(solution)/shard_map/ppermute | solution.py:26
  129.9 8.1 %collective-permute-start.2 = (bf16[137,1032]{1,0:T(8,128)(2,1)S(1)}, bf16[137,1032]{1,0:T(8,128)(2,1)S(1)}, u32[]{:S(2)}, u32[]{:S(2)}) collective-permute-start(bf16[137,1032]{1,0:T(8,128)(2,1)S(1)} %fusion.34), channel_id=1, source_target_pairs={{0,2},{2,0},{1,3},{3,1},{4,6},{6,4},{5,7},{7,5},{8,10},{10,8},{9,1... | collective-permute-start | bytes 848312 | tf_op jit(solution)/shard_map/ppermute | solution.py:246
